TPU v7x, 128 devices: a whole 4x4x4 slice. The times are simulated.
128 devices in a mesh: dp: 16 (over x, y_lo, core), tensor: 8 (over z, y_hi).
Axes of the slice: x: 4, y: 4 (y_hi: 2, y_lo: 2; y = y_hi * 2 + y_lo), z: 4, core: 2. Of those that a mesh axis runs over, the one named last changes fastest.
Arguments:
- rows_in: bfloat16 [2048, 6144], P('dp'), may hold values from -6 to 6
- out_grad: bfloat16 [2048, 6144], P('dp'), may hold values from -1.5 to 1.5
- gate_pre: bfloat16 [2048, 12288], P('dp', 'tensor'), may hold values from -5 to 5
- up_pre: bfloat16 [2048, 12288], P('dp', 'tensor'), may hold values from -5 to 5
- w_gate: bfloat16 [2, 6144, 12288], P(None, 'dp', 'tensor'), may hold values from -0.078125 to 0.078125
- w_up: bfloat16 [2, 6144, 12288], P(None, 'dp', 'tensor'), may hold values from -0.078125 to 0.078125
- w_down: bfloat16 [2, 12288, 6144], P(None, 'tensor', 'dp'), may hold values from -0.0546875 to 0.0546875
- live_rows: int32 [16], P('dp'), may hold values from 32 to 128, as said below
- block_expert: int32 [16], replicated, may hold values from 0 to 1, as said below
Outputs:
- input_grad: bfloat16 [2048, 6144], P('dp', 'tensor')
- grad_gate: bfloat16 [2, 6144, 12288], P(None, 'dp', 'tensor')
- grad_up: bfloat16 [2, 6144, 12288], P(None, 'dp', 'tensor')
- grad_down: bfloat16 [2, 12288, 6144], P(None, 'tensor', 'dp')
Inputs may be any that keep to these rules, and one draw needn't show every extreme that they name: `live_rows`: entry k counts the live rows among rank k's 128 rows; they come first and the rest are padding; some rank is full. `block_expert`: the expert of each aligned block of 128 rows; every expert owns at least one block.
All inputs are finite; a program needn't handle non-finite values.
Results may differ from a plain program's by a relative error of at most 0.005.
Values may be sent and summed in bfloat16 or wider, within the bound.
No kernel may reach another device: no remote copies, remote signals or barrier semaphores. Data moves between devices by JAX's collectives and lax.ppermute only.
A program may use at most 128 MiB of HBM per device.

v0:
```python
import jax
import jax.numpy as jnp
from jax import lax
from jax.sharding import PartitionSpec as P

BLOCK = 128


def contract_rows(left_op, right_op):
    return lax.dot_general(
        left_op, right_op, (((0,), (0,)), ((), ())), preferred_element_type=jnp.float32
    )


def contract_cols(left_op, right_op):
    return lax.dot_general(
        left_op, right_op, (((1,), (1,)), ((), ())), preferred_element_type=jnp.float32
    )


def expert_masks(block_expert, row_count, expert_count):
    spread = jnp.broadcast_to(block_expert[:, None], (row_count // BLOCK, BLOCK)).reshape(
        row_count, 1
    )
    return [(spread == which).astype(jnp.bfloat16) for which in range(expert_count)]


def shards(rows_in, out_grad, gate_pre, up_pre, w_gate, w_up, w_down, live_rows, block_expert):
    rows_dev = rows_in.shape[0]
    expert_count = w_gate.shape[0]
    x_cols, dy_cols = (
        lax.all_to_all(rows_in, "dp", split_axis=1, concat_axis=0, tiled=True),
        lax.all_to_all(out_grad, "dp", split_axis=1, concat_axis=0, tiled=True),
    )
    positions = jnp.arange(rows_dev, dtype=jnp.int32)[:, None]
    row_mask = (positions < live_rows[0]).astype(jnp.float32)
    gate_vals = gate_pre.astype(jnp.float32)
    up_vals = up_pre.astype(jnp.float32)
    sigmoid = jax.nn.sigmoid(gate_vals)
    silu_vals = gate_vals * sigmoid
    hidden = (silu_vals * up_vals * row_mask).astype(jnp.bfloat16)

    def fold_grads(pieces):
        gate_piece, up_piece = pieces
        row_count = gate_piece.shape[0]
        masks = expert_masks(block_expert, row_count, expert_count)
        gate_terms = []
        up_terms = []
        partial_rows = jnp.zeros((row_count, w_gate.shape[1]), jnp.float32)
        for which in range(expert_count):
            gate_masked = gate_piece * masks[which]
            up_masked = up_piece * masks[which]
            gate_terms.append(contract_rows(x_cols, gate_masked))
            up_terms.append(contract_rows(x_cols, up_masked))
            partial_rows = (
                partial_rows
                + contract_cols(gate_masked, w_gate[which])
                + contract_cols(up_masked, w_up[which])
            )
        gate_total = jnp.stack(gate_terms, 0)
        up_total = jnp.stack(up_terms, 0)
        return (gate_total, up_total, partial_rows)

    masks = expert_masks(block_expert, rows_dev * lax.axis_size("dp"), expert_count)
    dy_rows = dy_cols
    result = jnp.zeros((rows_dev * lax.axis_size("dp"), w_down.shape[1]), jnp.float32)
    for down_which in range(expert_count):
        result = result + contract_cols(dy_rows * masks[down_which], w_down[down_which])
    hidden_grad = lax.psum_scatter(result, "dp", scatter_dimension=0, tiled=True)
    up_grad = (hidden_grad * silu_vals * row_mask).astype(jnp.bfloat16)
    gate_grad = (
        hidden_grad * up_vals * sigmoid * (1.0 + gate_vals * (1.0 - sigmoid)) * row_mask
    ).astype(jnp.bfloat16)
    pieces = (
        lax.all_gather(hidden, "dp", axis=0, tiled=True),
        lax.all_gather(gate_grad, "dp", axis=0, tiled=True),
        lax.all_gather(up_grad, "dp", axis=0, tiled=True),
    )
    fold_pieces = pieces[0]
    row_count = fold_pieces.shape[0]
    masks = expert_masks(block_expert, row_count, expert_count)
    dy_rows = dy_cols
    terms = [contract_rows(fold_pieces * masks[which], dy_rows) for which in range(expert_count)]
    down_total = jnp.stack(terms, 0)
    rest = fold_grads((pieces[1], pieces[2]))
    down_total, gate_total, up_total, partial_all = (down_total, rest[0], rest[1], rest[2])
    input_rows = lax.all_to_all(partial_all, "dp", split_axis=0, concat_axis=1, tiled=True)
    input_grad = lax.psum_scatter(input_rows, "tensor", scatter_dimension=1, tiled=True).astype(
        jnp.bfloat16
    )
    return (
        input_grad,
        gate_total.astype(jnp.bfloat16),
        up_total.astype(jnp.bfloat16),
        down_total.astype(jnp.bfloat16),
    )


def solution(mesh):
    return jax.shard_map(
        shards,
        mesh=mesh,
        in_specs=(
            P("dp", None),
            P("dp", None),
            P("dp", "tensor"),
            P("dp", "tensor"),
            P(None, "dp", "tensor"),
            P(None, "dp", "tensor"),
            P(None, "tensor", "dp"),
            P("dp"),
            P(),
        ),
        out_specs=(
            P("dp", "tensor"),
            P(None, "dp", "tensor"),
            P(None, "dp", "tensor"),
            P(None, "tensor", "dp"),
        ),
        check_vma=False,
    )
```

profile of v0, /device:TPU:3, one launch (start us, length us, event | category | flops | bytes accessed | tf_op | source)
XLA Modules:
  0.0 465.5 jit_solution(15119183994960991915)
XLA Ops:
  9.7 6.3 %all-to-all-start = ((bf16[128,16,384]{0,2,1:T(8,128)(2,1)}), bf16[128,16,384]{0,2,1:T(8,128)(2,1)S(1)}, u32[]{:S(2)}, u32[]{:S(2)}) async-start(bf16[128,16,384]{0,2,1:T(8,128)(2,1)} %bitcast), calls=%async_computation | async-start | bytes 3145728 | tf_op jit(solution)/shard_map/all_to_all | solution.py:33
  16.1 19.7 %all-to-all-done = bf16[128,16,384]{0,2,1:T(8,128)(2,1)S(1)} async-done(((bf16[128,16,384]{0,2,1:T(8,128)(2,1)}), bf16[128,16,384]{0,2,1:T(8,128)(2,1)S(1)}, u32[]{:S(2)}, u32[]{:S(2)}) %all-to-all-start) | async-done | bytes 1572896 | tf_op jit(solution)/shard_map/all_to_all | solution.py:33
  40.7 5.4 %fusion.73 = f32[2048,1536]{1,0:T(8,128)S(1)} fusion(bf16[2048,384]{1,0:T(8,128)(2,1)} %bitcast.69, bf16[2,1536,384]{2,1,0:T(8,128)(2,1)} %param.15), kind=kOutput, calls=%fused_computation.55 | convolution fusion | flops 2415919104 | bytes 15335424 | tf_op jit(solution)/shard_map/dot_general | solution.py:16
  46.0 6.5 %convolution_add_fusion = f32[2048,1536]{1,0:T(8,128)} fusion(f32[2048,1536]{1,0:T(8,128)S(1)} %fusion.73, bf16[2048,384]{1,0:T(8,128)(2,1)S(1)} %bitcast.68, bf16[2,1536,384]{2,1,0:T(8,128)(2,1)S(1)} %copy-done), kind=kOutput, calls=%fused_computation | convolution fusion | flops 2419064832 | bytes 27918336 | tf_op jit(solution)/shard_map/dot_general | solution.py:16
  53.4 140.1 %reduce-scatter.3.cloned.1.call-done = f32[128,1536]{1,0:T(8,128)} async-done(((f32[2048,1536]{1,0:T(8,128)}), f32[128,1536]{1,0:T(8,128)}) %reduce-scatter.3.cloned.1.call-update) | async-done | bytes 786448 | tf_op jit(solution)/shard_map/reduce_scatter | solution.py:69
  197.5 41.7 %all-gather.6.cloned.1.call-done = bf16[2048,1536]{1,0:T(8,128)(2,1)} async-done(((bf16[128,1536]{1,0:T(8,128)(2,1)}), bf16[2048,1536]{1,0:T(8,128)(2,1)}) %all-gather.6.cloned.1.call-update) | async-done | bytes 6291472 | tf_op jit(solution)/shard_map/all_gather | solution.py:77
  239.2 8.4 %fusion.14 = f32[2048,384]{1,0:T(8,128)} fusion(bf16[2048,1536]{1,0:T(8,128)(2,1)} %all-gather.6.cloned.1.call-done, bf16[2048]{0:T(1024)(128)(2,1)S(1)} %broadcast_bitcast_fusion.1, bf16[2,384,1536]{2,1,0:T(8,128)(2,1)} %param.14), kind=kOutput, calls=%fused_computation.15 | convolution fusion | flops 2419064832 | bytes 10620928 | tf_op jit(solution)/shard_map/dot_general | solution.py:16
  247.6 5.2 %fusion.6 = f32[2048,384]{1,0:T(8,128)} fusion(bf16[2048,1536]{1,0:T(8,128)(2,1)S(1)} %copy-done.8, bf16[2048]{0:T(1024)(128)(2,1)S(1)} %broadcast_bitcast_fusion, bf16[2,384,1536]{2,1,0:T(8,128)(2,1)S(1)} %copy-done.10), kind=kOutput, calls=%fused_computation.7 | convolution fusion | flops 2419064832 | bytes 10620928 | tf_op jit(solution)/shard_map/dot_general | solution.py:16
  252.9 31.8 %all-gather.4.cloned.1.call-done = bf16[2048,1536]{1,0:T(8,128)(2,1)} async-done(((bf16[128,1536]{1,0:T(8,128)(2,1)}), bf16[2048,1536]{1,0:T(8,128)(2,1)}) %all-gather.4.cloned.1.call-update) | async-done | bytes 6291472 | tf_op jit(solution)/shard_map/all_gather | solution.py:76
  284.6 6.2 %fusion.18 = f32[2048,384]{1,0:T(8,128)S(1)} fusion(bf16[2048,1536]{1,0:T(8,128)(2,1)} %all-gather.4.cloned.1.call-done, bf16[2048]{0:T(1024)(128)(2,1)S(1)} %broadcast_bitcast_fusion.1, bf16[2,384,1536]{2,1,0:T(8,128)(2,1)} %param.13), kind=kOutput, calls=%fused_computation.19 | convolution fusion | flops 2419064832 | bytes 10620928 | tf_op jit(solution)/shard_map/dot_general | solution.py:16
  292.1 5.3 %add_add_fusion = f32[2048,384]{1,0:T(8,128)} fusion(f32[2048,384]{1,0:T(8,128)S(1)} %copy-done.14, f32[2048,384]{1,0:T(8,128)S(1)} %fusion.18, f32[2048,384]{1,0:T(8,128)S(1)} %copy-done.13, bf16[2048,1536]{1,0:T(8,128)(2,1)S(1)} %copy-done.9, bf16[2048]{0:T(1024)(128)(2,1)S(1)} %broadcast_bitcast_fusion, bf16[2,384,1536]{2,1,0:T(8,128)(2,1)S(1)} %copy-done.11), kind=kOutput, calls=%fused_computation.21 | convolution fusion | flops 2421424128 | bytes 20058112 | tf_op jit(solution)/shard_map/dot_general | solution.py:16
  297.4 5.5 %all-to-all-start.1 = ((f32[16,128,384]{2,1,0:T(8,128)}), f32[16,128,384]{2,1,0:T(8,128)}, u32[]{:S(2)}, u32[]{:S(2)}) async-start(f32[16,128,384]{2,1,0:T(8,128)} %bitcast.71), calls=%async_computation.2 | async-start | bytes 6291456 | tf_op jit(solution)/shard_map/all_to_all | solution.py:87
  304.5 56.2 %all-to-all-done.1 = f32[16,128,384]{2,1,0:T(8,128)} async-done(((f32[16,128,384]{2,1,0:T(8,128)}), f32[16,128,384]{2,1,0:T(8,128)}, u32[]{:S(2)}, u32[]{:S(2)}) %all-to-all-start.1) | async-done | bytes 3145760 | tf_op jit(solution)/shard_map/all_to_all | solution.py:87
  360.7 7.3 %all-to-all-start.2 = ((bf16[128,16,384]{0,2,1:T(8,128)(2,1)}), bf16[128,16,384]{0,2,1:T(8,128)(2,1)S(1)}, u32[]{:S(2)}, u32[]{:S(2)}) async-start(bf16[128,16,384]{0,2,1:T(8,128)(2,1)} %bitcast.15), calls=%async_computation.4 | async-start | bytes 3145728 | tf_op jit(solution)/shard_map/all_to_all | solution.py:32
  368.6 3.9 copy.28
  372.5 15.1 %all-to-all-done.2 = bf16[128,16,384]{0,2,1:T(8,128)(2,1)S(1)} async-done(((bf16[128,16,384]{0,2,1:T(8,128)(2,1)}), bf16[128,16,384]{0,2,1:T(8,128)(2,1)S(1)}, u32[]{:S(2)}, u32[]{:S(2)}) %all-to-all-start.2) | async-done | bytes 1572896 | tf_op jit(solution)/shard_map/all_to_all | solution.py:32
  390.8 6.4 %fusion.56 = bf16[1,384,1536]{1,2,0:T(8,128)(2,1)S(1)} fusion(bf16[2048,384]{1,0:T(8,128)(2,1)S(1)} %bitcast.75, bf16[2048,1536]{1,0:T(8,128)(2,1)} %all-gather.6.cloned.1.call-done, bf16[2048]{0:T(1024)(128)(2,1)S(1)} %broadcast_bitcast_fusion), kind=kOutput, calls=%fused_computation.40 | convolution fusion | flops 2419654656 | bytes 9048064 | tf_op jit(solution)/shard_map/dot_general | solution.py:10
  397.2 6.4 %fusion.62 = bf16[1,384,1536]{1,2,0:T(8,128)(2,1)S(1)} fusion(bf16[2048,384]{1,0:T(8,128)(2,1)S(1)} %bitcast.76, bf16[2048,1536]{1,0:T(8,128)(2,1)} %all-gather.6.cloned.1.call-done, bf16[2048]{0:T(1024)(128)(2,1)S(1)} %broadcast_bitcast_fusion.1), kind=kOutput, calls=%fused_computation.42 | convolution fusion | flops 2419654656 | bytes 9048064 | tf_op jit(solution)/shard_map/dot_general | solution.py:10
  406.6 7.0 %fusion.59 = bf16[1,384,1536]{1,2,0:T(8,128)(2,1)S(1)} fusion(bf16[2048,384]{1,0:T(8,128)(2,1)} %bitcast.74, bf16[2048,1536]{1,0:T(8,128)(2,1)} %all-gather.4.cloned.1.call-done, bf16[2048]{0:T(1024)(128)(2,1)S(1)} %broadcast_bitcast_fusion), kind=kOutput, calls=%fused_computation.41 | convolution fusion | flops 2419654656 | bytes 9048064 | tf_op jit(solution)/shard_map/dot_general | solution.py:10
  413.6 6.4 %fusion.65 = bf16[1,384,1536]{1,2,0:T(8,128)(2,1)S(1)} fusion(bf16[2048,384]{1,0:T(8,128)(2,1)S(1)} %bitcast.77, bf16[2048,1536]{1,0:T(8,128)(2,1)} %all-gather.4.cloned.1.call-done, bf16[2048]{0:T(1024)(128)(2,1)S(1)} %broadcast_bitcast_fusion.1), kind=kOutput, calls=%fused_computation.43 | convolution fusion | flops 2419654656 | bytes 9048064 | tf_op jit(solution)/shard_map/dot_general | solution.py:10
  420.3 2.8 copy.26
  423.2 6.9 %fusion.50 = bf16[1,1536,384]{2,1,0:T(8,128)(2,1)S(1)} fusion(bf16[2048,384]{1,0:T(8,128)(2,1)} %bitcast.72, bf16[2048,1536]{1,0:T(8,128)(2,1)} %all-gather.8.cloned.1.call-done, bf16[2048]{0:T(1024)(128)(2,1)S(1)} %broadcast_bitcast_fusion), kind=kOutput, calls=%fused_computation.38 | convolution fusion | flops 2419654656 | bytes 9048064 | tf_op jit(solution)/shard_map/dot_general | solution.py:10
  430.1 3.7 fusion.53
  435.5 21.6 %reduce-scatter.5.cloned.1.call-done = f32[128,768]{1,0:T(8,128)} async-done(((f32[128,6144]{1,0:T(8,128)}), f32[128,768]{1,0:T(8,128)}) %reduce-scatter.5.cloned.1.call-update) | async-done | bytes 393232 | tf_op jit(solution)/shard_map/reduce_scatter | solution.py:88
  (58 shorter events, 24.8 us)
Async XLA Ops:
  9.7 6.4 %copy-start.12 = (s32[16]{0:T(128)S(1)}, s32[16]{0:T(128)}, u32[]{:S(2)}) copy-start(s32[16]{0:T(128)} %param.17) | copy-start | bytes 196
  9.7 26.0 %all-to-all-start = ((bf16[128,16,384]{0,2,1:T(8,128)(2,1)}), bf16[128,16,384]{0,2,1:T(8,128)(2,1)S(1)}, u32[]{:S(2)}, u32[]{:S(2)}) async-start(bf16[128,16,384]{0,2,1:T(8,128)(2,1)} %bitcast), calls=%async_computation | async-start | bytes 3145728 | tf_op jit(solution)/shard_map/all_to_all | solution.py:33
  16.1 177.4 %reduce-scatter.3.cloned.1.call-start = ((), (), s32[]{:S(2)}) async-start(), calls=%async_computation.5 | async-start | bytes 13369344 | tf_op jit(solution)/shard_map/reduce_scatter | solution.py:69
  40.6 5.4 %copy-start = (bf16[2,1536,384]{2,1,0:T(8,128)(2,1)S(1)}, bf16[2,1536,384]{2,1,0:T(8,128)(2,1)}, u32[]{:S(2)}) copy-start(bf16[2,1536,384]{2,1,0:T(8,128)(2,1)} %param.15) | copy-start | bytes 7077892
  52.6 140.9 %copy-start.5 = (bf16[128,1536]{1,0:T(8,128)(2,1)S(1)}, bf16[128,1536]{1,0:T(8,128)(2,1)}, u32[]{:S(2)}) copy-start(bf16[128,1536]{1,0:T(8,128)(2,1)} %param.12) | copy-start | bytes 1179652
  52.6 140.9 %copy-start.6 = (bf16[128,1536]{1,0:T(8,128)(2,1)S(1)}, bf16[128,1536]{1,0:T(8,128)(2,1)}, u32[]{:S(2)}) copy-start(bf16[128,1536]{1,0:T(8,128)(2,1)} %param.11) | copy-start | bytes 1179652
  52.6 186.6 %all-gather.6.cloned.1.call-start = ((), (), s32[]{:S(2)}) async-start(), calls=%async_computation.7 | async-start | bytes 6684672 | tf_op jit(solution)/shard_map/all_gather | solution.py:77
  196.1 88.6 %all-gather.4.cloned.1.call-start = ((), (), s32[]{:S(2)}) async-start(), calls=%async_computation.6 | async-start | bytes 6684672 | tf_op jit(solution)/shard_map/all_gather | solution.py:76
  196.8 226.3 %all-gather.8.cloned.1.call-start = ((), (), s32[]{:S(2)}) async-start(), calls=%async_computation.9 | async-start | bytes 6684672 | tf_op jit(solution)/shard_map/all_gather | solution.py:75
  239.2 8.4 %copy-start.8 = (bf16[2048,1536]{1,0:T(8,128)(2,1)S(1)}, bf16[2048,1536]{1,0:T(8,128)(2,1)}, u32[]{:S(2)}) copy-start(bf16[2048,1536]{1,0:T(8,128)(2,1)} %all-gather.6.cloned.1.call-done) | copy-start | bytes 18874372
  239.2 8.4 %copy-start.10 = (bf16[2,384,1536]{2,1,0:T(8,128)(2,1)S(1)}, bf16[2,384,1536]{2,1,0:T(8,128)(2,1)}, u32[]{:S(2)}) copy-start(bf16[2,384,1536]{2,1,0:T(8,128)(2,1)} %param.14) | copy-start | bytes 7077892
  284.6 6.2 %copy-start.9 = (bf16[2048,1536]{1,0:T(8,128)(2,1)S(1)}, bf16[2048,1536]{1,0:T(8,128)(2,1)}, u32[]{:S(2)}) copy-start(bf16[2048,1536]{1,0:T(8,128)(2,1)} %all-gather.4.cloned.1.call-done) | copy-start | bytes 18874372
  284.6 6.2 %copy-start.11 = (bf16[2,384,1536]{2,1,0:T(8,128)(2,1)S(1)}, bf16[2,384,1536]{2,1,0:T(8,128)(2,1)}, u32[]{:S(2)}) copy-start(bf16[2,384,1536]{2,1,0:T(8,128)(2,1)} %param.13) | copy-start | bytes 7077892
  284.6 6.6 %copy-start.13 = (f32[2048,384]{1,0:T(8,128)S(1)}, f32[2048,384]{1,0:T(8,128)}, u32[]{:S(2)}) copy-start(f32[2048,384]{1,0:T(8,128)} %fusion.14) | copy-start | bytes 9437188
  284.6 7.5 %copy-start.14 = (f32[2048,384]{1,0:T(8,128)S(1)}, f32[2048,384]{1,0:T(8,128)}, u32[]{:S(2)}) copy-start(f32[2048,384]{1,0:T(8,128)} %fusion.6) | copy-start | bytes 9437188
  297.4 5.6 %copy-start.1 = (bf16[128,6144]{1,0:T(8,128)(2,1)S(1)}, bf16[128,6144]{1,0:T(8,128)(2,1)}, u32[]{:S(2)}) copy-start(bf16[128,6144]{1,0:T(8,128)(2,1)} %param.9) | copy-start | bytes 4718596
  297.4 63.3 %all-to-all-start.1 = ((f32[16,128,384]{2,1,0:T(8,128)}), f32[16,128,384]{2,1,0:T(8,128)}, u32[]{:S(2)}, u32[]{:S(2)}) async-start(f32[16,128,384]{2,1,0:T(8,128)} %bitcast.71), calls=%async_computation.2 | async-start | bytes 6291456 | tf_op jit(solution)/shard_map/all_to_all | solution.py:87
  360.7 26.9 %all-to-all-start.2 = ((bf16[128,16,384]{0,2,1:T(8,128)(2,1)}), bf16[128,16,384]{0,2,1:T(8,128)(2,1)S(1)}, u32[]{:S(2)}, u32[]{:S(2)}) async-start(bf16[128,16,384]{0,2,1:T(8,128)(2,1)} %bitcast.15), calls=%async_computation.4 | async-start | bytes 3145728 | tf_op jit(solution)/shard_map/all_to_all | solution.py:32
  368.0 89.1 %reduce-scatter.5.cloned.1.call-start = ((), (), s32[]{:S(2)}) async-start(), calls=%async_computation.8 | async-start | bytes 3538944 | tf_op jit(solution)/shard_map/reduce_scatter | solution.py:88
  389.2 1.6 copy-start.3
  406.6 7.0 %copy-start.4 = (bf16[16,128,384]{2,1,0:T(8,128)(2,1)S(1)}, bf16[16,128,384]{2,1,0:T(8,128)(2,1)}, u32[]{:S(2)}) copy-start(bf16[16,128,384]{2,1,0:T(8,128)(2,1)} %copy.24) | copy-start | bytes 4718596
  423.1 7.0 %copy-start.2 = (bf16[16,128,384]{2,1,0:T(8,128)(2,1)S(1)}, bf16[16,128,384]{2,1,0:T(8,128)(2,1)}, u32[]{:S(2)}) copy-start(bf16[16,128,384]{2,1,0:T(8,128)(2,1)} %copy.25) | copy-start | bytes 4718596
  423.1 7.0 %copy-start.7 = (bf16[2048,1536]{1,0:T(8,128)(2,1)S(1)}, bf16[2048,1536]{1,0:T(8,128)(2,1)}, u32[]{:S(2)}) copy-start(bf16[2048,1536]{1,0:T(8,128)(2,1)} %all-gather.8.cloned.1.call-done) | copy-start | bytes 18874372
Sparse Core Ops, SparseCore 0:
  52.7 140.6 reduce-scatter.2
  196.2 42.9 all-gather.5
  241.5 43.1 all-gather.3
  286.2 78.5 all-gather.7
  372.6 84.4 reduce-scatter.4
where the time goes:
time: 473 us; the launch traced here: 466 us
  waiting for transfers between devices  327 us (69%)
  matrix products  73.9 us (16%)
  local copies, waits for them, and re-layouts  21.6 us (5%)
  starting transfers between devices  20.2 us (4%)
  between operations  14.9 us (3%)
  other arithmetic  7.93 us (2%)
    reduce_scatter x1, waiting for transfers between devices, shards(): lax.psum_scatter(result, 'dp', scatter_dimension=0, tiled=True)  140 us
    all_to_all x1, waiting for transfers between devices, shards(): lax.all_to_all(partial_all, 'dp', split_axis=0, concat_axis=1, tiled=True)  56.2 us
    all_gather x1, waiting for transfers between devices, shards(): lax.all_gather(up_grad, 'dp', axis=0, tiled=True)  41.7 us
    dot_general x6, matrix products, contract_cols(): lax.dot_general(left_op, right_op, (((1,), (1,)), ((), ())), preferred_el...  37.1 us
    dot_general x6, matrix products, contract_rows(): lax.dot_general(left_op, right_op, (((0,), (0,)), ((), ())), preferred_el...  36.8 us
    all_gather x1, waiting for transfers between devices, shards(): lax.all_gather(gate_grad, 'dp', axis=0, tiled=True)  31.8 us
    reduce_scatter x1, waiting for transfers between devices, shards(): lax.psum_scatter(input_rows, 'tensor', scatter_dimension=1, tiled=True)  21.6 us
    all_to_all x1, waiting for transfers between devices, shards(): lax.all_to_all(out_grad, 'dp', split_axis=1, concat_axis=0, tiled=True)  19.7 us
  transfers between devices with their start and end apart: 8, of which 7 were waited for; matrix products, arithmetic and copies ran while one was open for 17% of the time, Pallas kernels for 0%

commit v1 on v0

v1 whole, which is shorter than its diff:
```python
import numpy as np
import jax
import jax.numpy as jnp
from jax import lax
from jax.sharding import Mesh
from jax.sharding import PartitionSpec as P

BLOCK = 128
AXES = ("x", "ylo", "core", "z", "yhi")
SIZES = (4, 2, 2, 4, 2)
DP = ("x", "ylo", "core")
TP = ("z", "yhi")
CHIPS = ("x", "ylo")
N_DP = 16
N_TP = 8


def rank_of_pos(pos):
    core, x, ylo = pos // 8, (pos % 8) // 2, pos % 2
    return x * 4 + ylo * 2 + core


POS_RANK = np.array([rank_of_pos(p) for p in range(N_DP)], np.int32)


def deliver_perm(k):
    pairs = []
    for i in range(N_DP):
        for t in range(N_TP):
            dest = rank_of_pos(2 * t + ((i % 2) ^ k))
            pairs.append((i * N_TP + t, dest * N_TP + i // 2))
    return pairs


def contract_rows(left_op, right_op):
    return lax.dot_general(
        left_op, right_op, (((0,), (0,)), ((), ())), preferred_element_type=jnp.float32
    )


def contract_cols(left_op, right_op):
    return lax.dot_general(
        left_op, right_op, (((1,), (1,)), ((), ())), preferred_element_type=jnp.float32
    )


def expert_masks(block_expert, row_count, expert_count):
    spread = jnp.broadcast_to(block_expert[:, None], (row_count // BLOCK, BLOCK)).reshape(
        row_count, 1
    )
    return [(spread == which).astype(jnp.bfloat16) for which in range(expert_count)]


def to_gathered_order(cols):
    width = cols.shape[1]
    return cols.reshape(4, 2, 2, BLOCK, width).transpose(2, 0, 1, 3, 4).reshape(-1, width)


def shards(rows_in, out_grad, gate_pre, up_pre, w_gate, w_up, w_down, live_rows, block_expert):
    rows_dev = rows_in.shape[0]
    expert_count = w_gate.shape[0]
    ff = gate_pre.shape[1]
    dy_cols = to_gathered_order(
        lax.all_to_all(out_grad, DP, split_axis=1, concat_axis=0, tiled=True)
    )
    x_cols = to_gathered_order(
        lax.all_to_all(rows_in, DP, split_axis=1, concat_axis=0, tiled=True)
    )
    row_count = dy_cols.shape[0]
    expert_g = jnp.take(block_expert, jnp.asarray(POS_RANK), axis=0)
    masks = expert_masks(expert_g, row_count, expert_count)

    positions = jnp.arange(rows_dev, dtype=jnp.int32)[:, None]
    row_mask = (positions < live_rows[0]).astype(jnp.float32)
    gate_vals = gate_pre.astype(jnp.float32)
    up_vals = up_pre.astype(jnp.float32)
    sigmoid = jax.nn.sigmoid(gate_vals)
    silu_vals = gate_vals * sigmoid
    hidden = (silu_vals * up_vals * row_mask).astype(jnp.bfloat16)

    result = jnp.zeros((row_count, ff), jnp.float32)
    for which in range(expert_count):
        result = result + contract_cols(dy_cols * masks[which], w_down[which])
    result = lax.psum_scatter(
        result.reshape(2, row_count // 2, ff), "core", scatter_dimension=0, tiled=True
    ).reshape(row_count // 2, ff)
    hidden_grad = lax.psum_scatter(result, CHIPS, scatter_dimension=0, tiled=True)

    up_grad = (hidden_grad * silu_vals * row_mask).astype(jnp.bfloat16)
    gate_grad = (
        hidden_grad * up_vals * sigmoid * (1.0 + gate_vals * (1.0 - sigmoid)) * row_mask
    ).astype(jnp.bfloat16)
    packed = jnp.stack([hidden, gate_grad, up_grad], axis=1)
    packed = lax.all_gather(packed, CHIPS, axis=0, tiled=True)
    packed = lax.all_gather(packed, "core", axis=0, tiled=True)
    hid_g, gate_g, up_g = packed[:, 0], packed[:, 1], packed[:, 2]

    down_terms = []
    gate_terms = []
    up_terms = []
    partial_rows = jnp.zeros((row_count, w_gate.shape[1]), jnp.float32)
    for which in range(expert_count):
        down_terms.append(contract_rows(hid_g * masks[which], dy_cols))
        gate_masked = gate_g * masks[which]
        up_masked = up_g * masks[which]
        gate_terms.append(contract_rows(x_cols, gate_masked))
        up_terms.append(contract_rows(x_cols, up_masked))
        partial_rows = (
            partial_rows
            + contract_cols(gate_masked, w_gate[which])
            + contract_cols(up_masked, w_up[which])
        )
    down_total = jnp.stack(down_terms, 0)
    gate_total = jnp.stack(gate_terms, 0)
    up_total = jnp.stack(up_terms, 0)

    width = partial_rows.shape[1]
    summed = lax.psum_scatter(
        partial_rows.reshape(N_TP, row_count // N_TP, width), TP, scatter_dimension=0, tiled=True
    ).reshape(2, rows_dev, width)
    core = lax.axis_index("core")
    ylo = lax.axis_index("ylo")
    got = []
    for k in range(2):
        piece = lax.dynamic_index_in_dim(summed, core ^ k, 0, keepdims=False)
        got.append(lax.ppermute(piece, AXES, deliver_perm(k)))
    first = jnp.where(ylo == 0, got[0], got[1])
    second = jnp.where(ylo == 0, got[1], got[0])
    input_grad = jnp.concatenate([first, second], axis=1).astype(jnp.bfloat16)
    return (
        input_grad,
        gate_total.astype(jnp.bfloat16),
        up_total.astype(jnp.bfloat16),
        down_total.astype(jnp.bfloat16),
    )


def solution(mesh):
    fine = Mesh(mesh.devices.reshape(SIZES), AXES)
    return jax.shard_map(
        shards,
        mesh=fine,
        in_specs=(
            P(DP, None),
            P(DP, None),
            P(DP, TP),
            P(DP, TP),
            P(None, DP, TP),
            P(None, DP, TP),
            P(None, TP, DP),
            P(DP),
            P(),
        ),
        out_specs=(
            P(DP, TP),
            P(None, DP, TP),
            P(None, DP, TP),
            P(None, TP, DP),
        ),
        check_vma=False,
    )
```

time: 473 us -> 582 us (1.23)
  waiting for transfers between devices: 327 us -> 439 us
  matrix products: 73.9 us -> 65.2 us
    all_gather x3 -> x2, waiting for transfers between devices: 73.4 us -> 218 us  [the longest x1 189 us: shards(): packed = lax.all_gather(packed, CHIPS, axis=0, tiled=True)]
    all_to_all x3 -> x2, waiting for transfers between devices: 91 us -> 18.6 us  [the longest x1 18.5 us: shards(): lax.all_to_all(out_grad, DP, split_axis=1, concat_axis=0, tiled=True)]
    reduce_scatter x2 -> x3, waiting for transfers between devices: 162 us -> 203 us  [the longest x1 132 us: shards(): lax.psum_scatter(result, CHIPS, scatter_dimension=0, tiled=True)]
    ppermute x0 -> x2, starting transfers between devices: none -> 7.83 us  [shards(): got.append(lax.ppermute(piece, AXES, deliver_perm(k)))]
    dot_general x6, matrix products: 36.8 us -> 29.3 us  [contract_rows(): lax.dot_general(left_op, right_op, (((0,), (0,)), ((), ())), preferred_el...]
    all_to_all x3 -> x2, starting transfers between devices: 19.1 us -> 12.5 us  [the longest x1 6.31 us: shards(): lax.all_to_all(out_grad, DP, split_axis=1, concat_axis=0, tiled=True)]
    another operation x3 -> x6, other arithmetic: 2.21 us -> 8.69 us  [the longest x1 2.94 us: shards(): down_total = jnp.stack(down_terms, 0)]
    unnamed x34 -> x40, local copies, waits for them, and re-layouts: 11 us -> 17.2 us
  transfers between devices with their start and end apart: 8 -> 9, of which waited for: 7 -> 6; matrix products, arithmetic and copies ran while one was open for 17% -> 13% of each run, Pallas kernels for 0% -> 0%
where the time goes in v1:
time: 582 us; the launch traced here: 575 us
  waiting for transfers between devices  439 us (75%)
  matrix products  65.2 us (11%)
  local copies, waits for them, and re-layouts  24.7 us (4%)
  starting transfers between devices  20.7 us (4%)
  between operations  15.2 us (3%)
  other arithmetic  9.76 us (2%)
    all_gather x1, waiting for transfers between devices, shards(): packed = lax.all_gather(packed, CHIPS, axis=0, tiled=True)  189 us
    reduce_scatter x1, waiting for transfers between devices, shards(): lax.psum_scatter(result, CHIPS, scatter_dimension=0, tiled=True)  132 us
    reduce_scatter x1, waiting for transfers between devices, shards(): lax.psum_scatter(partial_rows.reshape(N_TP, row_count // N_TP, width), TP...  43.1 us
    dot_general x6, matrix products, contract_cols(): lax.dot_general(left_op, right_op, (((1,), (1,)), ((), ())), preferred_el...  36 us
    dot_general x6, matrix products, contract_rows(): lax.dot_general(left_op, right_op, (((0,), (0,)), ((), ())), preferred_el...  29.3 us
    all_gather x1, waiting for transfers between devices, shards(): packed = lax.all_gather(packed, 'core', axis=0, tiled=True)  28.6 us
    reduce_scatter x1, waiting for transfers between devices, shards(): lax.psum_scatter(result.reshape(2, row_count // 2, ff), 'core', scatter_d...  27.3 us
    all_to_all x1, waiting for transfers between devices, shards(): lax.all_to_all(out_grad, DP, split_axis=1, concat_axis=0, tiled=True)  18.5 us
  transfers between devices with their start and end apart: 9, of which 6 were waited for; matrix products, arithmetic and copies ran while one was open for 13% of the time, Pallas kernels for 0%

profile of v1, /device:TPU:3, one launch (start us, length us, event | category | flops | bytes accessed | tf_op | source)
XLA Modules:
  0.0 574.7 jit_solution(3465949403237092074)
XLA Ops:
  9.8 6.3 %all-to-all-start = ((bf16[128,16,384]{0,2,1:T(8,128)(2,1)}), bf16[128,16,384]{0,2,1:T(8,128)(2,1)S(1)}, u32[]{:S(2)}, u32[]{:S(2)}) async-start(bf16[128,16,384]{0,2,1:T(8,128)(2,1)} %bitcast.2), calls=%async_computation | async-start | bytes 3145728 | tf_op jit(solution)/shard_map/all_to_all | solution.py:64
  17.2 18.5 %all-to-all-done = bf16[128,16,384]{0,2,1:T(8,128)(2,1)S(1)} async-done(((bf16[128,16,384]{0,2,1:T(8,128)(2,1)}), bf16[128,16,384]{0,2,1:T(8,128)(2,1)S(1)}, u32[]{:S(2)}, u32[]{:S(2)}) %all-to-all-start) | async-done | bytes 1572896 | tf_op jit(solution)/shard_map/all_to_all | solution.py:64
  38.9 3.5 fusion.77
  42.4 6.5 %convolution_add_fusion = f32[2048,1536]{1,0:T(8,128)} fusion(f32[2048,1536]{1,0:T(8,128)S(1)} %fusion.77, bf16[2048,384]{1,0:T(8,128)(2,1)S(1)} %bitcast.138, bf16[2,1536,384]{2,1,0:T(8,128)(2,1)S(1)} %copy-done.2), kind=kOutput, calls=%fused_computation.1 | convolution fusion | flops 2419064832 | bytes 27918336 | tf_op jit(solution)/shard_map/dot_general | solution.py:42
  49.0 27.3 %reduce-scatter.4.cloned.1.call-done = f32[1,1024,1536]{2,1,0:T(8,128)} async-done(((f32[2,1024,1536]{2,1,0:T(8,128)}), f32[1,1024,1536]{2,1,0:T(8,128)}) %reduce-scatter.4.cloned.1.call-update) | async-done | bytes 6291472 | tf_op jit(solution)/shard_map/reduce_scatter | solution.py:84
  77.0 132.4 %reduce-scatter.6.cloned.1.call-done = f32[128,1536]{1,0:T(8,128)} async-done(((f32[1024,1536]{1,0:T(8,128)}), f32[128,1536]{1,0:T(8,128)}) %reduce-scatter.6.cloned.1.call-update) | async-done | bytes 786448 | tf_op jit(solution)/shard_map/reduce_scatter | solution.py:87
  212.3 189.2 %all-gather.3.cloned.1.call-done = bf16[1024,3,1536]{2,0,1:T(8,128)(2,1)} async-done(((bf16[128,3,1536]{2,0,1:T(8,128)(2,1)}), bf16[1024,3,1536]{2,0,1:T(8,128)(2,1)}) %all-gather.3.cloned.1.call-update) | async-done | bytes 9437200 | tf_op jit(solution)/shard_map/all_gather | solution.py:94
  404.5 6.2 %all-to-all-start.1 = ((bf16[128,16,384]{0,2,1:T(8,128)(2,1)}), bf16[128,16,384]{0,2,1:T(8,128)(2,1)S(1)}, u32[]{:S(2)}, u32[]{:S(2)}) async-start(bf16[128,16,384]{0,2,1:T(8,128)(2,1)} %bitcast.142), calls=%async_computation.4 | async-start | bytes 3145728 | tf_op jit(solution)/shard_map/all_to_all | solution.py:67
  410.9 28.6 %all-gather.5.cloned.1.call-done = bf16[2048,3,1536]{2,0,1:T(8,128)(2,1)} async-done(((bf16[1024,3,1536]{2,0,1:T(8,128)(2,1)}), bf16[2048,3,1536]{2,0,1:T(8,128)(2,1)}) %all-gather.5.cloned.1.call-update) | async-done | bytes 18874384 | tf_op jit(solution)/shard_map/all_gather | solution.py:95
  439.5 8.4 %fusion.6 = f32[2048,384]{1,0:T(8,128)} fusion(bf16[2048,3,1536]{2,0,1:T(8,128)(2,1)} %all-gather.5.cloned.1.call-done, bf16[2048]{0:T(1024)(128)(2,1)S(1)} %get-tuple-element.31, bf16[2,384,1536]{2,1,0:T(8,128)(2,1)} %param.15), kind=kOutput, calls=%fused_computation.8 | convolution fusion | flops 2419064832 | bytes 10620928 | tf_op jit(solution)/shard_map/dot_general | solution.py:42
  449.8 5.2 fusion.14
  455.1 5.2 fusion.18
  460.2 7.3 %add_add_fusion = f32[2048,384]{1,0:T(8,128)} fusion(f32[2048,384]{1,0:T(8,128)} %fusion.6, f32[2048,384]{1,0:T(8,128)} %fusion.18, f32[2048,384]{1,0:T(8,128)} %fusion.14, bf16[2048,3,1536]{2,0,1:T(8,128)(2,1)S(1)} %copy-done.10, bf16[2048]{0:T(1024)(128)(2,1)S(1)} %get-tuple-element.31, bf16[2,384,1536]{2,1,0:T(8,128)(2,1)S(1)} %copy-done.12), kind=kOutput, calls=%fused_computation.30 | convolution fusion | flops 2421424128 | bytes 20058112 | tf_op jit(solution)/shard_map/dot_general | solution.py:42
  470.9 6.5 %fusion.63 = bf16[1,384,1536]{1,2,0:T(8,128)(2,1)S(1)} fusion(bf16[2048,384]{1,0:T(8,128)(2,1)S(1)} %bitcast.147, bf16[2048,3,1536]{2,0,1:T(8,128)(2,1)} %all-gather.5.cloned.1.call-done, bf16[2048]{0:T(1024)(128)(2,1)S(1)} %get-tuple-element.31), kind=kOutput, calls=%fused_computation.50 | convolution fusion | flops 2419654656 | bytes 9048064 | tf_op jit(solution)/shard_map/dot_general | solution.py:36
  477.5 6.7 %fusion.69 = bf16[1,384,1536]{1,2,0:T(8,128)(2,1)S(1)} fusion(bf16[2048,384]{1,0:T(8,128)(2,1)S(1)} %bitcast.148, bf16[2048,3,1536]{2,0,1:T(8,128)(2,1)} %all-gather.5.cloned.1.call-done, bf16[2048]{0:T(1024)(128)(2,1)S(1)} %get-tuple-element.32), kind=kOutput, calls=%fused_computation.52 | convolution fusion | flops 2419654656 | bytes 9048064 | tf_op jit(solution)/shard_map/dot_general | solution.py:36
  485.6 3.7 fusion.60
  489.3 3.9 fusion.66
  495.2 3.7 fusion.54
  498.9 4.7 fusion.57
  503.6 43.1 %reduce-scatter.8.cloned.1.call-done = f32[1,256,384]{2,1,0:T(8,128)} async-done(((f32[8,256,384]{2,1,0:T(8,128)}), f32[1,256,384]{2,1,0:T(8,128)}) %reduce-scatter.8.cloned.1.call-update) | async-done | bytes 393232 | tf_op jit(solution)/shard_map/reduce_scatter | solution.py:118
  548.5 4.6 collective-permute-start
  553.1 3.2 collective-permute-start.1
  556.3 2.9 pad_maximum_fusion.2
  561.8 4.3 copy.39
  (75 shorter events, 27.7 us)
Async XLA Ops:
  7.2 9.0 %copy-start = (s32[16]{0:T(128)S(1)}, s32[16]{0:T(128)}, u32[]{:S(2)}) copy-start(s32[16]{0:T(128)} %param.18) | copy-start | bytes 196
  9.8 6.4 %copy-start.9 = (s32[16]{0:T(128)S(1)}, s32[16]{0:T(128)}, u32[]{:S(2)}) copy-start(s32[16]{0:T(128)} %constant.52) | copy-start | bytes 196
  9.8 26.0 %all-to-all-start = ((bf16[128,16,384]{0,2,1:T(8,128)(2,1)}), bf16[128,16,384]{0,2,1:T(8,128)(2,1)S(1)}, u32[]{:S(2)}, u32[]{:S(2)}) async-start(bf16[128,16,384]{0,2,1:T(8,128)(2,1)} %bitcast.2), calls=%async_computation | async-start | bytes 3145728 | tf_op jit(solution)/shard_map/all_to_all | solution.py:64
  16.1 60.2 %reduce-scatter.4.cloned.1.call-start = ((), (), s32[]{:S(2)}) async-start(), calls=%async_computation.5 | async-start | bytes 18874368 | tf_op jit(solution)/shard_map/reduce_scatter | solution.py:84
  48.9 160.5 %reduce-scatter.6.cloned.1.call-start = ((), (), s32[]{:S(2)}) async-start(), calls=%async_computation.6 | async-start | bytes 7077888 | tf_op jit(solution)/shard_map/reduce_scatter | solution.py:87
  76.2 133.2 %copy-start.7 = (bf16[128,1536]{1,0:T(8,128)(2,1)S(1)}, bf16[128,1536]{1,0:T(8,128)(2,1)}, u32[]{:S(2)}) copy-start(bf16[128,1536]{1,0:T(8,128)(2,1)} %param.12) | copy-start | bytes 1179652
  76.2 133.2 %copy-start.8 = (bf16[128,1536]{1,0:T(8,128)(2,1)S(1)}, bf16[128,1536]{1,0:T(8,128)(2,1)}, u32[]{:S(2)}) copy-start(bf16[128,1536]{1,0:T(8,128)(2,1)} %param.13) | copy-start | bytes 1179652
  76.3 325.3 %all-gather.3.cloned.1.call-start = ((), (), s32[]{:S(2)}) async-start(), calls=%async_computation.7 | async-start | bytes 10616832 | tf_op jit(solution)/shard_map/all_gather | solution.py:94
  212.3 227.2 %all-gather.5.cloned.1.call-start = ((), (), s32[]{:S(2)}) async-start(), calls=%async_computation.8 | async-start | bytes 28311552 | tf_op jit(solution)/shard_map/all_gather | solution.py:95
  404.5 63.0 %all-to-all-start.1 = ((bf16[128,16,384]{0,2,1:T(8,128)(2,1)}), bf16[128,16,384]{0,2,1:T(8,128)(2,1)S(1)}, u32[]{:S(2)}, u32[]{:S(2)}) async-start(bf16[128,16,384]{0,2,1:T(8,128)(2,1)} %bitcast.142), calls=%async_computation.4 | async-start | bytes 3145728 | tf_op jit(solution)/shard_map/all_to_all | solution.py:67
  410.6 136.1 %reduce-scatter.8.cloned.1.call-start = ((), (), s32[]{:S(2)}) async-start(), calls=%async_computation.9 | async-start | bytes 3538944 | tf_op jit(solution)/shard_map/reduce_scatter | solution.py:118
  439.5 9.7 %copy-start.10 = (bf16[2048,3,1536]{2,0,1:T(8,128)(2,1)S(1)}, bf16[2048,3,1536]{2,0,1:T(8,128)(2,1)}, u32[]{:S(2)}) copy-start(bf16[2048,3,1536]{2,0,1:T(8,128)(2,1)} %all-gather.5.cloned.1.call-done) | copy-start | bytes 56623108
  439.5 10.3 %copy-start.11 = (bf16[2,384,1536]{2,1,0:T(8,128)(2,1)S(1)}, bf16[2,384,1536]{2,1,0:T(8,128)(2,1)}, u32[]{:S(2)}) copy-start(bf16[2,384,1536]{2,1,0:T(8,128)(2,1)} %param.15) | copy-start | bytes 7077892
  449.8 5.2 copy-start.12
  469.1 1.8 copy-start.5
  470.9 13.6 %slice-start = ((s8[18874368]{0:T(1024)(128)(4,1)}), s8[4194304]{0:T(1024)(128)(4,1)S(1)}, s32[]{:S(2)}) async-start(s8[18874368]{0:T(1024)(128)(4,1)} %bitcast.152), calls=%async_computation.10 | async-start | bytes 8388608
  470.9 13.6 %slice-start.1 = ((s8[18874368]{0:T(1024)(128)(4,1)}), s8[4194304]{0:T(1024)(128)(4,1)S(1)}, s32[]{:S(2)}) async-start(s8[18874368]{0:T(1024)(128)(4,1)} %bitcast.152), calls=%async_computation.11 | async-start | bytes 8388608
  470.9 13.6 %slice-start.2 = ((s8[18874368]{0:T(1024)(128)(4,1)}), s8[4194304]{0:T(1024)(128)(4,1)S(1)}, s32[]{:S(2)}) async-start(s8[18874368]{0:T(1024)(128)(4,1)} %bitcast.152), calls=%async_computation.12 | async-start | bytes 8388608
  477.4 7.1 %slice-start.3 = ((s8[18874368]{0:T(1024)(128)(4,1)}), s8[4194304]{0:T(1024)(128)(4,1)S(1)}, s32[]{:S(2)}) async-start(s8[18874368]{0:T(1024)(128)(4,1)} %bitcast.152), calls=%async_computation.13 | async-start | bytes 8388608
  477.4 7.1 %slice-start.4 = ((s8[18874368]{0:T(1024)(128)(4,1)}), s8[2097152]{0:T(1024)(128)(4,1)S(1)}, s32[]{:S(2)}) async-start(s8[18874368]{0:T(1024)(128)(4,1)} %bitcast.152), calls=%async_computation.14 | async-start | bytes 4194304
  493.2 2.0 copy-start.4
  548.5 17.6 %collective-permute-start = (bf16[128,384]{1,0:T(8,128)(2,1)}, bf16[128,384]{1,0:T(8,128)(2,1)}, u32[]{:S(2)}, u32[]{:S(2)}) collective-permute-start(bf16[128,384]{1,0:T(8,128)(2,1)} %get-tuple-element.25), channel_id=1, source_target_pairs={{0,0},{1,32},{2,64},{3,96},{4,8},{5,40},{6,72},{7,104},{8,16},{9,4... | collective-permute-start | bytes 294920 | tf_op jit(solution)/shard_map/ppermute | solution.py:126
  553.1 13.0 %collective-permute-start.1 = (bf16[128,384]{1,0:T(8,128)(2,1)}, bf16[128,384]{1,0:T(8,128)(2,1)}, u32[]{:S(2)}, u32[]{:S(2)}) collective-permute-start(bf16[128,384]{1,0:T(8,128)(2,1)} %get-tuple-element.26), channel_id=1, source_target_pairs={{0,16},{1,48},{2,80},{3,112},{4,24},{5,56},{6,88},{7,120},{8,0},{9... | collective-permute-start | bytes 294920 | tf_op jit(solution)/shard_map/ppermute | solution.py:126
  559.2 8.5 %copy-start.1 = (s32[16]{0:T(128)S(1)}, s32[16]{0:T(128)}, u32[]{:S(2)}) copy-start(s32[16]{0:T(128)} %param.18) | copy-start | bytes 196
  (3 other events, 4.5 us)
Sparse Core Ops, SparseCore 0:
  49.1 27.1 reduce-scatter.3
  78.6 130.7 reduce-scatter.5
  212.4 189.0 all-gather.2
  403.0 36.4 all-gather.4
  467.6 79.0 reduce-scatter.7

commit v2 on v1

--- a/solution.py
+++ b/solution.py
@@ -27,7 +27,7 @@
     pairs = []
     for i in range(N_DP):
         for t in range(N_TP):
-            dest = rank_of_pos(2 * t + ((i % 2) ^ k))
+            dest = 2 * t + ((i % 2) ^ k)
             pairs.append((i * N_TP + t, dest * N_TP + i // 2))
     return pairs
 
@@ -60,15 +60,12 @@
     rows_dev = rows_in.shape[0]
     expert_count = w_gate.shape[0]
     ff = gate_pre.shape[1]
-    dy_cols = to_gathered_order(
-        lax.all_to_all(out_grad, DP, split_axis=1, concat_axis=0, tiled=True)
-    )
-    x_cols = to_gathered_order(
-        lax.all_to_all(rows_in, DP, split_axis=1, concat_axis=0, tiled=True)
-    )
+    dy_cols = lax.all_to_all(out_grad, DP, split_axis=1, concat_axis=0, tiled=True)
+    x_cols = lax.all_to_all(rows_in, DP, split_axis=1, concat_axis=0, tiled=True)
     row_count = dy_cols.shape[0]
     expert_g = jnp.take(block_expert, jnp.asarray(POS_RANK), axis=0)
-    masks = expert_masks(expert_g, row_count, expert_count)
+    masks_g = expert_masks(expert_g, row_count, expert_count)
+    masks = expert_masks(block_expert, row_count, expert_count)
 
     positions = jnp.arange(rows_dev, dtype=jnp.int32)[:, None]
     row_mask = (positions < live_rows[0]).astype(jnp.float32)
@@ -78,21 +75,24 @@
     silu_vals = gate_vals * sigmoid
     hidden = (silu_vals * up_vals * row_mask).astype(jnp.bfloat16)
 
+    dy_g = to_gathered_order(dy_cols)
     result = jnp.zeros((row_count, ff), jnp.float32)
     for which in range(expert_count):
-        result = result + contract_cols(dy_cols * masks[which], w_down[which])
+        result = result + contract_cols(dy_g * masks_g[which], w_down[which])
     result = lax.psum_scatter(
         result.reshape(2, row_count // 2, ff), "core", scatter_dimension=0, tiled=True
-    ).reshape(row_count // 2, ff)
-    hidden_grad = lax.psum_scatter(result, CHIPS, scatter_dimension=0, tiled=True)
+    ).reshape(N_DP // 2, rows_dev, ff)
+    pieces = lax.all_to_all(
+        result.astype(jnp.bfloat16), CHIPS, split_axis=0, concat_axis=0, tiled=True
+    )
+    hidden_grad = jnp.sum(pieces.astype(jnp.float32), axis=0)
 
     up_grad = (hidden_grad * silu_vals * row_mask).astype(jnp.bfloat16)
     gate_grad = (
         hidden_grad * up_vals * sigmoid * (1.0 + gate_vals * (1.0 - sigmoid)) * row_mask
     ).astype(jnp.bfloat16)
     packed = jnp.stack([hidden, gate_grad, up_grad], axis=1)
-    packed = lax.all_gather(packed, CHIPS, axis=0, tiled=True)
-    packed = lax.all_gather(packed, "core", axis=0, tiled=True)
+    packed = lax.all_gather(packed, DP, axis=0, tiled=True)
     hid_g, gate_g, up_g = packed[:, 0], packed[:, 1], packed[:, 2]
 
     down_terms = []
@@ -119,13 +119,12 @@
         partial_rows.reshape(N_TP, row_count // N_TP, width), TP, scatter_dimension=0, tiled=True
     ).reshape(2, rows_dev, width)
     core = lax.axis_index("core")
-    ylo = lax.axis_index("ylo")
     got = []
     for k in range(2):
         piece = lax.dynamic_index_in_dim(summed, core ^ k, 0, keepdims=False)
         got.append(lax.ppermute(piece, AXES, deliver_perm(k)))
-    first = jnp.where(ylo == 0, got[0], got[1])
-    second = jnp.where(ylo == 0, got[1], got[0])
+    first = jnp.where(core == 0, got[0], got[1])
+    second = jnp.where(core == 0, got[1], got[0])
     input_grad = jnp.concatenate([first, second], axis=1).astype(jnp.bfloat16)
     return (
         input_grad,

time: 582 us -> 397 us (0.68)
  the two profiles are of different devices: /device:TPU:3 before, /device:TPU:9 now
where the time goes in v2:
time: 397 us; the launch traced here: 390 us
  waiting for transfers between devices  249 us (63%)
  matrix products  65.7 us (17%)
  local copies, waits for them, and re-layouts  23.2 us (6%)
  starting transfers between devices  22.6 us (6%)
  between operations  15.2 us (4%)
  other arithmetic  13.9 us (4%)
    all_gather x1, waiting for transfers between devices, shards(): packed = lax.all_gather(packed, DP, axis=0, tiled=True)  110 us
    all_to_all x1, waiting for transfers between devices, shards(): lax.all_to_all(result.astype(jnp.bfloat16), CHIPS, split_axis=0, concat_a...  43.7 us
    reduce_scatter x1, waiting for transfers between devices, shards(): lax.psum_scatter(partial_rows.reshape(N_TP, row_count // N_TP, width), TP...  43.4 us
    dot_general x6, matrix products, contract_cols(): lax.dot_general(left_op, right_op, (((1,), (1,)), ((), ())), preferred_el...  36 us
    dot_general x6, matrix products, contract_rows(): lax.dot_general(left_op, right_op, (((0,), (0,)), ((), ())), preferred_el...  29.7 us
    reduce_scatter x1, waiting for transfers between devices, shards(): lax.psum_scatter(result.reshape(2, row_count // 2, ff), 'core', scatter_d...  25.6 us
    all_to_all x1, waiting for transfers between devices, shards(): lax.all_to_all(out_grad, DP, split_axis=1, concat_axis=0, tiled=True)  20.2 us
    unnamed x40, local copies, waits for them, and re-layouts  18 us
  transfers between devices with their start and end apart: 8, of which 6 were waited for; matrix products, arithmetic and copies ran while one was open for 18% of the time, Pallas kernels for 0%

profile of v2, /device:TPU:9, one launch (start us, length us, event | category | flops | bytes accessed | tf_op | source)
XLA Modules:
  0.0 390.0 jit_solution(11285738619436581066)
XLA Ops:
  9.7 6.2 %all-to-all-start = ((bf16[128,16,384]{0,2,1:T(8,128)(2,1)}), bf16[128,16,384]{0,2,1:T(8,128)(2,1)S(1)}, u32[]{:S(2)}, u32[]{:S(2)}) async-start(bf16[128,16,384]{0,2,1:T(8,128)(2,1)} %bitcast.2), calls=%async_computation | async-start | bytes 3145728 | tf_op jit(solution)/shard_map/all_to_all | solution.py:63
  17.1 20.2 %all-to-all-done = bf16[128,16,384]{0,2,1:T(8,128)(2,1)S(1)} async-done(((bf16[128,16,384]{0,2,1:T(8,128)(2,1)}), bf16[128,16,384]{0,2,1:T(8,128)(2,1)S(1)}, u32[]{:S(2)}, u32[]{:S(2)}) %all-to-all-start) | async-done | bytes 1572896 | tf_op jit(solution)/shard_map/all_to_all | solution.py:63
  41.2 3.5 fusion.77
  44.7 6.5 %convolution_add_fusion = f32[2048,1536]{1,0:T(8,128)} fusion(f32[2048,1536]{1,0:T(8,128)S(1)} %fusion.77, bf16[2048,384]{1,0:T(8,128)(2,1)S(1)} %bitcast.131, bf16[2,1536,384]{2,1,0:T(8,128)(2,1)S(1)} %copy-done.3), kind=kOutput, calls=%fused_computation.1 | convolution fusion | flops 2419064832 | bytes 27918336 | tf_op jit(solution)/shard_map/dot_general | solution.py:42
  51.2 25.6 %reduce-scatter.3.cloned.1.call-done = f32[1,1024,1536]{2,1,0:T(8,128)} async-done(((f32[2,1024,1536]{2,1,0:T(8,128)}), f32[1,1024,1536]{2,1,0:T(8,128)}) %reduce-scatter.3.cloned.1.call-update) | async-done | bytes 6291472 | tf_op jit(solution)/shard_map/reduce_scatter | solution.py:82
  76.9 4.8 %convert_element_type.92 = bf16[1,1024,1536]{2,1,0:T(8,128)(2,1)} convert(f32[1,1024,1536]{2,1,0:T(8,128)} %reduce-scatter.3.cloned.1.call-done) | non-fusion elementwise | flops 1572864 | bytes 9437184 | tf_op jit(solution)/shard_map/convert_element_type | solution.py:86
  81.7 5.2 %all-to-all-start.1 = ((bf16[8,128,1536]{2,1,0:T(8,128)(2,1)}), bf16[8,128,1536]{2,1,0:T(8,128)(2,1)S(1)}, u32[]{:S(2)}, u32[]{:S(2)}) async-start(bf16[8,128,1536]{2,1,0:T(8,128)(2,1)} %bitcast.130), calls=%async_computation.2 | async-start | bytes 6291456 | tf_op jit(solution)/shard_map/all_to_all | solution.py:85
  87.6 43.7 %all-to-all-done.1 = bf16[8,128,1536]{2,1,0:T(8,128)(2,1)S(1)} async-done(((bf16[8,128,1536]{2,1,0:T(8,128)(2,1)}), bf16[8,128,1536]{2,1,0:T(8,128)(2,1)S(1)}, u32[]{:S(2)}, u32[]{:S(2)}) %all-to-all-start.1) | async-done | bytes 3145760 | tf_op jit(solution)/shard_map/all_to_all | solution.py:85
  136.2 5.5 %all-to-all-start.2 = ((bf16[128,16,384]{0,2,1:T(8,128)(2,1)}), bf16[128,16,384]{0,2,1:T(8,128)(2,1)S(1)}, u32[]{:S(2)}, u32[]{:S(2)}) async-start(bf16[128,16,384]{0,2,1:T(8,128)(2,1)} %bitcast.29), calls=%async_computation.4 | async-start | bytes 3145728 | tf_op jit(solution)/shard_map/all_to_all | solution.py:64
  142.1 109.7 %all-gather.2.cloned.1.call-done = bf16[2048,3,1536]{2,0,1:T(8,128)(2,1)} async-done(((bf16[128,3,1536]{2,0,1:T(8,128)(2,1)}), bf16[2048,3,1536]{2,0,1:T(8,128)(2,1)}) %all-gather.2.cloned.1.call-update) | async-done | bytes 18874384 | tf_op jit(solution)/shard_map/all_gather | solution.py:95
  251.8 8.4 %fusion.6 = f32[2048,384]{1,0:T(8,128)} fusion(bf16[2048,3,1536]{2,0,1:T(8,128)(2,1)} %all-gather.2.cloned.1.call-done, bf16[2048]{0:T(1024)(128)(2,1)S(1)} %broadcast_bitcast_fusion, bf16[2,384,1536]{2,1,0:T(8,128)(2,1)} %param.15), kind=kOutput, calls=%fused_computation.8 | convolution fusion | flops 2419064832 | bytes 10620928 | tf_op jit(solution)/shard_map/dot_general | solution.py:42
  262.1 5.2 %fusion.14 = f32[2048,384]{1,0:T(8,128)} fusion(bf16[2048,3,1536]{2,0,1:T(8,128)(2,1)S(1)} %copy-done.10, bf16[2048]{0:T(1024)(128)(2,1)S(1)} %broadcast_bitcast_fusion.1, bf16[2,384,1536]{2,1,0:T(8,128)(2,1)S(1)} %copy-done.11), kind=kOutput, calls=%fused_computation.16 | convolution fusion | flops 2419064832 | bytes 10620928 | tf_op jit(solution)/shard_map/dot_general | solution.py:42
  267.3 5.2 %fusion.18 = f32[2048,384]{1,0:T(8,128)} fusion(bf16[2048,3,1536]{2,0,1:T(8,128)(2,1)S(1)} %copy-done.10, bf16[2048]{0:T(1024)(128)(2,1)S(1)} %broadcast_bitcast_fusion.1, bf16[2,384,1536]{2,1,0:T(8,128)(2,1)S(1)} %copy-done.12), kind=kOutput, calls=%fused_computation.20 | convolution fusion | flops 2419064832 | bytes 10620928 | tf_op jit(solution)/shard_map/dot_general | solution.py:42
  272.5 7.3 %add_add_fusion = f32[2048,384]{1,0:T(8,128)} fusion(f32[2048,384]{1,0:T(8,128)} %fusion.6, f32[2048,384]{1,0:T(8,128)} %fusion.18, f32[2048,384]{1,0:T(8,128)} %fusion.14, bf16[2048,3,1536]{2,0,1:T(8,128)(2,1)S(1)} %copy-done.10, bf16[2048]{0:T(1024)(128)(2,1)S(1)} %broadcast_bitcast_fusion, bf16[2,384,1536]{2,1,0:T(8,128)(2,1)S(1)} %copy-done.12), kind=kOutput, calls=%fused_computation.31 | convolution fusion | flops 2421424128 | bytes 20058112 | tf_op jit(solution)/shard_map/dot_general | solution.py:42
  280.9 6.9 %fusion.63 = bf16[1,384,1536]{1,2,0:T(8,128)(2,1)S(1)} fusion(bf16[2048,384]{1,0:T(8,128)(2,1)S(1)} %bitcast.139, bf16[2048,3,1536]{2,0,1:T(8,128)(2,1)} %all-gather.2.cloned.1.call-done, bf16[2048]{0:T(1024)(128)(2,1)S(1)} %broadcast_bitcast_fusion), kind=kOutput, calls=%fused_computation.51 | convolution fusion | flops 2419654656 | bytes 9048064 | tf_op jit(solution)/shard_map/dot_general | solution.py:36
  287.9 6.8 %fusion.69 = bf16[1,384,1536]{1,2,0:T(8,128)(2,1)S(1)} fusion(bf16[2048,384]{1,0:T(8,128)(2,1)S(1)} %bitcast.140, bf16[2048,3,1536]{2,0,1:T(8,128)(2,1)} %all-gather.2.cloned.1.call-done, bf16[2048]{0:T(1024)(128)(2,1)S(1)} %broadcast_bitcast_fusion.1), kind=kOutput, calls=%fused_computation.53 | convolution fusion | flops 2419654656 | bytes 9048064 | tf_op jit(solution)/shard_map/dot_general | solution.py:36
  296.1 3.7 fusion.60
  299.8 4.0 %fusion.66 = bf16[1,384,1536]{1,2,0:T(8,128)(2,1)S(1)} fusion(bf16[2048,384]{1,0:T(8,128)(2,1)S(1)} %bitcast.142, bf16[2048,3,1536]{2,0,1:T(8,128)(2,1)S(1)} %bitcast.145, bf16[2048]{0:T(1024)(128)(2,1)S(1)} %broadcast_bitcast_fusion.1), kind=kOutput, calls=%fused_computation.52 | convolution fusion | flops 2419654656 | bytes 9048064 | tf_op jit(solution)/shard_map/dot_general | solution.py:36
  305.9 3.7 fusion.54
  309.6 4.7 %fusion.57 = bf16[1,1536,384]{2,1,0:T(8,128)(2,1)} fusion(bf16[2048,384]{1,0:T(8,128)(2,1)S(1)} %bitcast.137, bf16[2048,3,1536]{2,0,1:T(8,128)(2,1)S(1)} %bitcast.145, bf16[2048]{0:T(1024)(128)(2,1)S(1)} %broadcast_bitcast_fusion.1), kind=kOutput, calls=%fused_computation.49 | convolution fusion | flops 2419654656 | bytes 9048064 | tf_op jit(solution)/shard_map/dot_general | solution.py:36
  314.3 43.4 %reduce-scatter.5.cloned.1.call-done = f32[1,256,384]{2,1,0:T(8,128)} async-done(((f32[8,256,384]{2,1,0:T(8,128)}), f32[1,256,384]{2,1,0:T(8,128)}) %reduce-scatter.5.cloned.1.call-update) | async-done | bytes 393232 | tf_op jit(solution)/shard_map/reduce_scatter | solution.py:118
  361.3 3.5 collective-permute-start.1
  370.3 4.3 %copy.30 = bf16[2,384,1536]{2,1,0:T(8,128)(2,1)} copy(bf16[2,384,1536]{1,2,0:T(8,128)(2,1)} %pad_maximum_fusion.1) | data formatting | bytes 4718592
  374.6 6.8 %collective-permute-done.1 = bf16[128,384]{1,0:T(8,128)(2,1)} collective-permute-done((bf16[128,384]{1,0:T(8,128)(2,1)}, bf16[128,384]{1,0:T(8,128)(2,1)}, u32[]{:S(2)}, u32[]{:S(2)}) %collective-permute-start.1) | collective-permute-done | bytes 98336 | tf_op jit(solution)/shard_map/ppermute | solution.py:125
  (73 shorter events, 30.3 us)
Async XLA Ops:
  9.7 6.3 %copy-start.9 = (s32[16]{0:T(128)S(1)}, s32[16]{0:T(128)}, u32[]{:S(2)}) copy-start(s32[16]{0:T(128)} %constant.50) | copy-start | bytes 196
  9.7 6.3 %copy-start = (s32[16]{0:T(128)S(1)}, s32[16]{0:T(128)}, u32[]{:S(2)}) copy-start(s32[16]{0:T(128)} %param.18) | copy-start | bytes 196
  9.7 27.6 %all-to-all-start = ((bf16[128,16,384]{0,2,1:T(8,128)(2,1)}), bf16[128,16,384]{0,2,1:T(8,128)(2,1)S(1)}, u32[]{:S(2)}, u32[]{:S(2)}) async-start(bf16[128,16,384]{0,2,1:T(8,128)(2,1)} %bitcast.2), calls=%async_computation | async-start | bytes 3145728 | tf_op jit(solution)/shard_map/all_to_all | solution.py:63
  16.0 60.9 %reduce-scatter.3.cloned.1.call-start = ((), (), s32[]{:S(2)}) async-start(), calls=%async_computation.5 | async-start | bytes 18874368 | tf_op jit(solution)/shard_map/reduce_scatter | solution.py:82
  39.6 1.7 copy-start.3
  81.7 49.5 %all-to-all-start.1 = ((bf16[8,128,1536]{2,1,0:T(8,128)(2,1)}), bf16[8,128,1536]{2,1,0:T(8,128)(2,1)S(1)}, u32[]{:S(2)}, u32[]{:S(2)}) async-start(bf16[8,128,1536]{2,1,0:T(8,128)(2,1)} %bitcast.130), calls=%async_computation.2 | async-start | bytes 6291456 | tf_op jit(solution)/shard_map/all_to_all | solution.py:85
  86.9 44.8 %copy-start.7 = (bf16[128,1536]{1,0:T(8,128)(2,1)S(1)}, bf16[128,1536]{1,0:T(8,128)(2,1)}, u32[]{:S(2)}) copy-start(bf16[128,1536]{1,0:T(8,128)(2,1)} %param.12) | copy-start | bytes 1179652
  86.9 164.9 %all-gather.2.cloned.1.call-start = ((), (), s32[]{:S(2)}) async-start(), calls=%async_computation.6 | async-start | bytes 20054016 | tf_op jit(solution)/shard_map/all_gather | solution.py:95
  132.8 1.8 copy-start.4
  136.2 143.6 %all-to-all-start.2 = ((bf16[128,16,384]{0,2,1:T(8,128)(2,1)}), bf16[128,16,384]{0,2,1:T(8,128)(2,1)S(1)}, u32[]{:S(2)}, u32[]{:S(2)}) async-start(bf16[128,16,384]{0,2,1:T(8,128)(2,1)} %bitcast.29), calls=%async_computation.4 | async-start | bytes 3145728 | tf_op jit(solution)/shard_map/all_to_all | solution.py:64
  141.7 215.9 %reduce-scatter.5.cloned.1.call-start = ((), (), s32[]{:S(2)}) async-start(), calls=%async_computation.7 | async-start | bytes 3538944 | tf_op jit(solution)/shard_map/reduce_scatter | solution.py:118
  251.8 9.7 %copy-start.10 = (bf16[2048,3,1536]{2,0,1:T(8,128)(2,1)S(1)}, bf16[2048,3,1536]{2,0,1:T(8,128)(2,1)}, u32[]{:S(2)}) copy-start(bf16[2048,3,1536]{2,0,1:T(8,128)(2,1)} %all-gather.2.cloned.1.call-done) | copy-start | bytes 56623108
  251.8 10.3 %copy-start.11 = (bf16[2,384,1536]{2,1,0:T(8,128)(2,1)S(1)}, bf16[2,384,1536]{2,1,0:T(8,128)(2,1)}, u32[]{:S(2)}) copy-start(bf16[2,384,1536]{2,1,0:T(8,128)(2,1)} %param.15) | copy-start | bytes 7077892
  262.1 5.2 %copy-start.12 = (bf16[2,384,1536]{2,1,0:T(8,128)(2,1)S(1)}, bf16[2,384,1536]{2,1,0:T(8,128)(2,1)}, u32[]{:S(2)}) copy-start(bf16[2,384,1536]{2,1,0:T(8,128)(2,1)} %param.14) | copy-start | bytes 7077892
  280.9 7.0 %copy-start.5 = (bf16[16,128,384]{2,1,0:T(8,128)(2,1)}, bf16[16,128,384]{2,1,0:T(8,128)(2,1)S(1)}, u32[]{:S(2)}) copy-start(bf16[16,128,384]{2,1,0:T(8,128)(2,1)S(1)} %copy.27) | copy-start | bytes 4718596
  280.9 14.1 %slice-start = ((s8[18874368]{0:T(1024)(128)(4,1)}), s8[4194304]{0:T(1024)(128)(4,1)S(1)}, s32[]{:S(2)}) async-start(s8[18874368]{0:T(1024)(128)(4,1)} %bitcast.144), calls=%async_computation.8 | async-start | bytes 8388608
  280.9 14.1 %slice-start.1 = ((s8[18874368]{0:T(1024)(128)(4,1)}), s8[4194304]{0:T(1024)(128)(4,1)S(1)}, s32[]{:S(2)}) async-start(s8[18874368]{0:T(1024)(128)(4,1)} %bitcast.144), calls=%async_computation.9 | async-start | bytes 8388608
  280.9 14.1 %slice-start.2 = ((s8[18874368]{0:T(1024)(128)(4,1)}), s8[4194304]{0:T(1024)(128)(4,1)S(1)}, s32[]{:S(2)}) async-start(s8[18874368]{0:T(1024)(128)(4,1)} %bitcast.144), calls=%async_computation.10 | async-start | bytes 8388608
  287.9 7.1 %slice-start.3 = ((s8[18874368]{0:T(1024)(128)(4,1)}), s8[4194304]{0:T(1024)(128)(4,1)S(1)}, s32[]{:S(2)}) async-start(s8[18874368]{0:T(1024)(128)(4,1)} %bitcast.144), calls=%async_computation.11 | async-start | bytes 8388608
  287.9 7.1 %slice-start.4 = ((s8[18874368]{0:T(1024)(128)(4,1)}), s8[2097152]{0:T(1024)(128)(4,1)S(1)}, s32[]{:S(2)}) async-start(s8[18874368]{0:T(1024)(128)(4,1)} %bitcast.144), calls=%async_computation.12 | async-start | bytes 4194304
  294.7 1.4 copy-start.6
  303.8 2.1 copy-start.2
  359.3 15.3 %collective-permute-start = (bf16[128,384]{1,0:T(8,128)(2,1)}, bf16[128,384]{1,0:T(8,128)(2,1)}, u32[]{:S(2)}, u32[]{:S(2)}) collective-permute-start(bf16[128,384]{1,0:T(8,128)(2,1)} %get-tuple-element.21), channel_id=1, source_target_pairs={{0,0},{1,16},{2,32},{3,48},{4,64},{5,80},{6,96},{7,112},{8,8},{9,2... | collective-permute-start | bytes 294920 | tf_op jit(solution)/shard_map/ppermute | solution.py:125
  361.3 20.1 %collective-permute-start.1 = (bf16[128,384]{1,0:T(8,128)(2,1)}, bf16[128,384]{1,0:T(8,128)(2,1)}, u32[]{:S(2)}, u32[]{:S(2)}) collective-permute-start(bf16[128,384]{1,0:T(8,128)(2,1)} %get-tuple-element.22), channel_id=1, source_target_pairs={{0,8},{1,24},{2,40},{3,56},{4,72},{5,88},{6,104},{7,120},{8,0},{9,... | collective-permute-start | bytes 294920 | tf_op jit(solution)/shard_map/ppermute | solution.py:125
  (2 other events, 2.1 us)
Sparse Core Ops, SparseCore 0:
  51.4 25.4 reduce-scatter.2
  134.1 117.5 all-gather.1
  279.9 77.6 reduce-scatter.4

commit v3 on v2

--- a/solution.py
+++ b/solution.py
@@ -27,7 +27,7 @@
     pairs = []
     for i in range(N_DP):
         for t in range(N_TP):
-            dest = 2 * t + ((i % 2) ^ k)
+            dest = 8 * ((i % 2) ^ k) + t
             pairs.append((i * N_TP + t, dest * N_TP + i // 2))
     return pairs
 
@@ -74,6 +74,7 @@
     sigmoid = jax.nn.sigmoid(gate_vals)
     silu_vals = gate_vals * sigmoid
     hidden = (silu_vals * up_vals * row_mask).astype(jnp.bfloat16)
+    hid_g = lax.all_gather(hidden, DP, axis=0, tiled=True)
 
     dy_g = to_gathered_order(dy_cols)
     result = jnp.zeros((row_count, ff), jnp.float32)
@@ -82,49 +83,58 @@
     result = lax.psum_scatter(
         result.reshape(2, row_count // 2, ff), "core", scatter_dimension=0, tiled=True
     ).reshape(N_DP // 2, rows_dev, ff)
-    pieces = lax.all_to_all(
-        result.astype(jnp.bfloat16), CHIPS, split_axis=0, concat_axis=0, tiled=True
-    )
-    hidden_grad = jnp.sum(pieces.astype(jnp.float32), axis=0)
+    pieces = lax.all_to_all(result, CHIPS, split_axis=0, concat_axis=0, tiled=True)
+    hidden_grad = jnp.sum(pieces, axis=0)
 
     up_grad = (hidden_grad * silu_vals * row_mask).astype(jnp.bfloat16)
     gate_grad = (
         hidden_grad * up_vals * sigmoid * (1.0 + gate_vals * (1.0 - sigmoid)) * row_mask
     ).astype(jnp.bfloat16)
-    packed = jnp.stack([hidden, gate_grad, up_grad], axis=1)
+    packed = jnp.stack([gate_grad, up_grad], axis=1)
     packed = lax.all_gather(packed, DP, axis=0, tiled=True)
-    hid_g, gate_g, up_g = packed[:, 0], packed[:, 1], packed[:, 2]
+    gate_g, up_g = packed[:, 0], packed[:, 1]
 
     down_terms = []
     gate_terms = []
     up_terms = []
-    partial_rows = jnp.zeros((row_count, w_gate.shape[1]), jnp.float32)
     for which in range(expert_count):
         down_terms.append(contract_rows(hid_g * masks[which], dy_cols))
         gate_masked = gate_g * masks[which]
         up_masked = up_g * masks[which]
         gate_terms.append(contract_rows(x_cols, gate_masked))
         up_terms.append(contract_rows(x_cols, up_masked))
-        partial_rows = (
-            partial_rows
-            + contract_cols(gate_masked, w_gate[which])
-            + contract_cols(up_masked, w_up[which])
-        )
     down_total = jnp.stack(down_terms, 0)
     gate_total = jnp.stack(gate_terms, 0)
     up_total = jnp.stack(up_terms, 0)
 
-    width = partial_rows.shape[1]
-    summed = lax.psum_scatter(
-        partial_rows.reshape(N_TP, row_count // N_TP, width), TP, scatter_dimension=0, tiled=True
-    ).reshape(2, rows_dev, width)
+    width = w_gate.shape[1]
+    half_rows = row_count // 2
+    summed = []
+    for half in range(2):
+        rows = slice(half * half_rows, (half + 1) * half_rows)
+        partial_rows = jnp.zeros((half_rows, width), jnp.float32)
+        for which in range(expert_count):
+            gate_masked = gate_g[rows] * masks[which][rows]
+            up_masked = up_g[rows] * masks[which][rows]
+            partial_rows = (
+                partial_rows
+                + contract_cols(gate_masked, w_gate[which])
+                + contract_cols(up_masked, w_up[which])
+            )
+        summed.append(
+            lax.psum_scatter(
+                partial_rows.reshape(N_TP, rows_dev, width), TP, scatter_dimension=0, tiled=True
+            ).reshape(rows_dev, width)
+        )
+    summed = jnp.stack(summed, 0)
     core = lax.axis_index("core")
+    low = lax.axis_index("x") < 2
     got = []
     for k in range(2):
         piece = lax.dynamic_index_in_dim(summed, core ^ k, 0, keepdims=False)
         got.append(lax.ppermute(piece, AXES, deliver_perm(k)))
-    first = jnp.where(core == 0, got[0], got[1])
-    second = jnp.where(core == 0, got[1], got[0])
+    first = jnp.where(low, got[0], got[1])
+    second = jnp.where(low, got[1], got[0])
     input_grad = jnp.concatenate([first, second], axis=1).astype(jnp.bfloat16)
     return (
         input_grad,

time: 397 us -> 509 us (1.28)
  the two profiles are of different devices: /device:TPU:9 before, /device:TPU:3 now
where the time goes in v3:
time: 509 us; the launch traced here: 500 us
  waiting for transfers between devices  353 us (69%)
  matrix products  66.4 us (13%)
  local copies, waits for them, and re-layouts  26.1 us (5%)
  starting transfers between devices  25.2 us (5%)
  between operations  15.2 us (3%)
  other arithmetic  13.8 us (3%)
    reduce_scatter x2, waiting for transfers between devices, shards(): lax.psum_scatter(partial_rows.reshape(N_TP, rows_dev, width), TP, scatter...  104 us
    all_to_all x1, waiting for transfers between devices, shards(): lax.all_to_all(result, CHIPS, split_axis=0, concat_axis=0, tiled=True)  84.2 us
    all_gather x1, waiting for transfers between devices, shards(): packed = lax.all_gather(packed, DP, axis=0, tiled=True)  68.7 us
    dot_general x6, matrix products, contract_rows(): lax.dot_general(left_op, right_op, (((0,), (0,)), ((), ())), preferred_el...  34.7 us
    all_to_all x1, waiting for transfers between devices, shards(): lax.all_to_all(rows_in, DP, split_axis=1, concat_axis=0, tiled=True)  33.2 us
    dot_general x10, matrix products, contract_cols(): lax.dot_general(left_op, right_op, (((1,), (1,)), ((), ())), preferred_el...  31.6 us
    reduce_scatter x1, waiting for transfers between devices, shards(): lax.psum_scatter(result.reshape(2, row_count // 2, ff), 'core', scatter_d...  27.3 us
    all_to_all x1, waiting for transfers between devices, shards(): lax.all_to_all(out_grad, DP, split_axis=1, concat_axis=0, tiled=True)  18.5 us
  transfers between devices with their start and end apart: 10, of which 9 were waited for; matrix products, arithmetic and copies ran while one was open for 13% of the time, Pallas kernels for 0%

profile of v3, /device:TPU:3, one launch (start us, length us, event | category | flops | bytes accessed | tf_op | source)
XLA Modules:
  0.0 499.8 jit_solution(13159368352002467831)
XLA Ops:
  9.7 6.3 %all-to-all-start = ((bf16[128,16,384]{0,2,1:T(8,128)(2,1)}), bf16[128,16,384]{0,2,1:T(8,128)(2,1)S(1)}, u32[]{:S(2)}, u32[]{:S(2)}) async-start(bf16[128,16,384]{0,2,1:T(8,128)(2,1)} %bitcast), calls=%async_computation | async-start | bytes 3145728 | tf_op jit(solution)/shard_map/all_to_all | solution.py:63
  17.2 18.5 %all-to-all-done = bf16[128,16,384]{0,2,1:T(8,128)(2,1)S(1)} async-done(((bf16[128,16,384]{0,2,1:T(8,128)(2,1)}), bf16[128,16,384]{0,2,1:T(8,128)(2,1)S(1)}, u32[]{:S(2)}, u32[]{:S(2)}) %all-to-all-start) | async-done | bytes 1572896 | tf_op jit(solution)/shard_map/all_to_all | solution.py:63
  38.9 3.5 fusion.115
  42.3 6.6 %convolution_add_fusion = f32[2048,1536]{1,0:T(8,128)} fusion(f32[2048,1536]{1,0:T(8,128)S(1)} %fusion.115, bf16[2048,384]{1,0:T(8,128)(2,1)S(1)} %bitcast.148, bf16[2,1536,384]{2,1,0:T(8,128)(2,1)S(1)} %copy-done.1), kind=kOutput, calls=%fused_computation.1 | convolution fusion | flops 2419064832 | bytes 27918336 | tf_op jit(solution)/shard_map/dot_general | solution.py:42
  48.9 27.3 %reduce-scatter.4.cloned.1.call-done = f32[1,1024,1536]{2,1,0:T(8,128)} async-done(((f32[2,1024,1536]{2,1,0:T(8,128)}), f32[1,1024,1536]{2,1,0:T(8,128)}) %reduce-scatter.4.cloned.1.call-update) | async-done | bytes 6291472 | tf_op jit(solution)/shard_map/reduce_scatter | solution.py:83
  76.2 5.2 %all-to-all-start.1 = ((f32[8,128,1536]{2,1,0:T(8,128)}), f32[8,128,1536]{2,1,0:T(8,128)}, u32[]{:S(2)}, u32[]{:S(2)}) async-start(f32[8,128,1536]{2,1,0:T(8,128)} %bitcast.150), calls=%async_computation.2 | async-start | bytes 12582912 | tf_op jit(solution)/shard_map/all_to_all | solution.py:86
  82.1 84.2 %all-to-all-done.1 = f32[8,128,1536]{2,1,0:T(8,128)} async-done(((f32[8,128,1536]{2,1,0:T(8,128)}), f32[8,128,1536]{2,1,0:T(8,128)}, u32[]{:S(2)}, u32[]{:S(2)}) %all-to-all-start.1) | async-done | bytes 6291488 | tf_op jit(solution)/shard_map/all_to_all | solution.py:86
  166.3 3.4 reduce_sum.9
  174.8 7.5 %all-to-all-start.2 = ((bf16[128,16,384]{0,2,1:T(8,128)(2,1)}), bf16[128,16,384]{0,2,1:T(8,128)(2,1)S(1)}, u32[]{:S(2)}, u32[]{:S(2)}) async-start(bf16[128,16,384]{0,2,1:T(8,128)(2,1)} %bitcast.36), calls=%async_computation.5 | async-start | bytes 3145728 | tf_op jit(solution)/shard_map/all_to_all | solution.py:64
  183.1 33.2 %all-to-all-done.2 = bf16[128,16,384]{0,2,1:T(8,128)(2,1)S(1)} async-done(((bf16[128,16,384]{0,2,1:T(8,128)(2,1)}), bf16[128,16,384]{0,2,1:T(8,128)(2,1)S(1)}, u32[]{:S(2)}, u32[]{:S(2)}) %all-to-all-start.2) | async-done | bytes 1572896 | tf_op jit(solution)/shard_map/all_to_all | solution.py:64
  217.9 15.7 %all-gather.5.cloned.1.call-done = bf16[2048,1536]{1,0:T(8,128)(2,1)} async-done(((bf16[128,1536]{1,0:T(8,128)(2,1)}), bf16[2048,1536]{1,0:T(8,128)(2,1)}) %all-gather.5.cloned.1.call-update) | async-done | bytes 6291472 | tf_op jit(solution)/shard_map/all_gather | solution.py:77
  233.6 6.4 %fusion.88 = bf16[1,1536,384]{2,1,0:T(8,128)(2,1)S(1)} fusion(bf16[2048,384]{1,0:T(8,128)(2,1)S(1)} %bitcast.154, bf16[2048,1536]{1,0:T(8,128)(2,1)} %all-gather.5.cloned.1.call-done, bf16[2048]{0:T(1024)(128)(2,1)S(1)} %broadcast_bitcast_fusion), kind=kOutput, calls=%fused_computation.70 | convolution fusion | flops 2419654656 | bytes 9048064 | tf_op jit(solution)/shard_map/dot_general | solution.py:36
  240.0 68.7 %all-gather.3.cloned.1.call-done = bf16[2048,2,1536]{2,0,1:T(8,128)(2,1)} async-done(((bf16[128,2,1536]{2,0,1:T(8,128)(2,1)}), bf16[2048,2,1536]{2,0,1:T(8,128)(2,1)}) %all-gather.3.cloned.1.call-update) | async-done | bytes 12582928 | tf_op jit(solution)/shard_map/all_gather | solution.py:94
  308.7 4.2 fusion.32
  322.2 6.5 %fusion.91 = bf16[1,1536,384]{2,1,0:T(8,128)(2,1)S(1)} fusion(bf16[2048,384]{1,0:T(8,128)(2,1)S(1)} %bitcast.155, bf16[2048,1536]{1,0:T(8,128)(2,1)} %all-gather.5.cloned.1.call-done, bf16[2048]{0:T(1024)(128)(2,1)S(1)} %broadcast_bitcast_fusion.1), kind=kOutput, calls=%fused_computation.71 | convolution fusion | flops 2419654656 | bytes 9048064 | tf_op jit(solution)/shard_map/dot_general | solution.py:36
  331.3 4.0 fusion.24
  342.2 6.6 %fusion.76 = bf16[1,384,1536]{1,2,0:T(8,128)(2,1)S(1)} fusion(bf16[2048,384]{1,0:T(8,128)(2,1)S(1)} %bitcast.156, bf16[2048,2,1536]{2,0,1:T(8,128)(2,1)} %all-gather.3.cloned.1.call-done, bf16[2048]{0:T(1024)(128)(2,1)S(1)} %broadcast_bitcast_fusion), kind=kOutput, calls=%fused_computation.66 | convolution fusion | flops 2419654656 | bytes 9048064 | tf_op jit(solution)/shard_map/dot_general | solution.py:36
  348.8 6.8 %fusion.79 = bf16[1,384,1536]{1,2,0:T(8,128)(2,1)S(1)} fusion(bf16[2048,384]{1,0:T(8,128)(2,1)S(1)} %bitcast.157, bf16[2048,2,1536]{2,0,1:T(8,128)(2,1)} %all-gather.3.cloned.1.call-done, bf16[2048]{0:T(1024)(128)(2,1)S(1)} %broadcast_bitcast_fusion.1), kind=kOutput, calls=%fused_computation.67 | convolution fusion | flops 2419654656 | bytes 9048064 | tf_op jit(solution)/shard_map/dot_general | solution.py:36
  357.0 3.7 fusion.82
  360.7 4.7 fusion.85
  365.4 29.3 %reduce-scatter.6.cloned.1.call-done = f32[1,128,384]{2,1,0:T(8,128)} async-done(((f32[8,128,384]{2,1,0:T(8,128)}), f32[1,128,384]{2,1,0:T(8,128)}) %reduce-scatter.6.cloned.1.call-update) | async-done | bytes 196624 | tf_op jit(solution)/shard_map/reduce_scatter | solution.py:125
  396.3 75.0 %reduce-scatter.8.cloned.1.call-done = f32[1,128,384]{2,1,0:T(8,128)} async-done(((f32[8,128,384]{2,1,0:T(8,128)}), f32[1,128,384]{2,1,0:T(8,128)}) %reduce-scatter.8.cloned.1.call-update) | async-done | bytes 196624 | tf_op jit(solution)/shard_map/reduce_scatter | solution.py:125
  474.5 5.5 %collective-permute-start = (bf16[128,384]{1,0:T(8,128)(2,1)}, bf16[128,384]{1,0:T(8,128)(2,1)}, u32[]{:S(2)}, u32[]{:S(2)}) collective-permute-start(bf16[128,384]{1,0:T(8,128)(2,1)} %get-tuple-element.23), channel_id=1, source_target_pairs={{0,0},{1,8},{2,16},{3,24},{4,32},{5,40},{6,48},{7,56},{8,64},{9,72... | collective-permute-start | bytes 294920 | tf_op jit(solution)/shard_map/ppermute | solution.py:135
  485.7 4.3 copy.29
  (93 shorter events, 47.5 us)
Async XLA Ops:
  9.7 6.4 %copy-start.7 = (s32[16]{0:T(128)S(1)}, s32[16]{0:T(128)}, u32[]{:S(2)}) copy-start(s32[16]{0:T(128)} %constant.55) | copy-start | bytes 196
  9.7 6.4 %copy-start = (s32[16]{0:T(128)S(1)}, s32[16]{0:T(128)}, u32[]{:S(2)}) copy-start(s32[16]{0:T(128)} %param.18) | copy-start | bytes 196
  9.7 26.0 %all-to-all-start = ((bf16[128,16,384]{0,2,1:T(8,128)(2,1)}), bf16[128,16,384]{0,2,1:T(8,128)(2,1)S(1)}, u32[]{:S(2)}, u32[]{:S(2)}) async-start(bf16[128,16,384]{0,2,1:T(8,128)(2,1)} %bitcast), calls=%async_computation | async-start | bytes 3145728 | tf_op jit(solution)/shard_map/all_to_all | solution.py:63
  16.1 60.2 %reduce-scatter.4.cloned.1.call-start = ((), (), s32[]{:S(2)}) async-start(), calls=%async_computation.6 | async-start | bytes 18874368 | tf_op jit(solution)/shard_map/reduce_scatter | solution.py:83
  76.2 90.1 %all-to-all-start.1 = ((f32[8,128,1536]{2,1,0:T(8,128)}), f32[8,128,1536]{2,1,0:T(8,128)}, u32[]{:S(2)}, u32[]{:S(2)}) async-start(f32[8,128,1536]{2,1,0:T(8,128)} %bitcast.150), calls=%async_computation.2 | async-start | bytes 12582912 | tf_op jit(solution)/shard_map/all_to_all | solution.py:86
  81.4 152.2 %all-gather.5.cloned.1.call-start = ((), (), s32[]{:S(2)}) async-start(), calls=%async_computation.10 | async-start | bytes 6684672 | tf_op jit(solution)/shard_map/all_gather | solution.py:77
  82.1 87.6 %copy-start.5 = (bf16[128,1536]{1,0:T(8,128)(2,1)S(1)}, bf16[128,1536]{1,0:T(8,128)(2,1)}, u32[]{:S(2)}) copy-start(bf16[128,1536]{1,0:T(8,128)(2,1)} %param.12) | copy-start | bytes 1179652
  82.1 87.6 %copy-start.6 = (bf16[128,1536]{1,0:T(8,128)(2,1)S(1)}, bf16[128,1536]{1,0:T(8,128)(2,1)}, u32[]{:S(2)}) copy-start(bf16[128,1536]{1,0:T(8,128)(2,1)} %param.13) | copy-start | bytes 1179652
  171.1 137.6 %all-gather.3.cloned.1.call-start = ((), (), s32[]{:S(2)}) async-start(), calls=%async_computation.7 | async-start | bytes 13369344 | tf_op jit(solution)/shard_map/all_gather | solution.py:94
  174.8 41.5 %all-to-all-start.2 = ((bf16[128,16,384]{0,2,1:T(8,128)(2,1)}), bf16[128,16,384]{0,2,1:T(8,128)(2,1)S(1)}, u32[]{:S(2)}, u32[]{:S(2)}) async-start(bf16[128,16,384]{0,2,1:T(8,128)(2,1)} %bitcast.36), calls=%async_computation.5 | async-start | bytes 3145728 | tf_op jit(solution)/shard_map/all_to_all | solution.py:64
  182.3 212.4 %reduce-scatter.6.cloned.1.call-start = ((), (), s32[]{:S(2)}) async-start(), calls=%async_computation.8 | async-start | bytes 1769472 | tf_op jit(solution)/shard_map/reduce_scatter | solution.py:125
  308.7 5.9 %copy-start.8 = (bf16[2048,2,1536]{2,0,1:T(8,128)(2,1)S(1)}, bf16[2048,2,1536]{2,0,1:T(8,128)(2,1)}, u32[]{:S(2)}) copy-start(bf16[2048,2,1536]{2,0,1:T(8,128)(2,1)} %all-gather.3.cloned.1.call-done) | copy-start | bytes 37748740
  308.7 6.5 %copy-start.11 = (bf16[2,384,1536]{2,1,0:T(8,128)(2,1)S(1)}, bf16[2,384,1536]{2,1,0:T(8,128)(2,1)}, u32[]{:S(2)}) copy-start(bf16[2,384,1536]{2,1,0:T(8,128)(2,1)} %param.14) | copy-start | bytes 7077892
  321.9 149.4 %reduce-scatter.8.cloned.1.call-start = ((), (), s32[]{:S(2)}) async-start(), calls=%async_computation.9 | async-start | bytes 1769472 | tf_op jit(solution)/shard_map/reduce_scatter | solution.py:125
  322.2 13.1 %slice-start = ((s8[12582912]{0:T(1024)(128)(4,1)}), s8[4194304]{0:T(1024)(128)(4,1)S(1)}, s32[]{:S(2)}) async-start(s8[12582912]{0:T(1024)(128)(4,1)} %bitcast.162), calls=%async_computation.11 | async-start | bytes 8388608
  322.2 13.1 %slice-start.1 = ((s8[12582912]{0:T(1024)(128)(4,1)}), s8[4194304]{0:T(1024)(128)(4,1)S(1)}, s32[]{:S(2)}) async-start(s8[12582912]{0:T(1024)(128)(4,1)} %bitcast.162), calls=%async_computation.12 | async-start | bytes 8388608
  331.3 4.0 slice-start.2
  331.3 4.0 copy-start.12
  339.0 3.2 copy-start.3
  342.2 13.8 %slice-start.3 = ((s8[12582912]{0:T(1024)(128)(4,1)}), s8[4194304]{0:T(1024)(128)(4,1)S(1)}, s32[]{:S(2)}) async-start(s8[12582912]{0:T(1024)(128)(4,1)} %bitcast.164), calls=%async_computation.14 | async-start | bytes 8388608
  342.2 13.8 %slice-start.4 = ((s8[12582912]{0:T(1024)(128)(4,1)}), s8[4194304]{0:T(1024)(128)(4,1)S(1)}, s32[]{:S(2)}) async-start(s8[12582912]{0:T(1024)(128)(4,1)} %bitcast.164), calls=%async_computation.15 | async-start | bytes 8388608
  348.8 7.1 %slice-start.5 = ((s8[12582912]{0:T(1024)(128)(4,1)}), s8[4194304]{0:T(1024)(128)(4,1)S(1)}, s32[]{:S(2)}) async-start(s8[12582912]{0:T(1024)(128)(4,1)} %bitcast.164), calls=%async_computation.16 | async-start | bytes 8388608
  474.5 15.4 %collective-permute-start = (bf16[128,384]{1,0:T(8,128)(2,1)}, bf16[128,384]{1,0:T(8,128)(2,1)}, u32[]{:S(2)}, u32[]{:S(2)}) collective-permute-start(bf16[128,384]{1,0:T(8,128)(2,1)} %get-tuple-element.23), channel_id=1, source_target_pairs={{0,0},{1,8},{2,16},{3,24},{4,32},{5,40},{6,48},{7,56},{8,64},{9,72... | collective-permute-start | bytes 294920 | tf_op jit(solution)/shard_map/ppermute | solution.py:135
  480.1 11.1 %collective-permute-start.1 = (bf16[128,384]{1,0:T(8,128)(2,1)}, bf16[128,384]{1,0:T(8,128)(2,1)}, u32[]{:S(2)}, u32[]{:S(2)}) collective-permute-start(bf16[128,384]{1,0:T(8,128)(2,1)} %get-tuple-element.24), channel_id=1, source_target_pairs={{0,64},{1,72},{2,80},{3,88},{4,96},{5,104},{6,112},{7,120},{8,0},{... | collective-permute-start | bytes 294920 | tf_op jit(solution)/shard_map/ppermute | solution.py:135
  (5 other events, 9.6 us)
Sparse Core Ops, SparseCore 0:
  49.0 27.1 reduce-scatter.3
  171.2 62.3 all-gather.4
  235.9 72.7 all-gather.2
  322.1 72.6 reduce-scatter.5
  399.3 72.0 reduce-scatter.7

commit v4 on v3

--- a/solution.py
+++ b/solution.py
@@ -62,6 +62,7 @@
     ff = gate_pre.shape[1]
     dy_cols = lax.all_to_all(out_grad, DP, split_axis=1, concat_axis=0, tiled=True)
     x_cols = lax.all_to_all(rows_in, DP, split_axis=1, concat_axis=0, tiled=True)
+    x_cols, dy_cols = lax.optimization_barrier((x_cols, dy_cols))
     row_count = dy_cols.shape[0]
     expert_g = jnp.take(block_expert, jnp.asarray(POS_RANK), axis=0)
     masks_g = expert_masks(expert_g, row_count, expert_count)
@@ -74,7 +75,6 @@
     sigmoid = jax.nn.sigmoid(gate_vals)
     silu_vals = gate_vals * sigmoid
     hidden = (silu_vals * up_vals * row_mask).astype(jnp.bfloat16)
-    hid_g = lax.all_gather(hidden, DP, axis=0, tiled=True)
 
     dy_g = to_gathered_order(dy_cols)
     result = jnp.zeros((row_count, ff), jnp.float32)
@@ -83,6 +83,8 @@
     result = lax.psum_scatter(
         result.reshape(2, row_count // 2, ff), "core", scatter_dimension=0, tiled=True
     ).reshape(N_DP // 2, rows_dev, ff)
+    hidden, result = lax.optimization_barrier((hidden, result))
+    hid_g = lax.all_gather(hidden, DP, axis=0, tiled=True)
     pieces = lax.all_to_all(result, CHIPS, split_axis=0, concat_axis=0, tiled=True)
     hidden_grad = jnp.sum(pieces, axis=0)
 
@@ -121,11 +123,10 @@
                 + contract_cols(gate_masked, w_gate[which])
                 + contract_cols(up_masked, w_up[which])
             )
-        summed.append(
-            lax.psum_scatter(
-                partial_rows.reshape(N_TP, rows_dev, width), TP, scatter_dimension=0, tiled=True
-            ).reshape(rows_dev, width)
+        pieces = lax.all_to_all(
+            partial_rows.reshape(N_TP, rows_dev, width), TP, split_axis=0, concat_axis=0, tiled=True
         )
+        summed.append(jnp.sum(pieces, axis=0))
     summed = jnp.stack(summed, 0)
     core = lax.axis_index("core")
     low = lax.axis_index("x") < 2

time: 509 us -> 379 us (0.74); the launches traced: 500 us -> 378 us
  waiting for transfers between devices: 353 us -> 142 us
  blocking collectives: 0 us -> 102 us
  local copies, waits for them, and re-layouts: 26.1 us -> 13 us
  starting transfers between devices: 25.2 us -> 30.7 us
    reduce_scatter x2 -> x0, waiting for transfers between devices: 104 us -> none  [shards(): lax.psum_scatter(partial_rows.reshape(N_TP, rows_dev, width), TP, scatter...]
    all_to_all x0 -> x1, blocking collectives: none -> 102 us  [shards(): lax.all_to_all(result, CHIPS, split_axis=0, concat_axis=0, tiled=True)]
    all_to_all x1 -> x2, waiting for transfers between devices: 84.2 us -> 9.26 us  [shards(): lax.all_to_all(partial_rows.reshape(N_TP, rows_dev, width), TP, split_axi...]
    all_gather x1, waiting for transfers between devices: 15.7 us -> 0.01 us  [shards(): hid_g = lax.all_gather(hidden, DP, axis=0, tiled=True)]
    all_to_all x1, waiting for transfers between devices: 33.2 us -> 18.1 us  [shards(): lax.all_to_all(rows_in, DP, split_axis=1, concat_axis=0, tiled=True)]
    unnamed x43 -> x38, local copies, waits for them, and re-layouts: 18.4 us -> 9.13 us
    all_to_all x1 -> x2, starting transfers between devices: 5.19 us -> 12 us  [shards(): lax.all_to_all(partial_rows.reshape(N_TP, rows_dev, width), TP, split_axi...]
    ppermute x2, waiting for transfers between devices: 1.2 us -> 7.88 us  [shards(): got.append(lax.ppermute(piece, AXES, deliver_perm(k)))]
  transfers between devices with their start and end apart: 10 -> 9, of which waited for: 9 -> 8; matrix products, arithmetic and copies ran while one was open for 13% -> 16% of each run, Pallas kernels for 0% -> 0%
where the time goes in v4:
time: 379 us; the launch traced here: 378 us
  waiting for transfers between devices  142 us (37%)
  blocking collectives  102 us (27%)
  matrix products  63.3 us (17%)
  starting transfers between devices  30.7 us (8%)
  between operations  14.7 us (4%)
  other arithmetic  13.4 us (4%)
  local copies, waits for them, and re-layouts  13 us (3%)
    all_to_all x1, blocking collectives, shards(): lax.all_to_all(result, CHIPS, split_axis=0, concat_axis=0, tiled=True)  102 us
    all_gather x1, waiting for transfers between devices, shards(): packed = lax.all_gather(packed, DP, axis=0, tiled=True)  64 us
    dot_general x10, matrix products, contract_cols(): lax.dot_general(left_op, right_op, (((1,), (1,)), ((), ())), preferred_el...  34 us
    dot_general x6, matrix products, contract_rows(): lax.dot_general(left_op, right_op, (((0,), (0,)), ((), ())), preferred_el...  29.2 us
    reduce_scatter x1, waiting for transfers between devices, shards(): lax.psum_scatter(result.reshape(2, row_count // 2, ff), 'core', scatter_d...  25.2 us
    all_to_all x1, waiting for transfers between devices, shards(): lax.all_to_all(rows_in, DP, split_axis=1, concat_axis=0, tiled=True)  18.1 us
    all_to_all x1, waiting for transfers between devices, shards(): lax.all_to_all(out_grad, DP, split_axis=1, concat_axis=0, tiled=True)  17.2 us
    all_to_all x2, starting transfers between devices, shards(): lax.all_to_all(partial_rows.reshape(N_TP, rows_dev, width), TP, split_axi...  12 us
  transfers between devices with their start and end apart: 9, of which 8 were waited for; matrix products, arithmetic and copies ran while one was open for 16% of the time, Pallas kernels for 0%

profile of v4, /device:TPU:3, one launch (start us, length us, event | category | flops | bytes accessed | tf_op | source)
XLA Modules:
  0.0 378.4 jit_solution(12524587742832676110)
XLA Ops:
  9.7 6.3 %all-to-all-start = ((bf16[128,16,384]{0,2,1:T(8,128)(2,1)}), bf16[128,16,384]{0,2,1:T(8,128)(2,1)S(1)}, u32[]{:S(2)}, u32[]{:S(2)}) async-start(bf16[128,16,384]{0,2,1:T(8,128)(2,1)} %bitcast.1), calls=%async_computation | async-start | bytes 3145728 | tf_op jit(solution)/shard_map/all_to_all | solution.py:64
  17.6 18.1 %all-to-all-done = bf16[128,16,384]{0,2,1:T(8,128)(2,1)S(1)} async-done(((bf16[128,16,384]{0,2,1:T(8,128)(2,1)}), bf16[128,16,384]{0,2,1:T(8,128)(2,1)S(1)}, u32[]{:S(2)}, u32[]{:S(2)}) %all-to-all-start) | async-done | bytes 1572896 | tf_op jit(solution)/shard_map/all_to_all | solution.py:64
  35.8 6.4 %all-to-all-start.1 = ((bf16[128,16,384]{0,2,1:T(8,128)(2,1)}), bf16[128,16,384]{0,2,1:T(8,128)(2,1)S(1)}, u32[]{:S(2)}, u32[]{:S(2)}) async-start(bf16[128,16,384]{0,2,1:T(8,128)(2,1)} %bitcast.4), calls=%async_computation.1 | async-start | bytes 3145728 | tf_op jit(solution)/shard_map/all_to_all | solution.py:63
  44.7 17.2 %all-to-all-done.1 = bf16[128,16,384]{0,2,1:T(8,128)(2,1)S(1)} async-done(((bf16[128,16,384]{0,2,1:T(8,128)(2,1)}), bf16[128,16,384]{0,2,1:T(8,128)(2,1)S(1)}, u32[]{:S(2)}, u32[]{:S(2)}) %all-to-all-start.1) | async-done | bytes 1572896 | tf_op jit(solution)/shard_map/all_to_all | solution.py:63
  64.5 3.5 fusion.107
  67.9 6.5 %convolution_add_fusion = f32[2048,1536]{1,0:T(8,128)} fusion(f32[2048,1536]{1,0:T(8,128)S(1)} %fusion.107, bf16[2048,384]{1,0:T(8,128)(2,1)S(1)} %bitcast.147, bf16[2,1536,384]{2,1,0:T(8,128)(2,1)S(1)} %copy-done.1), kind=kOutput, calls=%fused_computation.1 | convolution fusion | flops 2419064832 | bytes 27918336 | tf_op jit(solution)/shard_map/dot_general | solution.py:42
  76.5 25.2 %reduce-scatter.2.cloned.1.call-done = f32[1,1024,1536]{2,1,0:T(8,128)} async-done(((f32[2,1024,1536]{2,1,0:T(8,128)}), f32[1,1024,1536]{2,1,0:T(8,128)}) %reduce-scatter.2.cloned.1.call-update) | async-done | bytes 6291472 | tf_op jit(solution)/shard_map/reduce_scatter | solution.py:83
  101.8 101.6 %all_to_all.53 = f32[8,128,1536]{2,1,0:T(8,128)} all-to-all(f32[8,128,1536]{2,1,0:T(8,128)} %bitcast.149), channel_id=1, replica_groups=mesh['x'=4,'ylo'=2,'core'=2,'z'=4,'yhi'=2] {'x','ylo'}, dimensions={0} | all-to-all | bytes 12582912 | tf_op jit(solution)/shard_map/all_to_all | solution.py:88
  203.3 3.4 reduce_sum.27
  208.8 6.5 %fusion.68 = bf16[1,1536,384]{2,1,0:T(8,128)(2,1)S(1)} fusion(bf16[2048,384]{1,0:T(8,128)(2,1)S(1)} %bitcast.153, bf16[2048,1536]{1,0:T(8,128)(2,1)} %all-gather.5.cloned.1.call-done, bf16[2048]{0:T(1024)(128)(2,1)S(1)} %broadcast_bitcast_fusion), kind=kOutput, calls=%fused_computation.60 | convolution fusion | flops 2419654656 | bytes 9048064 | tf_op jit(solution)/shard_map/dot_general | solution.py:36
  215.3 3.7 fusion.71
  220.7 64.0 %all-gather.3.cloned.1.call-done = bf16[2048,2,1536]{2,0,1:T(8,128)(2,1)} async-done(((bf16[128,2,1536]{2,0,1:T(8,128)(2,1)}), bf16[2048,2,1536]{2,0,1:T(8,128)(2,1)}) %all-gather.3.cloned.1.call-update) | async-done | bytes 12582928 | tf_op jit(solution)/shard_map/all_gather | solution.py:96
  284.7 4.2 %fusion.12 = f32[1024,384]{1,0:T(8,128)S(1)} fusion(bf16[2048,2,1536]{2,0,1:T(8,128)(2,1)} %all-gather.3.cloned.1.call-done, bf16[1024]{0:T(1024)(128)(2,1)S(1)} %broadcast_bitcast_fusion.2, bf16[2,384,1536]{2,1,0:T(8,128)(2,1)} %param.15), kind=kOutput, calls=%fused_computation.16 | convolution fusion | flops 1209532416 | bytes 5900288 | tf_op jit(solution)/shard_map/dot_general | solution.py:42
  294.9 3.3 add_add_fusion
  298.2 6.6 %all-to-all-start.4 = ((f32[8,128,384]{2,1,0:T(8,128)}), f32[8,128,384]{2,1,0:T(8,128)S(1)}, u32[]{:S(2)}, u32[]{:S(2)}) async-start(f32[8,128,384]{2,1,0:T(8,128)} %bitcast.35), calls=%async_computation.5 | async-start | bytes 3145728 | tf_op jit(solution)/shard_map/all_to_all | solution.py:126
  304.8 4.2 %fusion.24 = f32[1024,384]{1,0:T(8,128)S(1)} fusion(bf16[2048,2,1536]{2,0,1:T(8,128)(2,1)} %all-gather.3.cloned.1.call-done, bf16[1024]{0:T(1024)(128)(2,1)S(1)} %broadcast_bitcast_fusion.5, bf16[2,384,1536]{2,1,0:T(8,128)(2,1)} %param.15), kind=kOutput, calls=%fused_computation.28 | convolution fusion | flops 1209532416 | bytes 5900288 | tf_op jit(solution)/shard_map/dot_general | solution.py:42
  309.0 3.9 %fusion.26 = f32[1024,384]{1,0:T(8,128)S(1)} fusion(bf16[2048,2,1536]{2,0,1:T(8,128)(2,1)} %all-gather.3.cloned.1.call-done, bf16[1024]{0:T(1024)(128)(2,1)S(1)} %broadcast_bitcast_fusion.5, bf16[2,384,1536]{2,1,0:T(8,128)(2,1)S(1)} %copy-done.14), kind=kOutput, calls=%fused_computation.30 | convolution fusion | flops 1209532416 | bytes 5900288 | tf_op jit(solution)/shard_map/dot_general | solution.py:42
  322.8 3.1 add_add_fusion.1
  327.2 5.4 %all-to-all-start.3 = ((f32[8,128,384]{2,1,0:T(8,128)}), f32[8,128,384]{2,1,0:T(8,128)S(1)}, u32[]{:S(2)}, u32[]{:S(2)}) async-start(f32[8,128,384]{2,1,0:T(8,128)} %bitcast.159), calls=%async_computation.4 | async-start | bytes 3145728 | tf_op jit(solution)/shard_map/all_to_all | solution.py:126
  332.6 7.1 %fusion.80 = bf16[1,384,1536]{2,1,0:T(8,128)(2,1)} fusion(bf16[2048,384]{1,0:T(8,128)(2,1)} %bitcast.155, bf16[2048,2,1536]{2,0,1:T(8,128)(2,1)} %all-gather.3.cloned.1.call-done, bf16[2048]{0:T(1024)(128)(2,1)S(1)} %broadcast_bitcast_fusion), kind=kOutput, calls=%fused_computation.64 | convolution fusion | flops 2419654656 | bytes 9048064 | tf_op jit(solution)/shard_map/dot_general | solution.py:36
  339.7 6.5 %fusion.83 = bf16[1,384,1536]{2,1,0:T(8,128)(2,1)} fusion(bf16[2048,384]{1,0:T(8,128)(2,1)S(1)} %bitcast.158, bf16[2048,2,1536]{2,0,1:T(8,128)(2,1)} %all-gather.3.cloned.1.call-done, bf16[2048]{0:T(1024)(128)(2,1)S(1)} %broadcast_bitcast_fusion.1), kind=kOutput, calls=%fused_computation.65 | convolution fusion | flops 2419654656 | bytes 9048064 | tf_op jit(solution)/shard_map/dot_general | solution.py:36
  346.3 8.0 %all-to-all-done.3 = f32[8,128,384]{2,1,0:T(8,128)S(1)} async-done(((f32[8,128,384]{2,1,0:T(8,128)}), f32[8,128,384]{2,1,0:T(8,128)S(1)}, u32[]{:S(2)}, u32[]{:S(2)}) %all-to-all-start.3) | async-done | bytes 1572896 | tf_op jit(solution)/shard_map/all_to_all | solution.py:126
  354.5 3.5 collective-permute-start
  363.2 5.2 %collective-permute-done = bf16[128,384]{1,0:T(8,128)(2,1)S(1)} collective-permute-done((bf16[128,384]{1,0:T(8,128)(2,1)S(1)}, bf16[128,384]{1,0:T(8,128)(2,1)S(1)}, u32[]{:S(2)}, u32[]{:S(2)}) %collective-permute-start) | collective-permute-done | bytes 98336 | tf_op jit(solution)/shard_map/ppermute | solution.py:136
  (82 shorter events, 40.2 us)
Async XLA Ops:
  9.7 6.3 %copy-start.2 = (bf16[128,6144]{1,0:T(8,128)(2,1)S(1)}, bf16[128,6144]{1,0:T(8,128)(2,1)}, u32[]{:S(2)}) copy-start(bf16[128,6144]{1,0:T(8,128)(2,1)} %param.11) | copy-start | bytes 4718596
  9.7 26.0 %all-to-all-start = ((bf16[128,16,384]{0,2,1:T(8,128)(2,1)}), bf16[128,16,384]{0,2,1:T(8,128)(2,1)S(1)}, u32[]{:S(2)}, u32[]{:S(2)}) async-start(bf16[128,16,384]{0,2,1:T(8,128)(2,1)} %bitcast.1), calls=%async_computation | async-start | bytes 3145728 | tf_op jit(solution)/shard_map/all_to_all | solution.py:64
  17.6 24.6 %copy-start.8 = (s32[16]{0:T(128)S(1)}, s32[16]{0:T(128)}, u32[]{:S(2)}) copy-start(s32[16]{0:T(128)} %constant.55) | copy-start | bytes 196
  17.6 24.6 %copy-start = (s32[16]{0:T(128)S(1)}, s32[16]{0:T(128)}, u32[]{:S(2)}) copy-start(s32[16]{0:T(128)} %param.18) | copy-start | bytes 196
  35.8 26.1 %all-to-all-start.1 = ((bf16[128,16,384]{0,2,1:T(8,128)(2,1)}), bf16[128,16,384]{0,2,1:T(8,128)(2,1)S(1)}, u32[]{:S(2)}, u32[]{:S(2)}) async-start(bf16[128,16,384]{0,2,1:T(8,128)(2,1)} %bitcast.4), calls=%async_computation.1 | async-start | bytes 3145728 | tf_op jit(solution)/shard_map/all_to_all | solution.py:63
  42.2 59.5 %reduce-scatter.2.cloned.1.call-start = ((), (), s32[]{:S(2)}) async-start(), calls=%async_computation.6 | async-start | bytes 18874368 | tf_op jit(solution)/shard_map/reduce_scatter | solution.py:83
  74.4 134.4 %all-gather.5.cloned.1.call-start = ((), (), s32[]{:S(2)}) async-start(), calls=%async_computation.8 | async-start | bytes 6684672 | tf_op jit(solution)/shard_map/all_gather | solution.py:87
  101.7 183.0 %all-gather.3.cloned.1.call-start = ((), (), s32[]{:S(2)}) async-start(), calls=%async_computation.7 | async-start | bytes 13369344 | tf_op jit(solution)/shard_map/all_gather | solution.py:96
  208.8 6.5 %copy-start.10 = (bf16[2048,1536]{1,0:T(8,128)(2,1)S(1)}, bf16[2048,1536]{1,0:T(8,128)(2,1)}, u32[]{:S(2)}) copy-start(bf16[2048,1536]{1,0:T(8,128)(2,1)} %all-gather.5.cloned.1.call-done) | copy-start | bytes 18874372
  284.7 5.9 %copy-start.9 = (bf16[2048,2,1536]{2,0,1:T(8,128)(2,1)S(1)}, bf16[2048,2,1536]{2,0,1:T(8,128)(2,1)}, u32[]{:S(2)}) copy-start(bf16[2048,2,1536]{2,0,1:T(8,128)(2,1)} %all-gather.3.cloned.1.call-done) | copy-start | bytes 37748740
  284.7 6.5 %copy-start.11 = (bf16[2,384,1536]{2,1,0:T(8,128)(2,1)S(1)}, bf16[2,384,1536]{2,1,0:T(8,128)(2,1)}, u32[]{:S(2)}) copy-start(bf16[2,384,1536]{2,1,0:T(8,128)(2,1)} %param.15) | copy-start | bytes 7077892
  291.3 1.8 copy-start.13
  298.2 29.0 %all-to-all-start.4 = ((f32[8,128,384]{2,1,0:T(8,128)}), f32[8,128,384]{2,1,0:T(8,128)S(1)}, u32[]{:S(2)}, u32[]{:S(2)}) async-start(f32[8,128,384]{2,1,0:T(8,128)} %bitcast.35), calls=%async_computation.5 | async-start | bytes 3145728 | tf_op jit(solution)/shard_map/all_to_all | solution.py:126
  304.8 4.2 %copy-start.14 = (bf16[2,384,1536]{2,1,0:T(8,128)(2,1)S(1)}, bf16[2,384,1536]{2,1,0:T(8,128)(2,1)}, u32[]{:S(2)}) copy-start(bf16[2,384,1536]{2,1,0:T(8,128)(2,1)} %param.14) | copy-start | bytes 7077892
  304.8 8.2 %slice-start = ((s8[12582912]{0:T(1024)(128)(4,1)}), s8[4194304]{0:T(1024)(128)(4,1)S(1)}, s32[]{:S(2)}) async-start(s8[12582912]{0:T(1024)(128)(4,1)} %bitcast.162), calls=%async_computation.9 | async-start | bytes 8388608
  304.8 8.2 %slice-start.1 = ((s8[12582912]{0:T(1024)(128)(4,1)}), s8[4194304]{0:T(1024)(128)(4,1)S(1)}, s32[]{:S(2)}) async-start(s8[12582912]{0:T(1024)(128)(4,1)} %bitcast.162), calls=%async_computation.10 | async-start | bytes 8388608
  309.0 3.9 %copy-start.3 = (bf16[16,128,384]{2,1,0:T(8,128)(2,1)S(1)}, bf16[16,128,384]{2,1,0:T(8,128)(2,1)}, u32[]{:S(2)}) copy-start(bf16[16,128,384]{2,1,0:T(8,128)(2,1)} %copy.18) | copy-start | bytes 4718596
  309.0 4.0 %slice-start.2 = ((s8[12582912]{0:T(1024)(128)(4,1)}), s8[4194304]{0:T(1024)(128)(4,1)S(1)}, s32[]{:S(2)}) async-start(s8[12582912]{0:T(1024)(128)(4,1)} %bitcast.162), calls=%async_computation.11 | async-start | bytes 8388608
  318.5 2.5 copy-start.12
  327.2 27.1 %all-to-all-start.3 = ((f32[8,128,384]{2,1,0:T(8,128)}), f32[8,128,384]{2,1,0:T(8,128)S(1)}, u32[]{:S(2)}, u32[]{:S(2)}) async-start(f32[8,128,384]{2,1,0:T(8,128)} %bitcast.159), calls=%async_computation.4 | async-start | bytes 3145728 | tf_op jit(solution)/shard_map/all_to_all | solution.py:126
  332.6 7.1 %copy-start.4 = (bf16[16,128,384]{2,1,0:T(8,128)(2,1)S(1)}, bf16[16,128,384]{2,1,0:T(8,128)(2,1)}, u32[]{:S(2)}) copy-start(bf16[16,128,384]{2,1,0:T(8,128)(2,1)} %copy.18) | copy-start | bytes 4718596
  346.3 14.1 %copy-start.7 = (bf16[1,384,1536]{2,1,0:T(8,128)(2,1)S(1)}, bf16[1,384,1536]{2,1,0:T(8,128)(2,1)}, u32[]{:S(2)}) copy-start(bf16[1,384,1536]{2,1,0:T(8,128)(2,1)} %fusion.80) | copy-start | bytes 3538948
  354.5 14.0 %collective-permute-start = (bf16[128,384]{1,0:T(8,128)(2,1)S(1)}, bf16[128,384]{1,0:T(8,128)(2,1)S(1)}, u32[]{:S(2)}, u32[]{:S(2)}) collective-permute-start(bf16[128,384]{1,0:T(8,128)(2,1)S(1)} %get-tuple-element.18), channel_id=1, source_target_pairs={{0,0},{1,8},{2,16},{3,24},{4,32},{5,40},{6,48},{7,56},{8,64},{9,72... | collective-permute-start | bytes 294920 | tf_op jit(solution)/shard_map/ppermute | solution.py:136
  358.0 13.1 %collective-permute-start.1 = (bf16[128,384]{1,0:T(8,128)(2,1)S(1)}, bf16[128,384]{1,0:T(8,128)(2,1)S(1)}, u32[]{:S(2)}, u32[]{:S(2)}) collective-permute-start(bf16[128,384]{1,0:T(8,128)(2,1)S(1)} %get-tuple-element.19), channel_id=1, source_target_pairs={{0,64},{1,72},{2,80},{3,88},{4,96},{5,104},{6,112},{7,120},{8,0},{... | collective-permute-start | bytes 294920 | tf_op jit(solution)/shard_map/ppermute | solution.py:136
  (3 other events, 3.8 us)
Sparse Core Ops, SparseCore 0:
  74.5 27.1 reduce-scatter.1
  104.0 104.3 all-gather.4
  210.6 74.0 all-gather.2

commit v5 on v4

--- a/solution.py
+++ b/solution.py
@@ -61,8 +61,6 @@
     expert_count = w_gate.shape[0]
     ff = gate_pre.shape[1]
     dy_cols = lax.all_to_all(out_grad, DP, split_axis=1, concat_axis=0, tiled=True)
-    x_cols = lax.all_to_all(rows_in, DP, split_axis=1, concat_axis=0, tiled=True)
-    x_cols, dy_cols = lax.optimization_barrier((x_cols, dy_cols))
     row_count = dy_cols.shape[0]
     expert_g = jnp.take(block_expert, jnp.asarray(POS_RANK), axis=0)
     masks_g = expert_masks(expert_g, row_count, expert_count)
@@ -87,6 +85,8 @@
     hid_g = lax.all_gather(hidden, DP, axis=0, tiled=True)
     pieces = lax.all_to_all(result, CHIPS, split_axis=0, concat_axis=0, tiled=True)
     hidden_grad = jnp.sum(pieces, axis=0)
+    rows_in, hidden_grad = lax.optimization_barrier((rows_in, hidden_grad))
+    x_cols = lax.all_to_all(rows_in, DP, split_axis=1, concat_axis=0, tiled=True)
 
     up_grad = (hidden_grad * silu_vals * row_mask).astype(jnp.bfloat16)
     gate_grad = (

time: 379 us -> 368 us (0.971)
  waiting for transfers between devices: 142 us -> 128 us
    all_gather x1, waiting for transfers between devices: 64 us -> 33.3 us  [shards(): packed = lax.all_gather(packed, DP, axis=0, tiled=True)]
    all_to_all x1, waiting for transfers between devices: 18.1 us -> 32.9 us  [shards(): lax.all_to_all(rows_in, DP, split_axis=1, concat_axis=0, tiled=True)]
    unnamed x38 -> x37, local copies, waits for them, and re-layouts: 9.13 us -> 7.48 us
where the time goes in v5:
time: 368 us; the launch traced here: 367 us
  waiting for transfers between devices  128 us (35%)
  blocking collectives  102 us (28%)
  matrix products  63.1 us (17%)
  starting transfers between devices  32.9 us (9%)
  between operations  14.8 us (4%)
  local copies, waits for them, and re-layouts  13.5 us (4%)
  other arithmetic  13.4 us (4%)
    all_to_all x1, blocking collectives, shards(): lax.all_to_all(result, CHIPS, split_axis=0, concat_axis=0, tiled=True)  102 us
    dot_general x10, matrix products, contract_cols(): lax.dot_general(left_op, right_op, (((1,), (1,)), ((), ())), preferred_el...  33.8 us
    all_gather x1, waiting for transfers between devices, shards(): packed = lax.all_gather(packed, DP, axis=0, tiled=True)  33.3 us
    all_to_all x1, waiting for transfers between devices, shards(): lax.all_to_all(rows_in, DP, split_axis=1, concat_axis=0, tiled=True)  32.9 us
    dot_general x6, matrix products, contract_rows(): lax.dot_general(left_op, right_op, (((0,), (0,)), ((), ())), preferred_el...  29.3 us
    reduce_scatter x1, waiting for transfers between devices, shards(): lax.psum_scatter(result.reshape(2, row_count // 2, ff), 'core', scatter_d...  25.2 us
    all_to_all x1, waiting for transfers between devices, shards(): lax.all_to_all(out_grad, DP, split_axis=1, concat_axis=0, tiled=True)  18.5 us
    all_to_all x2, starting transfers between devices, shards(): lax.all_to_all(partial_rows.reshape(N_TP, rows_dev, width), TP, split_axi...  11.3 us
  transfers between devices with their start and end apart: 9, of which 8 were waited for; matrix products, arithmetic and copies ran while one was open for 16% of the time, Pallas kernels for 0%

profile of v5, /device:TPU:3, one launch (start us, length us, event | category | flops | bytes accessed | tf_op | source)
XLA Modules:
  0.0 366.9 jit_solution(9967107635289437218)
XLA Ops:
  9.7 6.3 %all-to-all-start = ((bf16[128,16,384]{0,2,1:T(8,128)(2,1)}), bf16[128,16,384]{0,2,1:T(8,128)(2,1)S(1)}, u32[]{:S(2)}, u32[]{:S(2)}) async-start(bf16[128,16,384]{0,2,1:T(8,128)(2,1)} %bitcast.1), calls=%async_computation | async-start | bytes 3145728 | tf_op jit(solution)/shard_map/all_to_all | solution.py:63
  17.2 18.5 %all-to-all-done = bf16[128,16,384]{0,2,1:T(8,128)(2,1)S(1)} async-done(((bf16[128,16,384]{0,2,1:T(8,128)(2,1)}), bf16[128,16,384]{0,2,1:T(8,128)(2,1)S(1)}, u32[]{:S(2)}, u32[]{:S(2)}) %all-to-all-start) | async-done | bytes 1572896 | tf_op jit(solution)/shard_map/all_to_all | solution.py:63
  38.9 3.5 fusion.115
  42.3 6.5 %convolution_add_fusion = f32[2048,1536]{1,0:T(8,128)} fusion(f32[2048,1536]{1,0:T(8,128)S(1)} %fusion.115, bf16[2048,384]{1,0:T(8,128)(2,1)S(1)} %bitcast.142, bf16[2,1536,384]{2,1,0:T(8,128)(2,1)S(1)} %copy-done.1), kind=kOutput, calls=%fused_computation.1 | convolution fusion | flops 2419064832 | bytes 27918336 | tf_op jit(solution)/shard_map/dot_general | solution.py:42
  51.0 25.2 %reduce-scatter.2.cloned.1.call-done = f32[1,1024,1536]{2,1,0:T(8,128)} async-done(((f32[2,1024,1536]{2,1,0:T(8,128)}), f32[1,1024,1536]{2,1,0:T(8,128)}) %reduce-scatter.2.cloned.1.call-update) | async-done | bytes 6291472 | tf_op jit(solution)/shard_map/reduce_scatter | solution.py:81
  76.2 101.6 %all_to_all.53 = f32[8,128,1536]{2,1,0:T(8,128)} all-to-all(f32[8,128,1536]{2,1,0:T(8,128)} %bitcast.144), channel_id=1, replica_groups=mesh['x'=4,'ylo'=2,'core'=2,'z'=4,'yhi'=2] {'x','ylo'}, dimensions={0} | all-to-all | bytes 12582912 | tf_op jit(solution)/shard_map/all_to_all | solution.py:86
  177.8 3.4 reduce_sum.27
  185.0 8.9 %all-to-all-start.4 = ((bf16[128,16,384]{0,2,1:T(8,128)(2,1)}), bf16[128,16,384]{0,2,1:T(8,128)(2,1)S(1)}, u32[]{:S(2)}, u32[]{:S(2)}) async-start(bf16[128,16,384]{0,2,1:T(8,128)(2,1)} %bitcast.36), calls=%async_computation.5 | async-start | bytes 3145728 | tf_op jit(solution)/shard_map/all_to_all | solution.py:89
  194.4 32.9 %all-to-all-done.4 = bf16[128,16,384]{0,2,1:T(8,128)(2,1)S(1)} async-done(((bf16[128,16,384]{0,2,1:T(8,128)(2,1)}), bf16[128,16,384]{0,2,1:T(8,128)(2,1)S(1)}, u32[]{:S(2)}, u32[]{:S(2)}) %all-to-all-start.4) | async-done | bytes 1572896 | tf_op jit(solution)/shard_map/all_to_all | solution.py:89
  228.9 6.6 %fusion.88 = bf16[1,1536,384]{2,1,0:T(8,128)(2,1)S(1)} fusion(bf16[2048,384]{1,0:T(8,128)(2,1)S(1)} %bitcast.148, bf16[2048,1536]{1,0:T(8,128)(2,1)} %all-gather.5.cloned.1.call-done, bf16[2048]{0:T(1024)(128)(2,1)S(1)} %broadcast_bitcast_fusion), kind=kOutput, calls=%fused_computation.70 | convolution fusion | flops 2419654656 | bytes 9048064 | tf_op jit(solution)/shard_map/dot_general | solution.py:36
  235.5 3.7 fusion.91
  240.9 33.3 %all-gather.3.cloned.1.call-done = bf16[2048,2,1536]{2,0,1:T(8,128)(2,1)} async-done(((bf16[128,2,1536]{2,0,1:T(8,128)(2,1)}), bf16[2048,2,1536]{2,0,1:T(8,128)(2,1)}) %all-gather.3.cloned.1.call-update) | async-done | bytes 12582928 | tf_op jit(solution)/shard_map/all_gather | solution.py:96
  274.2 4.2 %fusion.28 = f32[1024,384]{1,0:T(8,128)S(1)} fusion(bf16[2048,2,1536]{2,0,1:T(8,128)(2,1)} %all-gather.3.cloned.1.call-done, bf16[1024]{0:T(1024)(128)(2,1)S(1)} %broadcast_bitcast_fusion.4, bf16[2,384,1536]{2,1,0:T(8,128)(2,1)} %param.15), kind=kOutput, calls=%fused_computation.30 | convolution fusion | flops 1209532416 | bytes 5900288 | tf_op jit(solution)/shard_map/dot_general | solution.py:42
  284.4 3.0 add_add_fusion.1
  287.4 6.8 %all-to-all-start.2 = ((f32[8,128,384]{2,1,0:T(8,128)}), f32[8,128,384]{2,1,0:T(8,128)S(1)}, u32[]{:S(2)}, u32[]{:S(2)}) async-start(f32[8,128,384]{2,1,0:T(8,128)} %bitcast.24), calls=%async_computation.3 | async-start | bytes 3145728 | tf_op jit(solution)/shard_map/all_to_all | solution.py:126
  294.2 4.2 %fusion.26 = f32[1024,384]{1,0:T(8,128)S(1)} fusion(bf16[2048,2,1536]{2,0,1:T(8,128)(2,1)} %all-gather.3.cloned.1.call-done, bf16[1024]{0:T(1024)(128)(2,1)S(1)} %broadcast_bitcast_fusion.3, bf16[2,384,1536]{2,1,0:T(8,128)(2,1)} %param.14), kind=kOutput, calls=%fused_computation.28 | convolution fusion | flops 1209532416 | bytes 5900288 | tf_op jit(solution)/shard_map/dot_general | solution.py:42
  298.4 3.9 %fusion.24 = f32[1024,384]{1,0:T(8,128)S(1)} fusion(bf16[2048,2,1536]{2,0,1:T(8,128)(2,1)} %all-gather.3.cloned.1.call-done, bf16[1024]{0:T(1024)(128)(2,1)S(1)} %broadcast_bitcast_fusion.3, bf16[2,384,1536]{2,1,0:T(8,128)(2,1)S(1)} %copy-done.12), kind=kOutput, calls=%fused_computation.26 | convolution fusion | flops 1209532416 | bytes 5900288 | tf_op jit(solution)/shard_map/dot_general | solution.py:42
  311.3 3.1 add_add_fusion
  316.5 4.5 %all-to-all-start.3 = ((f32[8,128,384]{2,1,0:T(8,128)}), f32[8,128,384]{2,1,0:T(8,128)S(1)}, u32[]{:S(2)}, u32[]{:S(2)}) async-start(f32[8,128,384]{2,1,0:T(8,128)} %bitcast.154), calls=%async_computation.4 | async-start | bytes 3145728 | tf_op jit(solution)/shard_map/all_to_all | solution.py:126
  321.1 7.1 %fusion.76 = bf16[1,384,1536]{2,1,0:T(8,128)(2,1)} fusion(bf16[2048,384]{1,0:T(8,128)(2,1)} %bitcast.150, bf16[2048,2,1536]{2,0,1:T(8,128)(2,1)} %all-gather.3.cloned.1.call-done, bf16[2048]{0:T(1024)(128)(2,1)S(1)} %broadcast_bitcast_fusion), kind=kOutput, calls=%fused_computation.66 | convolution fusion | flops 2419654656 | bytes 9048064 | tf_op jit(solution)/shard_map/dot_general | solution.py:36
  328.2 6.5 %fusion.79 = bf16[1,384,1536]{2,1,0:T(8,128)(2,1)} fusion(bf16[2048,384]{1,0:T(8,128)(2,1)S(1)} %bitcast.153, bf16[2048,2,1536]{2,0,1:T(8,128)(2,1)} %all-gather.3.cloned.1.call-done, bf16[2048]{0:T(1024)(128)(2,1)S(1)} %broadcast_bitcast_fusion.1), kind=kOutput, calls=%fused_computation.67 | convolution fusion | flops 2419654656 | bytes 9048064 | tf_op jit(solution)/shard_map/dot_general | solution.py:36
  334.8 8.0 %all-to-all-done.3 = f32[8,128,384]{2,1,0:T(8,128)S(1)} async-done(((f32[8,128,384]{2,1,0:T(8,128)}), f32[8,128,384]{2,1,0:T(8,128)S(1)}, u32[]{:S(2)}, u32[]{:S(2)}) %all-to-all-start.3) | async-done | bytes 1572896 | tf_op jit(solution)/shard_map/all_to_all | solution.py:126
  343.0 3.6 collective-permute-start
  352.1 4.6 %collective-permute-done = bf16[128,384]{1,0:T(8,128)(2,1)S(1)} collective-permute-done((bf16[128,384]{1,0:T(8,128)(2,1)S(1)}, bf16[128,384]{1,0:T(8,128)(2,1)S(1)}, u32[]{:S(2)}, u32[]{:S(2)}) %collective-permute-start) | collective-permute-done | bytes 98336 | tf_op jit(solution)/shard_map/ppermute | solution.py:136
  (86 shorter events, 42.2 us)
Async XLA Ops:
  9.7 6.4 %copy-start.8 = (s32[16]{0:T(128)S(1)}, s32[16]{0:T(128)}, u32[]{:S(2)}) copy-start(s32[16]{0:T(128)} %constant.55) | copy-start | bytes 196
  9.7 6.4 %copy-start = (s32[16]{0:T(128)S(1)}, s32[16]{0:T(128)}, u32[]{:S(2)}) copy-start(s32[16]{0:T(128)} %param.18) | copy-start | bytes 196
  9.7 26.0 %all-to-all-start = ((bf16[128,16,384]{0,2,1:T(8,128)(2,1)}), bf16[128,16,384]{0,2,1:T(8,128)(2,1)S(1)}, u32[]{:S(2)}, u32[]{:S(2)}) async-start(bf16[128,16,384]{0,2,1:T(8,128)(2,1)} %bitcast.1), calls=%async_computation | async-start | bytes 3145728 | tf_op jit(solution)/shard_map/all_to_all | solution.py:63
  16.1 60.1 %reduce-scatter.2.cloned.1.call-start = ((), (), s32[]{:S(2)}) async-start(), calls=%async_computation.6 | async-start | bytes 18874368 | tf_op jit(solution)/shard_map/reduce_scatter | solution.py:81
  48.8 180.0 %all-gather.5.cloned.1.call-start = ((), (), s32[]{:S(2)}) async-start(), calls=%async_computation.8 | async-start | bytes 6684672 | tf_op jit(solution)/shard_map/all_gather | solution.py:85
  76.2 198.0 %all-gather.3.cloned.1.call-start = ((), (), s32[]{:S(2)}) async-start(), calls=%async_computation.7 | async-start | bytes 13369344 | tf_op jit(solution)/shard_map/all_gather | solution.py:96
  181.7 1.7 copy-start.2
  185.0 42.3 %all-to-all-start.4 = ((bf16[128,16,384]{0,2,1:T(8,128)(2,1)}), bf16[128,16,384]{0,2,1:T(8,128)(2,1)S(1)}, u32[]{:S(2)}, u32[]{:S(2)}) async-start(bf16[128,16,384]{0,2,1:T(8,128)(2,1)} %bitcast.36), calls=%async_computation.5 | async-start | bytes 3145728 | tf_op jit(solution)/shard_map/all_to_all | solution.py:89
  228.9 6.6 %copy-start.10 = (bf16[2048,1536]{1,0:T(8,128)(2,1)S(1)}, bf16[2048,1536]{1,0:T(8,128)(2,1)}, u32[]{:S(2)}) copy-start(bf16[2048,1536]{1,0:T(8,128)(2,1)} %all-gather.5.cloned.1.call-done) | copy-start | bytes 18874372
  274.2 5.9 %copy-start.9 = (bf16[2048,2,1536]{2,0,1:T(8,128)(2,1)S(1)}, bf16[2048,2,1536]{2,0,1:T(8,128)(2,1)}, u32[]{:S(2)}) copy-start(bf16[2048,2,1536]{2,0,1:T(8,128)(2,1)} %all-gather.3.cloned.1.call-done) | copy-start | bytes 37748740
  274.2 6.5 %copy-start.11 = (bf16[2,384,1536]{2,1,0:T(8,128)(2,1)S(1)}, bf16[2,384,1536]{2,1,0:T(8,128)(2,1)}, u32[]{:S(2)}) copy-start(bf16[2,384,1536]{2,1,0:T(8,128)(2,1)} %param.15) | copy-start | bytes 7077892
  280.7 1.8 copy-start.13
  287.4 29.1 %all-to-all-start.2 = ((f32[8,128,384]{2,1,0:T(8,128)}), f32[8,128,384]{2,1,0:T(8,128)S(1)}, u32[]{:S(2)}, u32[]{:S(2)}) async-start(f32[8,128,384]{2,1,0:T(8,128)} %bitcast.24), calls=%async_computation.3 | async-start | bytes 3145728 | tf_op jit(solution)/shard_map/all_to_all | solution.py:126
  294.2 4.2 %copy-start.12 = (bf16[2,384,1536]{2,1,0:T(8,128)(2,1)S(1)}, bf16[2,384,1536]{2,1,0:T(8,128)(2,1)}, u32[]{:S(2)}) copy-start(bf16[2,384,1536]{2,1,0:T(8,128)(2,1)} %param.15) | copy-start | bytes 7077892
  294.2 8.2 %slice-start = ((s8[12582912]{0:T(1024)(128)(4,1)}), s8[4194304]{0:T(1024)(128)(4,1)S(1)}, s32[]{:S(2)}) async-start(s8[12582912]{0:T(1024)(128)(4,1)} %bitcast.157), calls=%async_computation.9 | async-start | bytes 8388608
  294.2 8.1 %slice-start.1 = ((s8[12582912]{0:T(1024)(128)(4,1)}), s8[4194304]{0:T(1024)(128)(4,1)S(1)}, s32[]{:S(2)}) async-start(s8[12582912]{0:T(1024)(128)(4,1)} %bitcast.157), calls=%async_computation.10 | async-start | bytes 8388608
  298.4 3.9 %copy-start.3 = (bf16[16,128,384]{2,1,0:T(8,128)(2,1)S(1)}, bf16[16,128,384]{2,1,0:T(8,128)(2,1)}, u32[]{:S(2)}) copy-start(bf16[16,128,384]{2,1,0:T(8,128)(2,1)} %copy.23) | copy-start | bytes 4718596
  298.4 4.0 %slice-start.2 = ((s8[12582912]{0:T(1024)(128)(4,1)}), s8[4194304]{0:T(1024)(128)(4,1)S(1)}, s32[]{:S(2)}) async-start(s8[12582912]{0:T(1024)(128)(4,1)} %bitcast.157), calls=%async_computation.11 | async-start | bytes 8388608
  309.5 1.8 copy-start.14
  316.5 26.3 %all-to-all-start.3 = ((f32[8,128,384]{2,1,0:T(8,128)}), f32[8,128,384]{2,1,0:T(8,128)S(1)}, u32[]{:S(2)}, u32[]{:S(2)}) async-start(f32[8,128,384]{2,1,0:T(8,128)} %bitcast.154), calls=%async_computation.4 | async-start | bytes 3145728 | tf_op jit(solution)/shard_map/all_to_all | solution.py:126
  321.1 7.1 %copy-start.4 = (bf16[16,128,384]{2,1,0:T(8,128)(2,1)S(1)}, bf16[16,128,384]{2,1,0:T(8,128)(2,1)}, u32[]{:S(2)}) copy-start(bf16[16,128,384]{2,1,0:T(8,128)(2,1)} %copy.23) | copy-start | bytes 4718596
  334.8 14.4 %copy-start.7 = (bf16[1,384,1536]{2,1,0:T(8,128)(2,1)S(1)}, bf16[1,384,1536]{2,1,0:T(8,128)(2,1)}, u32[]{:S(2)}) copy-start(bf16[1,384,1536]{2,1,0:T(8,128)(2,1)} %fusion.76) | copy-start | bytes 3538948
  343.0 13.7 %collective-permute-start = (bf16[128,384]{1,0:T(8,128)(2,1)S(1)}, bf16[128,384]{1,0:T(8,128)(2,1)S(1)}, u32[]{:S(2)}, u32[]{:S(2)}) collective-permute-start(bf16[128,384]{1,0:T(8,128)(2,1)S(1)} %get-tuple-element.18), channel_id=1, source_target_pairs={{0,0},{1,8},{2,16},{3,24},{4,32},{5,40},{6,48},{7,56},{8,64},{9,72... | collective-permute-start | bytes 294920 | tf_op jit(solution)/shard_map/ppermute | solution.py:136
  346.6 13.0 %collective-permute-start.1 = (bf16[128,384]{1,0:T(8,128)(2,1)S(1)}, bf16[128,384]{1,0:T(8,128)(2,1)S(1)}, u32[]{:S(2)}, u32[]{:S(2)}) collective-permute-start(bf16[128,384]{1,0:T(8,128)(2,1)S(1)} %get-tuple-element.19), channel_id=1, source_target_pairs={{0,64},{1,72},{2,80},{3,88},{4,96},{5,104},{6,112},{7,120},{8,0},{... | collective-permute-start | bytes 294920 | tf_op jit(solution)/shard_map/ppermute | solution.py:136
  (3 other events, 3.8 us)
Sparse Core Ops, SparseCore 0:
  49.0 27.1 reduce-scatter.1
  78.4 104.3 all-gather.4
  185.1 89.0 all-gather.2

commit v6 on v5

--- a/solution.py
+++ b/solution.py
@@ -92,9 +92,9 @@
     gate_grad = (
         hidden_grad * up_vals * sigmoid * (1.0 + gate_vals * (1.0 - sigmoid)) * row_mask
     ).astype(jnp.bfloat16)
-    packed = jnp.stack([gate_grad, up_grad], axis=1)
-    packed = lax.all_gather(packed, DP, axis=0, tiled=True)
-    gate_g, up_g = packed[:, 0], packed[:, 1]
+    gate_g = lax.all_gather(gate_grad, DP, axis=0, tiled=True)
+    gate_g, up_grad = lax.optimization_barrier((gate_g, up_grad))
+    up_g = lax.all_gather(up_grad, DP, axis=0, tiled=True)
 
     down_terms = []
     gate_terms = []

time: 368 us -> 395 us (1.073)
  waiting for transfers between devices: 128 us -> 185 us
  blocking collectives: 102 us -> 75.3 us
  starting transfers between devices: 32.9 us -> 28.5 us
    all_gather x1 -> x2, waiting for transfers between devices: 33.3 us -> 64.9 us  [the longest x1 43.5 us: shards(): gate_g = lax.all_gather(gate_grad, DP, axis=0, tiled=True)]
    all_to_all x1, blocking collectives: 102 us -> 75.3 us  [shards(): lax.all_to_all(result, CHIPS, split_axis=0, concat_axis=0, tiled=True)]
    all_gather x1, waiting for transfers between devices: 0.01 us -> 18.2 us  [shards(): hid_g = lax.all_gather(hidden, DP, axis=0, tiled=True)]
    all_to_all x2, waiting for transfers between devices: 10.1 us -> 18.4 us  [shards(): lax.all_to_all(partial_rows.reshape(N_TP, rows_dev, width), TP, split_axi...]
  transfers between devices with their start and end apart: 9 -> 10, of which waited for: 8 -> 10; matrix products, arithmetic and copies ran while one was open for 16% -> 15% of each run, Pallas kernels for 0% -> 0%
where the time goes in v6:
time: 395 us; the launch traced here: 394 us
  waiting for transfers between devices  185 us (47%)
  blocking collectives  75.3 us (19%)
  matrix products  63.3 us (16%)
  starting transfers between devices  28.5 us (7%)
  between operations  14.8 us (4%)
  local copies, waits for them, and re-layouts  14.1 us (4%)
  other arithmetic  13.2 us (3%)
    all_to_all x1, blocking collectives, shards(): lax.all_to_all(result, CHIPS, split_axis=0, concat_axis=0, tiled=True)  75.3 us
    all_gather x1, waiting for transfers between devices, shards(): gate_g = lax.all_gather(gate_grad, DP, axis=0, tiled=True)  43.5 us
    dot_general x10, matrix products, contract_cols(): lax.dot_general(left_op, right_op, (((1,), (1,)), ((), ())), preferred_el...  34 us
    all_to_all x1, waiting for transfers between devices, shards(): lax.all_to_all(rows_in, DP, split_axis=1, concat_axis=0, tiled=True)  31.1 us
    dot_general x6, matrix products, contract_rows(): lax.dot_general(left_op, right_op, (((0,), (0,)), ((), ())), preferred_el...  29.3 us
    reduce_scatter x1, waiting for transfers between devices, shards(): lax.psum_scatter(result.reshape(2, row_count // 2, ff), 'core', scatter_d...  25.2 us
    all_gather x1, waiting for transfers between devices, shards(): up_g = lax.all_gather(up_grad, DP, axis=0, tiled=True)  21.4 us
    all_to_all x1, waiting for transfers between devices, shards(): lax.all_to_all(out_grad, DP, split_axis=1, concat_axis=0, tiled=True)  18.5 us
  transfers between devices with their start and end apart: 10, of which 10 were waited for; matrix products, arithmetic and copies ran while one was open for 15% of the time, Pallas kernels for 0%

profile of v6, /device:TPU:3, one launch (start us, length us, event | category | flops | bytes accessed | tf_op | source)
XLA Modules:
  0.0 394.1 jit_solution(7735772528799671028)
XLA Ops:
  9.7 6.3 %all-to-all-start = ((bf16[128,16,384]{0,2,1:T(8,128)(2,1)}), bf16[128,16,384]{0,2,1:T(8,128)(2,1)S(1)}, u32[]{:S(2)}, u32[]{:S(2)}) async-start(bf16[128,16,384]{0,2,1:T(8,128)(2,1)} %bitcast.1), calls=%async_computation | async-start | bytes 3145728 | tf_op jit(solution)/shard_map/all_to_all | solution.py:63
  17.2 18.5 %all-to-all-done = bf16[128,16,384]{0,2,1:T(8,128)(2,1)S(1)} async-done(((bf16[128,16,384]{0,2,1:T(8,128)(2,1)}), bf16[128,16,384]{0,2,1:T(8,128)(2,1)S(1)}, u32[]{:S(2)}, u32[]{:S(2)}) %all-to-all-start) | async-done | bytes 1572896 | tf_op jit(solution)/shard_map/all_to_all | solution.py:63
  38.9 3.5 fusion.99
  42.3 6.5 %convolution_add_fusion = f32[2048,1536]{1,0:T(8,128)} fusion(f32[2048,1536]{1,0:T(8,128)S(1)} %fusion.99, bf16[2048,384]{1,0:T(8,128)(2,1)S(1)} %bitcast.82, bf16[2,1536,384]{2,1,0:T(8,128)(2,1)S(1)} %copy-done.1), kind=kOutput, calls=%fused_computation.1 | convolution fusion | flops 2419064832 | bytes 27918336 | tf_op jit(solution)/shard_map/dot_general | solution.py:42
  51.0 25.2 %reduce-scatter.2.cloned.1.call-done = f32[1,1024,1536]{2,1,0:T(8,128)} async-done(((f32[2,1024,1536]{2,1,0:T(8,128)}), f32[1,1024,1536]{2,1,0:T(8,128)}) %reduce-scatter.2.cloned.1.call-update) | async-done | bytes 6291472 | tf_op jit(solution)/shard_map/reduce_scatter | solution.py:81
  76.2 75.3 %all_to_all.53 = f32[8,128,1536]{2,1,0:T(8,128)} all-to-all(f32[8,128,1536]{2,1,0:T(8,128)} %bitcast.84), channel_id=1, replica_groups=mesh['x'=4,'ylo'=2,'core'=2,'z'=4,'yhi'=2] {'x','ylo'}, dimensions={0} | all-to-all | bytes 12582912 | tf_op jit(solution)/shard_map/all_to_all | solution.py:86
  157.0 43.5 %all-gather.4.cloned.1.call-done = bf16[2048,1536]{1,0:T(8,128)(2,1)} async-done(((bf16[128,1536]{1,0:T(8,128)(2,1)}), bf16[2048,1536]{1,0:T(8,128)(2,1)}) %all-gather.4.cloned.1.call-update) | async-done | bytes 6291472 | tf_op jit(solution)/shard_map/all_gather | solution.py:95
  203.2 5.4 %all-to-all-start.4 = ((bf16[128,16,384]{0,2,1:T(8,128)(2,1)}), bf16[128,16,384]{0,2,1:T(8,128)(2,1)S(1)}, u32[]{:S(2)}, u32[]{:S(2)}) async-start(bf16[128,16,384]{0,2,1:T(8,128)(2,1)} %bitcast.26), calls=%async_computation.5 | async-start | bytes 3145728 | tf_op jit(solution)/shard_map/all_to_all | solution.py:89
  209.1 31.1 %all-to-all-done.4 = bf16[128,16,384]{0,2,1:T(8,128)(2,1)S(1)} async-done(((bf16[128,16,384]{0,2,1:T(8,128)(2,1)}), bf16[128,16,384]{0,2,1:T(8,128)(2,1)S(1)}, u32[]{:S(2)}, u32[]{:S(2)}) %all-to-all-start.4) | async-done | bytes 1572896 | tf_op jit(solution)/shard_map/all_to_all | solution.py:89
  241.8 18.2 %all-gather.8.cloned.1.call-done = bf16[2048,1536]{1,0:T(8,128)(2,1)} async-done(((bf16[128,1536]{1,0:T(8,128)(2,1)}), bf16[2048,1536]{1,0:T(8,128)(2,1)}) %all-gather.8.cloned.1.call-update) | async-done | bytes 6291472 | tf_op jit(solution)/shard_map/all_gather | solution.py:85
  259.9 6.5 %fusion.60 = bf16[1,1536,384]{2,1,0:T(8,128)(2,1)S(1)} fusion(bf16[2048,384]{1,0:T(8,128)(2,1)S(1)} %bitcast.88, bf16[2048,1536]{1,0:T(8,128)(2,1)} %all-gather.8.cloned.1.call-done, bf16[2048]{0:T(1024)(128)(2,1)S(1)} %broadcast_bitcast_fusion), kind=kOutput, calls=%fused_computation.50 | convolution fusion | flops 2419654656 | bytes 9048064 | tf_op jit(solution)/shard_map/dot_general | solution.py:36
  266.5 3.7 fusion.63
  283.9 21.4 %all-gather.6.cloned.1.call-done = bf16[2048,1536]{1,0:T(8,128)(2,1)} async-done(((bf16[128,1536]{1,0:T(8,128)(2,1)}), bf16[2048,1536]{1,0:T(8,128)(2,1)}) %all-gather.6.cloned.1.call-update) | async-done | bytes 6291472 | tf_op jit(solution)/shard_map/all_gather | solution.py:97
  305.3 4.2 %fusion.30 = f32[1024,384]{1,0:T(8,128)S(1)} fusion(bf16[2048,1536]{1,0:T(8,128)(2,1)} %all-gather.6.cloned.1.call-done, bf16[1024]{0:T(1024)(128)(2,1)S(1)} %broadcast_bitcast_fusion.5, bf16[2,384,1536]{2,1,0:T(8,128)(2,1)} %param.15), kind=kOutput, calls=%fused_computation.32 | convolution fusion | flops 1209532416 | bytes 5900288 | tf_op jit(solution)/shard_map/dot_general | solution.py:42
  315.8 6.6 %all-to-all-start.2 = ((f32[8,128,384]{2,1,0:T(8,128)}), f32[8,128,384]{2,1,0:T(8,128)S(1)}, u32[]{:S(2)}, u32[]{:S(2)}) async-start(f32[8,128,384]{2,1,0:T(8,128)} %bitcast.18), calls=%async_computation.3 | async-start | bytes 3145728 | tf_op jit(solution)/shard_map/all_to_all | solution.py:126
  322.4 4.2 %fusion.22 = f32[1024,384]{1,0:T(8,128)S(1)} fusion(bf16[2048,1536]{1,0:T(8,128)(2,1)} %all-gather.6.cloned.1.call-done, bf16[1024]{0:T(1024)(128)(2,1)S(1)} %broadcast_bitcast_fusion.3, bf16[2,384,1536]{2,1,0:T(8,128)(2,1)} %param.15), kind=kOutput, calls=%fused_computation.24 | convolution fusion | flops 1209532416 | bytes 5900288 | tf_op jit(solution)/shard_map/dot_general | solution.py:42
  326.6 3.9 fusion.18
  333.6 11.2 %all-to-all-done.2 = f32[8,128,384]{2,1,0:T(8,128)S(1)} async-done(((f32[8,128,384]{2,1,0:T(8,128)}), f32[8,128,384]{2,1,0:T(8,128)S(1)}, u32[]{:S(2)}, u32[]{:S(2)}) %all-to-all-start.2) | async-done | bytes 1572896 | tf_op jit(solution)/shard_map/all_to_all | solution.py:126
  344.7 3.8 all-to-all-start.3
  348.6 7.1 %fusion.66 = bf16[1,384,1536]{2,1,0:T(8,128)(2,1)} fusion(bf16[2048,384]{1,0:T(8,128)(2,1)} %bitcast.90, bf16[2048,1536]{1,0:T(8,128)(2,1)} %all-gather.6.cloned.1.call-done, bf16[2048]{0:T(1024)(128)(2,1)S(1)} %broadcast_bitcast_fusion), kind=kOutput, calls=%fused_computation.52 | convolution fusion | flops 2419654656 | bytes 9048064 | tf_op jit(solution)/shard_map/dot_general | solution.py:36
  355.7 6.6 %fusion.69 = bf16[1,384,1536]{2,1,0:T(8,128)(2,1)} fusion(bf16[2048,384]{1,0:T(8,128)(2,1)S(1)} %bitcast.93, bf16[2048,1536]{1,0:T(8,128)(2,1)} %all-gather.6.cloned.1.call-done, bf16[2048]{0:T(1024)(128)(2,1)S(1)} %broadcast_bitcast_fusion.1), kind=kOutput, calls=%fused_computation.53 | convolution fusion | flops 2419654656 | bytes 9048064 | tf_op jit(solution)/shard_map/dot_general | solution.py:36
  362.4 7.3 %all-to-all-done.3 = f32[8,128,384]{2,1,0:T(8,128)S(1)} async-done(((f32[8,128,384]{2,1,0:T(8,128)}), f32[8,128,384]{2,1,0:T(8,128)S(1)}, u32[]{:S(2)}, u32[]{:S(2)}) %all-to-all-start.3) | async-done | bytes 1572896 | tf_op jit(solution)/shard_map/all_to_all | solution.py:126
  369.9 3.8 collective-permute-start
  378.9 4.9 %collective-permute-done = bf16[128,384]{1,0:T(8,128)(2,1)S(1)} collective-permute-done((bf16[128,384]{1,0:T(8,128)(2,1)S(1)}, bf16[128,384]{1,0:T(8,128)(2,1)S(1)}, u32[]{:S(2)}, u32[]{:S(2)}) %collective-permute-start) | collective-permute-done | bytes 98336 | tf_op jit(solution)/shard_map/ppermute | solution.py:136
  (96 shorter events, 50.6 us)
Async XLA Ops:
  9.7 6.4 %copy-start.7 = (s32[16]{0:T(128)S(1)}, s32[16]{0:T(128)}, u32[]{:S(2)}) copy-start(s32[16]{0:T(128)} %constant.55) | copy-start | bytes 196
  9.7 6.4 %copy-start = (s32[16]{0:T(128)S(1)}, s32[16]{0:T(128)}, u32[]{:S(2)}) copy-start(s32[16]{0:T(128)} %param.18) | copy-start | bytes 196
  9.7 26.0 %all-to-all-start = ((bf16[128,16,384]{0,2,1:T(8,128)(2,1)}), bf16[128,16,384]{0,2,1:T(8,128)(2,1)S(1)}, u32[]{:S(2)}, u32[]{:S(2)}) async-start(bf16[128,16,384]{0,2,1:T(8,128)(2,1)} %bitcast.1), calls=%async_computation | async-start | bytes 3145728 | tf_op jit(solution)/shard_map/all_to_all | solution.py:63
  16.1 60.1 %reduce-scatter.2.cloned.1.call-start = ((), (), s32[]{:S(2)}) async-start(), calls=%async_computation.6 | async-start | bytes 18874368 | tf_op jit(solution)/shard_map/reduce_scatter | solution.py:81
  48.9 151.6 %all-gather.4.cloned.1.call-start = ((), (), s32[]{:S(2)}) async-start(), calls=%async_computation.7 | async-start | bytes 6684672 | tf_op jit(solution)/shard_map/all_gather | solution.py:95
  156.2 103.7 %all-gather.8.cloned.1.call-start = ((), (), s32[]{:S(2)}) async-start(), calls=%async_computation.9 | async-start | bytes 6684672 | tf_op jit(solution)/shard_map/all_gather | solution.py:85
  157.0 148.3 %all-gather.6.cloned.1.call-start = ((), (), s32[]{:S(2)}) async-start(), calls=%async_computation.8 | async-start | bytes 6684672 | tf_op jit(solution)/shard_map/all_gather | solution.py:97
  203.2 37.0 %all-to-all-start.4 = ((bf16[128,16,384]{0,2,1:T(8,128)(2,1)}), bf16[128,16,384]{0,2,1:T(8,128)(2,1)S(1)}, u32[]{:S(2)}, u32[]{:S(2)}) async-start(bf16[128,16,384]{0,2,1:T(8,128)(2,1)} %bitcast.26), calls=%async_computation.5 | async-start | bytes 3145728 | tf_op jit(solution)/shard_map/all_to_all | solution.py:89
  259.9 6.5 %copy-start.9 = (bf16[2048,1536]{1,0:T(8,128)(2,1)S(1)}, bf16[2048,1536]{1,0:T(8,128)(2,1)}, u32[]{:S(2)}) copy-start(bf16[2048,1536]{1,0:T(8,128)(2,1)} %all-gather.8.cloned.1.call-done) | copy-start | bytes 18874372
  259.9 11.9 %slice-start = ((s8[6291456]{0:T(1024)(128)(4,1)}), s8[4194304]{0:T(1024)(128)(4,1)S(1)}, s32[]{:S(2)}) async-start(s8[6291456]{0:T(1024)(128)(4,1)} %bitcast.97), calls=%async_computation.10 | async-start | bytes 8388608
  266.4 5.4 %slice-start.1 = ((s8[6291456]{0:T(1024)(128)(4,1)}), s8[2097152]{0:T(1024)(128)(4,1)S(1)}, s32[]{:S(2)}) async-start(s8[6291456]{0:T(1024)(128)(4,1)} %bitcast.97), calls=%async_computation.11 | async-start | bytes 4194304
  305.3 4.2 %copy-start.8 = (bf16[2048,1536]{1,0:T(8,128)(2,1)S(1)}, bf16[2048,1536]{1,0:T(8,128)(2,1)}, u32[]{:S(2)}) copy-start(bf16[2048,1536]{1,0:T(8,128)(2,1)} %all-gather.6.cloned.1.call-done) | copy-start | bytes 18874372
  305.3 4.8 %copy-start.10 = (bf16[2,384,1536]{2,1,0:T(8,128)(2,1)S(1)}, bf16[2,384,1536]{2,1,0:T(8,128)(2,1)}, u32[]{:S(2)}) copy-start(bf16[2,384,1536]{2,1,0:T(8,128)(2,1)} %param.15) | copy-start | bytes 7077892
  305.3 6.6 %slice-start.2 = ((s8[6291456]{0:T(1024)(128)(4,1)}), s8[4194304]{0:T(1024)(128)(4,1)S(1)}, s32[]{:S(2)}) async-start(s8[6291456]{0:T(1024)(128)(4,1)} %bitcast.99), calls=%async_computation.12 | async-start | bytes 8388608
  315.8 29.0 %all-to-all-start.2 = ((f32[8,128,384]{2,1,0:T(8,128)}), f32[8,128,384]{2,1,0:T(8,128)S(1)}, u32[]{:S(2)}, u32[]{:S(2)}) async-start(f32[8,128,384]{2,1,0:T(8,128)} %bitcast.18), calls=%async_computation.3 | async-start | bytes 3145728 | tf_op jit(solution)/shard_map/all_to_all | solution.py:126
  322.4 4.2 %copy-start.11 = (bf16[2,384,1536]{2,1,0:T(8,128)(2,1)S(1)}, bf16[2,384,1536]{2,1,0:T(8,128)(2,1)}, u32[]{:S(2)}) copy-start(bf16[2,384,1536]{2,1,0:T(8,128)(2,1)} %param.15) | copy-start | bytes 7077892
  322.4 8.1 %slice-start.4 = ((s8[6291456]{0:T(1024)(128)(4,1)}), s8[4194304]{0:T(1024)(128)(4,1)S(1)}, s32[]{:S(2)}) async-start(s8[6291456]{0:T(1024)(128)(4,1)} %bitcast.101), calls=%async_computation.14 | async-start | bytes 8388608
  326.6 3.9 slice-start.5
  326.6 3.9 copy-start.14
  344.7 24.9 %all-to-all-start.3 = ((f32[8,128,384]{2,1,0:T(8,128)}), f32[8,128,384]{2,1,0:T(8,128)S(1)}, u32[]{:S(2)}, u32[]{:S(2)}) async-start(f32[8,128,384]{2,1,0:T(8,128)} %bitcast.94), calls=%async_computation.4 | async-start | bytes 3145728 | tf_op jit(solution)/shard_map/all_to_all | solution.py:126
  348.6 7.1 %copy-start.3 = (bf16[16,128,384]{2,1,0:T(8,128)(2,1)S(1)}, bf16[16,128,384]{2,1,0:T(8,128)(2,1)}, u32[]{:S(2)}) copy-start(bf16[16,128,384]{2,1,0:T(8,128)(2,1)} %copy.23) | copy-start | bytes 4718596
  362.4 13.6 %copy-start.6 = (bf16[1,384,1536]{2,1,0:T(8,128)(2,1)S(1)}, bf16[1,384,1536]{2,1,0:T(8,128)(2,1)}, u32[]{:S(2)}) copy-start(bf16[1,384,1536]{2,1,0:T(8,128)(2,1)} %fusion.66) | copy-start | bytes 3538948
  369.9 14.0 %collective-permute-start = (bf16[128,384]{1,0:T(8,128)(2,1)S(1)}, bf16[128,384]{1,0:T(8,128)(2,1)S(1)}, u32[]{:S(2)}, u32[]{:S(2)}) collective-permute-start(bf16[128,384]{1,0:T(8,128)(2,1)S(1)} %get-tuple-element.22), channel_id=1, source_target_pairs={{0,0},{1,8},{2,16},{3,24},{4,32},{5,40},{6,48},{7,56},{8,64},{9,72... | collective-permute-start | bytes 294920 | tf_op jit(solution)/shard_map/ppermute | solution.py:136
  373.7 13.1 %collective-permute-start.1 = (bf16[128,384]{1,0:T(8,128)(2,1)S(1)}, bf16[128,384]{1,0:T(8,128)(2,1)S(1)}, u32[]{:S(2)}, u32[]{:S(2)}) collective-permute-start(bf16[128,384]{1,0:T(8,128)(2,1)S(1)} %get-tuple-element.23), channel_id=1, source_target_pairs={{0,64},{1,72},{2,80},{3,88},{4,96},{5,104},{6,112},{7,120},{8,0},{... | collective-permute-start | bytes 294920 | tf_op jit(solution)/shard_map/ppermute | solution.py:136
  (7 other events, 13.0 us)
Sparse Core Ops, SparseCore 0:
  49.0 27.1 reduce-scatter.1
  156.4 44.1 all-gather.3
  202.8 57.0 all-gather.7
  262.1 43.1 all-gather.5

commit v7 on v5

--- a/solution.py
+++ b/solution.py
@@ -73,16 +73,16 @@
     sigmoid = jax.nn.sigmoid(gate_vals)
     silu_vals = gate_vals * sigmoid
     hidden = (silu_vals * up_vals * row_mask).astype(jnp.bfloat16)
+    hid_g = lax.all_gather(hidden, DP, axis=0, tiled=True)
 
     dy_g = to_gathered_order(dy_cols)
     result = jnp.zeros((row_count, ff), jnp.float32)
     for which in range(expert_count):
         result = result + contract_cols(dy_g * masks_g[which], w_down[which])
+    hid_g, result = lax.optimization_barrier((hid_g, result))
     result = lax.psum_scatter(
         result.reshape(2, row_count // 2, ff), "core", scatter_dimension=0, tiled=True
     ).reshape(N_DP // 2, rows_dev, ff)
-    hidden, result = lax.optimization_barrier((hidden, result))
-    hid_g = lax.all_gather(hidden, DP, axis=0, tiled=True)
     pieces = lax.all_to_all(result, CHIPS, split_axis=0, concat_axis=0, tiled=True)
     hidden_grad = jnp.sum(pieces, axis=0)
     rows_in, hidden_grad = lax.optimization_barrier((rows_in, hidden_grad))

time: 368 us -> 360 us (0.978)
  blocking collectives: 102 us -> 75.3 us
  waiting for transfers between devices: 128 us -> 147 us
    all_to_all x1, blocking collectives: 102 us -> 75.3 us  [shards(): lax.all_to_all(result, CHIPS, split_axis=0, concat_axis=0, tiled=True)]
    all_to_all x1, waiting for transfers between devices: 32.9 us -> 18.7 us  [shards(): lax.all_to_all(rows_in, DP, split_axis=1, concat_axis=0, tiled=True)]
    all_gather x1, waiting for transfers between devices: 33.3 us -> 45.7 us  [shards(): packed = lax.all_gather(packed, DP, axis=0, tiled=True)]
    all_to_all x1, waiting for transfers between devices: 18.5 us -> 30.3 us  [shards(): lax.all_to_all(out_grad, DP, split_axis=1, concat_axis=0, tiled=True)]
    all_gather x1, waiting for transfers between devices: 0.01 us -> 6.63 us  [shards(): hid_g = lax.all_gather(hidden, DP, axis=0, tiled=True)]
  transfers between devices with their start and end apart: 9 -> 9, of which waited for: 8 -> 9; matrix products, arithmetic and copies ran while one was open for 16% -> 19% of each run, Pallas kernels for 0% -> 0%
where the time goes in v7:
time: 360 us
  waiting for transfers between devices  147 us (41%)
  blocking collectives  75.3 us (21%)
  matrix products  65.7 us (18%)
  starting transfers between devices  30.8 us (9%)
  between operations  14.8 us (4%)
  other arithmetic  14.5 us (4%)
  local copies, waits for them, and re-layouts  11.9 us (3%)
    all_to_all x1, blocking collectives, shards(): lax.all_to_all(result, CHIPS, split_axis=0, concat_axis=0, tiled=True)  75.3 us
    all_gather x1, waiting for transfers between devices, shards(): packed = lax.all_gather(packed, DP, axis=0, tiled=True)  45.7 us
    dot_general x10, matrix products, contract_cols(): lax.dot_general(left_op, right_op, (((1,), (1,)), ((), ())), preferred_el...  34 us
    dot_general x6, matrix products, contract_rows(): lax.dot_general(left_op, right_op, (((0,), (0,)), ((), ())), preferred_el...  31.7 us
    all_to_all x1, waiting for transfers between devices, shards(): lax.all_to_all(out_grad, DP, split_axis=1, concat_axis=0, tiled=True)  30.3 us
    reduce_scatter x1, waiting for transfers between devices, shards(): lax.psum_scatter(result.reshape(2, row_count // 2, ff), 'core', scatter_d...  28.4 us
    all_to_all x1, waiting for transfers between devices, shards(): lax.all_to_all(rows_in, DP, split_axis=1, concat_axis=0, tiled=True)  18.7 us
    all_to_all x2, starting transfers between devices, shards(): lax.all_to_all(partial_rows.reshape(N_TP, rows_dev, width), TP, split_axi...  12.2 us
  transfers between devices with their start and end apart: 9, of which 9 were waited for; matrix products, arithmetic and copies ran while one was open for 19% of the time, Pallas kernels for 0%

profile of v7, /device:TPU:3, one launch (start us, length us, event | category | flops | bytes accessed | tf_op | source)
XLA Modules:
  0.0 359.7 jit_solution(13972185572916459537)
XLA Ops:
  11.7 6.3 %all-to-all-start = ((bf16[128,16,384]{0,2,1:T(8,128)(2,1)}), bf16[128,16,384]{0,2,1:T(8,128)(2,1)S(1)}, u32[]{:S(2)}, u32[]{:S(2)}) async-start(bf16[128,16,384]{0,2,1:T(8,128)(2,1)} %bitcast.1), calls=%async_computation | async-start | bytes 3145728 | tf_op jit(solution)/shard_map/all_to_all | solution.py:63
  19.2 30.3 %all-to-all-done = bf16[128,16,384]{0,2,1:T(8,128)(2,1)S(1)} async-done(((bf16[128,16,384]{0,2,1:T(8,128)(2,1)}), bf16[128,16,384]{0,2,1:T(8,128)(2,1)S(1)}, u32[]{:S(2)}, u32[]{:S(2)}) %all-to-all-start) | async-done | bytes 1572896 | tf_op jit(solution)/shard_map/all_to_all | solution.py:63
  52.7 3.5 fusion.115
  56.1 6.7 %convolution_add_fusion = f32[2048,1536]{1,0:T(8,128)} fusion(f32[2048,1536]{1,0:T(8,128)S(1)} %fusion.115, bf16[2048,384]{1,0:T(8,128)(2,1)S(1)} %bitcast.142, bf16[2,1536,384]{2,1,0:T(8,128)(2,1)S(1)} %copy-done.1), kind=kOutput, calls=%fused_computation.1 | convolution fusion | flops 2419064832 | bytes 27918336 | tf_op jit(solution)/shard_map/dot_general | solution.py:42
  62.8 6.6 %all-gather.3.cloned.1.call-done = bf16[2048,1536]{1,0:T(8,128)(2,1)} async-done(((bf16[128,1536]{1,0:T(8,128)(2,1)}), bf16[2048,1536]{1,0:T(8,128)(2,1)}) %all-gather.3.cloned.1.call-update) | async-done | bytes 6291472 | tf_op jit(solution)/shard_map/all_gather | solution.py:76
  69.5 28.4 %reduce-scatter.2.cloned.1.call-done = f32[1,1024,1536]{2,1,0:T(8,128)} async-done(((f32[2,1024,1536]{2,1,0:T(8,128)}), f32[1,1024,1536]{2,1,0:T(8,128)}) %reduce-scatter.2.cloned.1.call-update) | async-done | bytes 6291472 | tf_op jit(solution)/shard_map/reduce_scatter | solution.py:83
  97.9 75.3 %all_to_all.53 = f32[8,128,1536]{2,1,0:T(8,128)} all-to-all(f32[8,128,1536]{2,1,0:T(8,128)} %bitcast.144), channel_id=1, replica_groups=mesh['x'=4,'ylo'=2,'core'=2,'z'=4,'yhi'=2] {'x','ylo'}, dimensions={0} | all-to-all | bytes 12582912 | tf_op jit(solution)/shard_map/all_to_all | solution.py:86
  173.2 3.4 reduce_sum.27
  180.4 6.1 %all-to-all-start.4 = ((bf16[128,16,384]{0,2,1:T(8,128)(2,1)}), bf16[128,16,384]{0,2,1:T(8,128)(2,1)S(1)}, u32[]{:S(2)}, u32[]{:S(2)}) async-start(bf16[128,16,384]{0,2,1:T(8,128)(2,1)} %bitcast.36), calls=%async_computation.5 | async-start | bytes 3145728 | tf_op jit(solution)/shard_map/all_to_all | solution.py:89
  186.5 6.3 %fusion.88 = bf16[1,1536,384]{2,1,0:T(8,128)(2,1)S(1)} fusion(bf16[2048,384]{1,0:T(8,128)(2,1)S(1)} %bitcast.148, bf16[2048,1536]{1,0:T(8,128)(2,1)} %all-gather.3.cloned.1.call-done, bf16[2048]{0:T(1024)(128)(2,1)S(1)} %broadcast_bitcast_fusion), kind=kOutput, calls=%fused_computation.70 | convolution fusion | flops 2419654656 | bytes 9048064 | tf_op jit(solution)/shard_map/dot_general | solution.py:36
  192.8 6.3 %fusion.91 = bf16[1,1536,384]{2,1,0:T(8,128)(2,1)S(1)} fusion(bf16[2048,384]{1,0:T(8,128)(2,1)S(1)} %bitcast.149, bf16[2048,1536]{1,0:T(8,128)(2,1)} %all-gather.3.cloned.1.call-done, bf16[2048]{0:T(1024)(128)(2,1)S(1)} %broadcast_bitcast_fusion.1), kind=kOutput, calls=%fused_computation.71 | convolution fusion | flops 2419654656 | bytes 9048064 | tf_op jit(solution)/shard_map/dot_general | solution.py:36
  200.8 18.7 %all-to-all-done.4 = bf16[128,16,384]{0,2,1:T(8,128)(2,1)S(1)} async-done(((bf16[128,16,384]{0,2,1:T(8,128)(2,1)}), bf16[128,16,384]{0,2,1:T(8,128)(2,1)S(1)}, u32[]{:S(2)}, u32[]{:S(2)}) %all-to-all-start.4) | async-done | bytes 1572896 | tf_op jit(solution)/shard_map/all_to_all | solution.py:89
  221.1 45.7 %all-gather.5.cloned.1.call-done = bf16[2048,2,1536]{2,0,1:T(8,128)(2,1)} async-done(((bf16[128,2,1536]{2,0,1:T(8,128)(2,1)}), bf16[2048,2,1536]{2,0,1:T(8,128)(2,1)}) %all-gather.5.cloned.1.call-update) | async-done | bytes 12582928 | tf_op jit(solution)/shard_map/all_gather | solution.py:96
  266.8 4.2 %fusion.20 = f32[1024,384]{1,0:T(8,128)S(1)} fusion(bf16[2048,2,1536]{2,0,1:T(8,128)(2,1)} %all-gather.5.cloned.1.call-done, bf16[1024]{0:T(1024)(128)(2,1)S(1)} %broadcast_bitcast_fusion.2, bf16[2,384,1536]{2,1,0:T(8,128)(2,1)} %param.15), kind=kOutput, calls=%fused_computation.22 | convolution fusion | flops 1209532416 | bytes 5900288 | tf_op jit(solution)/shard_map/dot_general | solution.py:42
  279.3 6.8 %all-to-all-start.3 = ((f32[8,128,384]{2,1,0:T(8,128)}), f32[8,128,384]{2,1,0:T(8,128)S(1)}, u32[]{:S(2)}, u32[]{:S(2)}) async-start(f32[8,128,384]{2,1,0:T(8,128)} %bitcast.32), calls=%async_computation.4 | async-start | bytes 3145728 | tf_op jit(solution)/shard_map/all_to_all | solution.py:126
  286.1 4.2 %fusion.32 = f32[1024,384]{1,0:T(8,128)S(1)} fusion(bf16[2048,2,1536]{2,0,1:T(8,128)(2,1)} %all-gather.5.cloned.1.call-done, bf16[1024]{0:T(1024)(128)(2,1)S(1)} %broadcast_bitcast_fusion.5, bf16[2,384,1536]{2,1,0:T(8,128)(2,1)} %param.15), kind=kOutput, calls=%fused_computation.34 | convolution fusion | flops 1209532416 | bytes 5900288 | tf_op jit(solution)/shard_map/dot_general | solution.py:42
  290.3 3.9 %fusion.34 = f32[1024,384]{1,0:T(8,128)S(1)} fusion(bf16[2048,2,1536]{2,0,1:T(8,128)(2,1)} %all-gather.5.cloned.1.call-done, bf16[1024]{0:T(1024)(128)(2,1)S(1)} %broadcast_bitcast_fusion.5, bf16[2,384,1536]{2,1,0:T(8,128)(2,1)S(1)} %copy-done.14), kind=kOutput, calls=%fused_computation.36 | convolution fusion | flops 1209532416 | bytes 5900288 | tf_op jit(solution)/shard_map/dot_general | solution.py:42
  304.1 3.1 add_add_fusion.1
  308.4 5.4 %all-to-all-start.2 = ((f32[8,128,384]{2,1,0:T(8,128)}), f32[8,128,384]{2,1,0:T(8,128)S(1)}, u32[]{:S(2)}, u32[]{:S(2)}) async-start(f32[8,128,384]{2,1,0:T(8,128)} %bitcast.154), calls=%async_computation.3 | async-start | bytes 3145728 | tf_op jit(solution)/shard_map/all_to_all | solution.py:126
  313.9 7.1 %fusion.76 = bf16[1,384,1536]{2,1,0:T(8,128)(2,1)} fusion(bf16[2048,384]{1,0:T(8,128)(2,1)} %bitcast.150, bf16[2048,2,1536]{2,0,1:T(8,128)(2,1)} %all-gather.5.cloned.1.call-done, bf16[2048]{0:T(1024)(128)(2,1)S(1)} %broadcast_bitcast_fusion), kind=kOutput, calls=%fused_computation.66 | convolution fusion | flops 2419654656 | bytes 9048064 | tf_op jit(solution)/shard_map/dot_general | solution.py:36
  321.0 6.5 %fusion.79 = bf16[1,384,1536]{2,1,0:T(8,128)(2,1)} fusion(bf16[2048,384]{1,0:T(8,128)(2,1)S(1)} %bitcast.153, bf16[2048,2,1536]{2,0,1:T(8,128)(2,1)} %all-gather.5.cloned.1.call-done, bf16[2048]{0:T(1024)(128)(2,1)S(1)} %broadcast_bitcast_fusion.1), kind=kOutput, calls=%fused_computation.67 | convolution fusion | flops 2419654656 | bytes 9048064 | tf_op jit(solution)/shard_map/dot_general | solution.py:36
  327.6 8.1 %all-to-all-done.2 = f32[8,128,384]{2,1,0:T(8,128)S(1)} async-done(((f32[8,128,384]{2,1,0:T(8,128)}), f32[8,128,384]{2,1,0:T(8,128)S(1)}, u32[]{:S(2)}, u32[]{:S(2)}) %all-to-all-start.2) | async-done | bytes 1572896 | tf_op jit(solution)/shard_map/all_to_all | solution.py:126
  335.8 3.6 collective-permute-start
  344.9 4.6 %collective-permute-done = bf16[128,384]{1,0:T(8,128)(2,1)S(1)} collective-permute-done((bf16[128,384]{1,0:T(8,128)(2,1)S(1)}, bf16[128,384]{1,0:T(8,128)(2,1)S(1)}, u32[]{:S(2)}, u32[]{:S(2)}) %collective-permute-start) | collective-permute-done | bytes 98336 | tf_op jit(solution)/shard_map/ppermute | solution.py:136
  (86 shorter events, 43.8 us)
Async XLA Ops:
  7.2 3.0 copy-start.2
  7.2 62.3 %all-gather.3.cloned.1.call-start = ((), (), s32[]{:S(2)}) async-start(), calls=%async_computation.6 | async-start | bytes 6684672 | tf_op jit(solution)/shard_map/all_gather | solution.py:76
  11.7 6.4 %copy-start.9 = (s32[16]{0:T(128)S(1)}, s32[16]{0:T(128)}, u32[]{:S(2)}) copy-start(s32[16]{0:T(128)} %constant.55) | copy-start | bytes 196
  11.7 6.4 %copy-start = (s32[16]{0:T(128)S(1)}, s32[16]{0:T(128)}, u32[]{:S(2)}) copy-start(s32[16]{0:T(128)} %param.18) | copy-start | bytes 196
  11.7 37.8 %all-to-all-start = ((bf16[128,16,384]{0,2,1:T(8,128)(2,1)}), bf16[128,16,384]{0,2,1:T(8,128)(2,1)S(1)}, u32[]{:S(2)}, u32[]{:S(2)}) async-start(bf16[128,16,384]{0,2,1:T(8,128)(2,1)} %bitcast.1), calls=%async_computation | async-start | bytes 3145728 | tf_op jit(solution)/shard_map/all_to_all | solution.py:63
  18.0 79.9 %reduce-scatter.2.cloned.1.call-start = ((), (), s32[]{:S(2)}) async-start(), calls=%async_computation.7 | async-start | bytes 18874368 | tf_op jit(solution)/shard_map/reduce_scatter | solution.py:83
  69.5 197.3 %all-gather.5.cloned.1.call-start = ((), (), s32[]{:S(2)}) async-start(), calls=%async_computation.8 | async-start | bytes 13369344 | tf_op jit(solution)/shard_map/all_gather | solution.py:96
  173.2 3.4 copy-start.6
  173.2 3.4 copy-start.7
  180.4 39.1 %all-to-all-start.4 = ((bf16[128,16,384]{0,2,1:T(8,128)(2,1)}), bf16[128,16,384]{0,2,1:T(8,128)(2,1)S(1)}, u32[]{:S(2)}, u32[]{:S(2)}) async-start(bf16[128,16,384]{0,2,1:T(8,128)(2,1)} %bitcast.36), calls=%async_computation.5 | async-start | bytes 3145728 | tf_op jit(solution)/shard_map/all_to_all | solution.py:89
  221.1 49.9 %copy-start.11 = (bf16[2,384,1536]{2,1,0:T(8,128)(2,1)S(1)}, bf16[2,384,1536]{2,1,0:T(8,128)(2,1)}, u32[]{:S(2)}) copy-start(bf16[2,384,1536]{2,1,0:T(8,128)(2,1)} %param.15) | copy-start | bytes 7077892
  266.8 5.9 %copy-start.10 = (bf16[2048,2,1536]{2,0,1:T(8,128)(2,1)S(1)}, bf16[2048,2,1536]{2,0,1:T(8,128)(2,1)}, u32[]{:S(2)}) copy-start(bf16[2048,2,1536]{2,0,1:T(8,128)(2,1)} %all-gather.5.cloned.1.call-done) | copy-start | bytes 37748740
  279.3 29.1 %all-to-all-start.3 = ((f32[8,128,384]{2,1,0:T(8,128)}), f32[8,128,384]{2,1,0:T(8,128)S(1)}, u32[]{:S(2)}, u32[]{:S(2)}) async-start(f32[8,128,384]{2,1,0:T(8,128)} %bitcast.32), calls=%async_computation.4 | async-start | bytes 3145728 | tf_op jit(solution)/shard_map/all_to_all | solution.py:126
  286.1 4.2 %copy-start.14 = (bf16[2,384,1536]{2,1,0:T(8,128)(2,1)S(1)}, bf16[2,384,1536]{2,1,0:T(8,128)(2,1)}, u32[]{:S(2)}) copy-start(bf16[2,384,1536]{2,1,0:T(8,128)(2,1)} %param.14) | copy-start | bytes 7077892
  286.1 8.2 %slice-start = ((s8[12582912]{0:T(1024)(128)(4,1)}), s8[4194304]{0:T(1024)(128)(4,1)S(1)}, s32[]{:S(2)}) async-start(s8[12582912]{0:T(1024)(128)(4,1)} %bitcast.157), calls=%async_computation.9 | async-start | bytes 8388608
  286.1 8.2 %slice-start.1 = ((s8[12582912]{0:T(1024)(128)(4,1)}), s8[4194304]{0:T(1024)(128)(4,1)S(1)}, s32[]{:S(2)}) async-start(s8[12582912]{0:T(1024)(128)(4,1)} %bitcast.157), calls=%async_computation.10 | async-start | bytes 8388608
  290.3 3.9 %copy-start.4 = (bf16[16,128,384]{2,1,0:T(8,128)(2,1)S(1)}, bf16[16,128,384]{2,1,0:T(8,128)(2,1)}, u32[]{:S(2)}) copy-start(bf16[16,128,384]{2,1,0:T(8,128)(2,1)} %copy.23) | copy-start | bytes 4718596
  290.3 4.0 %slice-start.2 = ((s8[12582912]{0:T(1024)(128)(4,1)}), s8[4194304]{0:T(1024)(128)(4,1)S(1)}, s32[]{:S(2)}) async-start(s8[12582912]{0:T(1024)(128)(4,1)} %bitcast.157), calls=%async_computation.11 | async-start | bytes 8388608
  299.8 2.5 copy-start.12
  308.4 27.2 %all-to-all-start.2 = ((f32[8,128,384]{2,1,0:T(8,128)}), f32[8,128,384]{2,1,0:T(8,128)S(1)}, u32[]{:S(2)}, u32[]{:S(2)}) async-start(f32[8,128,384]{2,1,0:T(8,128)} %bitcast.154), calls=%async_computation.3 | async-start | bytes 3145728 | tf_op jit(solution)/shard_map/all_to_all | solution.py:126
  313.9 7.1 %copy-start.5 = (bf16[16,128,384]{2,1,0:T(8,128)(2,1)S(1)}, bf16[16,128,384]{2,1,0:T(8,128)(2,1)}, u32[]{:S(2)}) copy-start(bf16[16,128,384]{2,1,0:T(8,128)(2,1)} %copy.23) | copy-start | bytes 4718596
  327.6 14.4 %copy-start.8 = (bf16[1,384,1536]{2,1,0:T(8,128)(2,1)S(1)}, bf16[1,384,1536]{2,1,0:T(8,128)(2,1)}, u32[]{:S(2)}) copy-start(bf16[1,384,1536]{2,1,0:T(8,128)(2,1)} %fusion.76) | copy-start | bytes 3538948
  335.8 13.7 %collective-permute-start = (bf16[128,384]{1,0:T(8,128)(2,1)S(1)}, bf16[128,384]{1,0:T(8,128)(2,1)S(1)}, u32[]{:S(2)}, u32[]{:S(2)}) collective-permute-start(bf16[128,384]{1,0:T(8,128)(2,1)S(1)} %get-tuple-element.18), channel_id=1, source_target_pairs={{0,0},{1,8},{2,16},{3,24},{4,32},{5,40},{6,48},{7,56},{8,64},{9,72... | collective-permute-start | bytes 294920 | tf_op jit(solution)/shard_map/ppermute | solution.py:136
  339.4 13.0 %collective-permute-start.1 = (bf16[128,384]{1,0:T(8,128)(2,1)S(1)}, bf16[128,384]{1,0:T(8,128)(2,1)S(1)}, u32[]{:S(2)}, u32[]{:S(2)}) collective-permute-start(bf16[128,384]{1,0:T(8,128)(2,1)S(1)} %get-tuple-element.19), channel_id=1, source_target_pairs={{0,64},{1,72},{2,80},{3,88},{4,96},{5,104},{6,112},{7,120},{8,0},{... | collective-permute-start | bytes 294920 | tf_op jit(solution)/shard_map/ppermute | solution.py:136
  (3 other events, 5.2 us)
Sparse Core Ops, SparseCore 0:
  10.3 59.0 all-gather.2
  71.8 26.0 reduce-scatter.1
  178.3 88.4 all-gather.4

commit v8 on v7

--- a/solution.py
+++ b/solution.py
@@ -92,9 +92,8 @@
     gate_grad = (
         hidden_grad * up_vals * sigmoid * (1.0 + gate_vals * (1.0 - sigmoid)) * row_mask
     ).astype(jnp.bfloat16)
-    packed = jnp.stack([gate_grad, up_grad], axis=1)
-    packed = lax.all_gather(packed, DP, axis=0, tiled=True)
-    gate_g, up_g = packed[:, 0], packed[:, 1]
+    gate_g = lax.all_gather(gate_grad, DP, axis=0, tiled=True)
+    up_g = lax.all_gather(up_grad, DP, axis=0, tiled=True)
 
     down_terms = []
     gate_terms = []

time: 360 us -> 373 us (1.036)
  waiting for transfers between devices: 147 us -> 156 us
  matrix products: 65.7 us -> 70.8 us
    all_gather x1 -> x2, waiting for transfers between devices: 45.7 us -> 53.3 us  [the longest x1 36.9 us: shards(): gate_g = lax.all_gather(gate_grad, DP, axis=0, tiled=True)]
    dot_general x10, matrix products: 34 us -> 38.6 us  [contract_cols(): lax.dot_general(left_op, right_op, (((1,), (1,)), ((), ())), preferred_el...]
  transfers between devices with their start and end apart: 9 -> 10, of which waited for: 9 -> 10; matrix products, arithmetic and copies ran while one was open for 19% -> 21% of each run, Pallas kernels for 0% -> 0%
where the time goes in v8:
time: 373 us; the launch traced here: 372 us
  waiting for transfers between devices  156 us (42%)
  blocking collectives  75.3 us (20%)
  matrix products  70.8 us (19%)
  starting transfers between devices  29.8 us (8%)
  between operations  14.9 us (4%)
  other arithmetic  14.4 us (4%)
  local copies, waits for them, and re-layouts  11.4 us (3%)
    all_to_all x1, blocking collectives, shards(): lax.all_to_all(result, CHIPS, split_axis=0, concat_axis=0, tiled=True)  75.3 us
    dot_general x10, matrix products, contract_cols(): lax.dot_general(left_op, right_op, (((1,), (1,)), ((), ())), preferred_el...  38.6 us
    all_gather x1, waiting for transfers between devices, shards(): gate_g = lax.all_gather(gate_grad, DP, axis=0, tiled=True)  36.9 us
    dot_general x6, matrix products, contract_rows(): lax.dot_general(left_op, right_op, (((0,), (0,)), ((), ())), preferred_el...  32.1 us
    all_to_all x1, waiting for transfers between devices, shards(): lax.all_to_all(out_grad, DP, split_axis=1, concat_axis=0, tiled=True)  30.3 us
    reduce_scatter x1, waiting for transfers between devices, shards(): lax.psum_scatter(result.reshape(2, row_count // 2, ff), 'core', scatter_d...  28.4 us
    all_to_all x1, waiting for transfers between devices, shards(): lax.all_to_all(rows_in, DP, split_axis=1, concat_axis=0, tiled=True)  18.7 us
    all_gather x1, waiting for transfers between devices, shards(): up_g = lax.all_gather(up_grad, DP, axis=0, tiled=True)  16.4 us
  transfers between devices with their start and end apart: 10, of which 10 were waited for; matrix products, arithmetic and copies ran while one was open for 21% of the time, Pallas kernels for 0%

profile of v8, /device:TPU:3, one launch (start us, length us, event | category | flops | bytes accessed | tf_op | source)
XLA Modules:
  0.0 372.1 jit_solution(3017363771048931167)
XLA Ops:
  11.7 6.3 %all-to-all-start = ((bf16[128,16,384]{0,2,1:T(8,128)(2,1)}), bf16[128,16,384]{0,2,1:T(8,128)(2,1)S(1)}, u32[]{:S(2)}, u32[]{:S(2)}) async-start(bf16[128,16,384]{0,2,1:T(8,128)(2,1)} %bitcast.1), calls=%async_computation | async-start | bytes 3145728 | tf_op jit(solution)/shard_map/all_to_all | solution.py:63
  19.2 30.3 %all-to-all-done = bf16[128,16,384]{0,2,1:T(8,128)(2,1)S(1)} async-done(((bf16[128,16,384]{0,2,1:T(8,128)(2,1)}), bf16[128,16,384]{0,2,1:T(8,128)(2,1)S(1)}, u32[]{:S(2)}, u32[]{:S(2)}) %all-to-all-start) | async-done | bytes 1572896 | tf_op jit(solution)/shard_map/all_to_all | solution.py:63
  52.7 3.5 fusion.99
  56.1 6.7 %convolution_add_fusion = f32[2048,1536]{1,0:T(8,128)} fusion(f32[2048,1536]{1,0:T(8,128)S(1)} %fusion.99, bf16[2048,384]{1,0:T(8,128)(2,1)S(1)} %bitcast.82, bf16[2,1536,384]{2,1,0:T(8,128)(2,1)S(1)} %copy-done.1), kind=kOutput, calls=%fused_computation.1 | convolution fusion | flops 2419064832 | bytes 27918336 | tf_op jit(solution)/shard_map/dot_general | solution.py:42
  62.8 6.6 %all-gather.4.cloned.1.call-done = bf16[2048,1536]{1,0:T(8,128)(2,1)} async-done(((bf16[128,1536]{1,0:T(8,128)(2,1)}), bf16[2048,1536]{1,0:T(8,128)(2,1)}) %all-gather.4.cloned.1.call-update) | async-done | bytes 6291472 | tf_op jit(solution)/shard_map/all_gather | solution.py:76
  69.5 28.4 %reduce-scatter.2.cloned.1.call-done = f32[1,1024,1536]{2,1,0:T(8,128)} async-done(((f32[2,1024,1536]{2,1,0:T(8,128)}), f32[1,1024,1536]{2,1,0:T(8,128)}) %reduce-scatter.2.cloned.1.call-update) | async-done | bytes 6291472 | tf_op jit(solution)/shard_map/reduce_scatter | solution.py:83
  98.0 75.3 %all_to_all.53 = f32[8,128,1536]{2,1,0:T(8,128)} all-to-all(f32[8,128,1536]{2,1,0:T(8,128)} %bitcast.84), channel_id=1, replica_groups=mesh['x'=4,'ylo'=2,'core'=2,'z'=4,'yhi'=2] {'x','ylo'}, dimensions={0} | all-to-all | bytes 12582912 | tf_op jit(solution)/shard_map/all_to_all | solution.py:86
  181.8 6.0 %all-to-all-start.4 = ((bf16[128,16,384]{0,2,1:T(8,128)(2,1)}), bf16[128,16,384]{0,2,1:T(8,128)(2,1)S(1)}, u32[]{:S(2)}, u32[]{:S(2)}) async-start(bf16[128,16,384]{0,2,1:T(8,128)(2,1)} %bitcast.26), calls=%async_computation.5 | async-start | bytes 3145728 | tf_op jit(solution)/shard_map/all_to_all | solution.py:89
  187.9 6.6 %fusion.60 = bf16[1,1536,384]{2,1,0:T(8,128)(2,1)S(1)} fusion(bf16[2048,384]{1,0:T(8,128)(2,1)S(1)} %bitcast.88, bf16[2048,1536]{1,0:T(8,128)(2,1)} %all-gather.4.cloned.1.call-done, bf16[2048]{0:T(1024)(128)(2,1)S(1)} %broadcast_bitcast_fusion), kind=kOutput, calls=%fused_computation.50 | convolution fusion | flops 2419654656 | bytes 9048064 | tf_op jit(solution)/shard_map/dot_general | solution.py:36
  194.5 6.4 %fusion.63 = bf16[1,1536,384]{2,1,0:T(8,128)(2,1)S(1)} fusion(bf16[2048,384]{1,0:T(8,128)(2,1)S(1)} %bitcast.89, bf16[2048,1536]{1,0:T(8,128)(2,1)} %all-gather.4.cloned.1.call-done, bf16[2048]{0:T(1024)(128)(2,1)S(1)} %broadcast_bitcast_fusion.1), kind=kOutput, calls=%fused_computation.51 | convolution fusion | flops 2419654656 | bytes 9048064 | tf_op jit(solution)/shard_map/dot_general | solution.py:36
  202.6 18.7 %all-to-all-done.4 = bf16[128,16,384]{0,2,1:T(8,128)(2,1)S(1)} async-done(((bf16[128,16,384]{0,2,1:T(8,128)(2,1)}), bf16[128,16,384]{0,2,1:T(8,128)(2,1)S(1)}, u32[]{:S(2)}, u32[]{:S(2)}) %all-to-all-start.4) | async-done | bytes 1572896 | tf_op jit(solution)/shard_map/all_to_all | solution.py:89
  222.8 16.4 %all-gather.8.cloned.1.call-done = bf16[2048,1536]{1,0:T(8,128)(2,1)} async-done(((bf16[128,1536]{1,0:T(8,128)(2,1)}), bf16[2048,1536]{1,0:T(8,128)(2,1)}) %all-gather.8.cloned.1.call-update) | async-done | bytes 6291472 | tf_op jit(solution)/shard_map/all_gather | solution.py:96
  239.2 5.3 %fusion.18 = f32[1024,384]{1,0:T(8,128)} fusion(bf16[2048,1536]{1,0:T(8,128)(2,1)} %all-gather.8.cloned.1.call-done, bf16[1024]{0:T(1024)(128)(2,1)S(1)} %broadcast_bitcast_fusion.2, bf16[2,384,1536]{2,1,0:T(8,128)(2,1)} %param.15), kind=kOutput, calls=%fused_computation.20 | convolution fusion | flops 1209532416 | bytes 5900288 | tf_op jit(solution)/shard_map/dot_general | solution.py:42
  247.5 36.9 %all-gather.6.cloned.1.call-done = bf16[2048,1536]{1,0:T(8,128)(2,1)} async-done(((bf16[128,1536]{1,0:T(8,128)(2,1)}), bf16[2048,1536]{1,0:T(8,128)(2,1)}) %all-gather.6.cloned.1.call-update) | async-done | bytes 6291472 | tf_op jit(solution)/shard_map/all_gather | solution.py:95
  284.4 4.2 %fusion.24 = f32[1024,384]{1,0:T(8,128)S(1)} fusion(bf16[2048,1536]{1,0:T(8,128)(2,1)} %all-gather.6.cloned.1.call-done, bf16[1024]{0:T(1024)(128)(2,1)S(1)} %broadcast_bitcast_fusion.3, bf16[2,384,1536]{2,1,0:T(8,128)(2,1)} %param.14), kind=kOutput, calls=%fused_computation.26 | convolution fusion | flops 1209532416 | bytes 5900288 | tf_op jit(solution)/shard_map/dot_general | solution.py:42
  292.4 6.6 %all-to-all-start.3 = ((f32[8,128,384]{2,1,0:T(8,128)}), f32[8,128,384]{2,1,0:T(8,128)S(1)}, u32[]{:S(2)}, u32[]{:S(2)}) async-start(f32[8,128,384]{2,1,0:T(8,128)} %bitcast.22), calls=%async_computation.4 | async-start | bytes 3145728 | tf_op jit(solution)/shard_map/all_to_all | solution.py:125
  299.0 4.2 %fusion.30 = f32[1024,384]{1,0:T(8,128)S(1)} fusion(bf16[2048,1536]{1,0:T(8,128)(2,1)} %all-gather.8.cloned.1.call-done, bf16[1024]{0:T(1024)(128)(2,1)S(1)} %broadcast_bitcast_fusion.5, bf16[2,384,1536]{2,1,0:T(8,128)(2,1)} %param.15), kind=kOutput, calls=%fused_computation.32 | convolution fusion | flops 1209532416 | bytes 5900288 | tf_op jit(solution)/shard_map/dot_general | solution.py:42
  303.2 3.9 %fusion.32 = f32[1024,384]{1,0:T(8,128)S(1)} fusion(bf16[2048,1536]{1,0:T(8,128)(2,1)} %all-gather.6.cloned.1.call-done, bf16[1024]{0:T(1024)(128)(2,1)S(1)} %broadcast_bitcast_fusion.5, bf16[2,384,1536]{2,1,0:T(8,128)(2,1)S(1)} %copy-done.14), kind=kOutput, calls=%fused_computation.34 | convolution fusion | flops 1209532416 | bytes 5900288 | tf_op jit(solution)/shard_map/dot_general | solution.py:42
  321.3 4.9 %all-to-all-start.2 = ((f32[8,128,384]{2,1,0:T(8,128)}), f32[8,128,384]{2,1,0:T(8,128)S(1)}, u32[]{:S(2)}, u32[]{:S(2)}) async-start(f32[8,128,384]{2,1,0:T(8,128)} %bitcast.94), calls=%async_computation.3 | async-start | bytes 3145728 | tf_op jit(solution)/shard_map/all_to_all | solution.py:125
  326.3 7.1 %fusion.75 = bf16[1,384,1536]{2,1,0:T(8,128)(2,1)} fusion(bf16[2048,384]{1,0:T(8,128)(2,1)} %bitcast.90, bf16[2048,1536]{1,0:T(8,128)(2,1)} %all-gather.6.cloned.1.call-done, bf16[2048]{0:T(1024)(128)(2,1)S(1)} %broadcast_bitcast_fusion.1), kind=kOutput, calls=%fused_computation.55 | convolution fusion | flops 2419654656 | bytes 9048064 | tf_op jit(solution)/shard_map/dot_general | solution.py:36
  333.4 6.6 %fusion.72 = bf16[1,384,1536]{2,1,0:T(8,128)(2,1)} fusion(bf16[2048,384]{1,0:T(8,128)(2,1)S(1)} %bitcast.93, bf16[2048,1536]{1,0:T(8,128)(2,1)} %all-gather.6.cloned.1.call-done, bf16[2048]{0:T(1024)(128)(2,1)S(1)} %broadcast_bitcast_fusion), kind=kOutput, calls=%fused_computation.54 | convolution fusion | flops 2419654656 | bytes 9048064 | tf_op jit(solution)/shard_map/dot_general | solution.py:36
  340.1 7.9 %all-to-all-done.2 = f32[8,128,384]{2,1,0:T(8,128)S(1)} async-done(((f32[8,128,384]{2,1,0:T(8,128)}), f32[8,128,384]{2,1,0:T(8,128)S(1)}, u32[]{:S(2)}, u32[]{:S(2)}) %all-to-all-start.2) | async-done | bytes 1572896 | tf_op jit(solution)/shard_map/all_to_all | solution.py:125
  348.2 3.5 collective-permute-start
  356.9 5.3 %collective-permute-done = bf16[128,384]{1,0:T(8,128)(2,1)S(1)} collective-permute-done((bf16[128,384]{1,0:T(8,128)(2,1)S(1)}, bf16[128,384]{1,0:T(8,128)(2,1)S(1)}, u32[]{:S(2)}, u32[]{:S(2)}) %collective-permute-start) | collective-permute-done | bytes 98336 | tf_op jit(solution)/shard_map/ppermute | solution.py:135
  (95 shorter events, 49.5 us)
Async XLA Ops:
  7.2 62.3 %all-gather.4.cloned.1.call-start = ((), (), s32[]{:S(2)}) async-start(), calls=%async_computation.6 | async-start | bytes 6684672 | tf_op jit(solution)/shard_map/all_gather | solution.py:76
  11.7 6.4 %copy-start.8 = (s32[16]{0:T(128)S(1)}, s32[16]{0:T(128)}, u32[]{:S(2)}) copy-start(s32[16]{0:T(128)} %constant.55) | copy-start | bytes 196
  11.7 6.4 %copy-start = (s32[16]{0:T(128)S(1)}, s32[16]{0:T(128)}, u32[]{:S(2)}) copy-start(s32[16]{0:T(128)} %param.18) | copy-start | bytes 196
  11.7 37.8 %all-to-all-start = ((bf16[128,16,384]{0,2,1:T(8,128)(2,1)}), bf16[128,16,384]{0,2,1:T(8,128)(2,1)S(1)}, u32[]{:S(2)}, u32[]{:S(2)}) async-start(bf16[128,16,384]{0,2,1:T(8,128)(2,1)} %bitcast.1), calls=%async_computation | async-start | bytes 3145728 | tf_op jit(solution)/shard_map/all_to_all | solution.py:63
  18.0 79.9 %reduce-scatter.2.cloned.1.call-start = ((), (), s32[]{:S(2)}) async-start(), calls=%async_computation.7 | async-start | bytes 18874368 | tf_op jit(solution)/shard_map/reduce_scatter | solution.py:83
  69.5 169.8 %all-gather.8.cloned.1.call-start = ((), (), s32[]{:S(2)}) async-start(), calls=%async_computation.9 | async-start | bytes 6684672 | tf_op jit(solution)/shard_map/all_gather | solution.py:96
  178.1 106.3 %all-gather.6.cloned.1.call-start = ((), (), s32[]{:S(2)}) async-start(), calls=%async_computation.8 | async-start | bytes 6684672 | tf_op jit(solution)/shard_map/all_gather | solution.py:95
  181.8 39.4 %all-to-all-start.4 = ((bf16[128,16,384]{0,2,1:T(8,128)(2,1)}), bf16[128,16,384]{0,2,1:T(8,128)(2,1)S(1)}, u32[]{:S(2)}, u32[]{:S(2)}) async-start(bf16[128,16,384]{0,2,1:T(8,128)(2,1)} %bitcast.26), calls=%async_computation.5 | async-start | bytes 3145728 | tf_op jit(solution)/shard_map/all_to_all | solution.py:89
  222.8 21.8 %copy-start.11 = (bf16[2,384,1536]{2,1,0:T(8,128)(2,1)S(1)}, bf16[2,384,1536]{2,1,0:T(8,128)(2,1)}, u32[]{:S(2)}) copy-start(bf16[2,384,1536]{2,1,0:T(8,128)(2,1)} %param.15) | copy-start | bytes 7077892
  239.2 5.3 %copy-start.10 = (bf16[2048,1536]{1,0:T(8,128)(2,1)S(1)}, bf16[2048,1536]{1,0:T(8,128)(2,1)}, u32[]{:S(2)}) copy-start(bf16[2048,1536]{1,0:T(8,128)(2,1)} %all-gather.8.cloned.1.call-done) | copy-start | bytes 18874372
  247.5 41.1 %copy-start.13 = (bf16[2,384,1536]{2,1,0:T(8,128)(2,1)S(1)}, bf16[2,384,1536]{2,1,0:T(8,128)(2,1)}, u32[]{:S(2)}) copy-start(bf16[2,384,1536]{2,1,0:T(8,128)(2,1)} %param.14) | copy-start | bytes 7077892
  284.4 4.2 %copy-start.9 = (bf16[2048,1536]{1,0:T(8,128)(2,1)S(1)}, bf16[2048,1536]{1,0:T(8,128)(2,1)}, u32[]{:S(2)}) copy-start(bf16[2048,1536]{1,0:T(8,128)(2,1)} %all-gather.6.cloned.1.call-done) | copy-start | bytes 18874372
  284.4 4.5 %copy-start.15 = (f32[1024,384]{1,0:T(8,128)S(1)}, f32[1024,384]{1,0:T(8,128)}, u32[]{:S(2)}) copy-start(f32[1024,384]{1,0:T(8,128)} %fusion.18) | copy-start | bytes 4718596
  284.4 5.0 %copy-start.16 = (f32[1024,384]{1,0:T(8,128)S(1)}, f32[1024,384]{1,0:T(8,128)}, u32[]{:S(2)}) copy-start(f32[1024,384]{1,0:T(8,128)} %fusion.22) | copy-start | bytes 4718596
  292.4 28.9 %all-to-all-start.3 = ((f32[8,128,384]{2,1,0:T(8,128)}), f32[8,128,384]{2,1,0:T(8,128)S(1)}, u32[]{:S(2)}, u32[]{:S(2)}) async-start(f32[8,128,384]{2,1,0:T(8,128)} %bitcast.22), calls=%async_computation.4 | async-start | bytes 3145728 | tf_op jit(solution)/shard_map/all_to_all | solution.py:125
  299.0 4.2 %copy-start.14 = (bf16[2,384,1536]{2,1,0:T(8,128)(2,1)S(1)}, bf16[2,384,1536]{2,1,0:T(8,128)(2,1)}, u32[]{:S(2)}) copy-start(bf16[2,384,1536]{2,1,0:T(8,128)(2,1)} %param.14) | copy-start | bytes 7077892
  299.0 8.1 %slice-start.2 = ((s8[6291456]{0:T(1024)(128)(4,1)}), s8[4194304]{0:T(1024)(128)(4,1)S(1)}, s32[]{:S(2)}) async-start(s8[6291456]{0:T(1024)(128)(4,1)} %bitcast.99), calls=%async_computation.12 | async-start | bytes 8388608
  303.2 3.9 %copy-start.3 = (bf16[16,128,384]{2,1,0:T(8,128)(2,1)S(1)}, bf16[16,128,384]{2,1,0:T(8,128)(2,1)}, u32[]{:S(2)}) copy-start(bf16[16,128,384]{2,1,0:T(8,128)(2,1)} %copy.23) | copy-start | bytes 4718596
  309.9 4.4 %copy-start.12 = (bf16[2,384,1536]{2,1,0:T(8,128)(2,1)S(1)}, bf16[2,384,1536]{2,1,0:T(8,128)(2,1)}, u32[]{:S(2)}) copy-start(bf16[2,384,1536]{2,1,0:T(8,128)(2,1)} %param.15) | copy-start | bytes 7077892
  321.3 26.7 %all-to-all-start.2 = ((f32[8,128,384]{2,1,0:T(8,128)}), f32[8,128,384]{2,1,0:T(8,128)S(1)}, u32[]{:S(2)}, u32[]{:S(2)}) async-start(f32[8,128,384]{2,1,0:T(8,128)} %bitcast.94), calls=%async_computation.3 | async-start | bytes 3145728 | tf_op jit(solution)/shard_map/all_to_all | solution.py:125
  326.3 7.1 %copy-start.4 = (bf16[16,128,384]{2,1,0:T(8,128)(2,1)S(1)}, bf16[16,128,384]{2,1,0:T(8,128)(2,1)}, u32[]{:S(2)}) copy-start(bf16[16,128,384]{2,1,0:T(8,128)(2,1)} %copy.23) | copy-start | bytes 4718596
  340.0 13.9 %copy-start.7 = (bf16[1,384,1536]{2,1,0:T(8,128)(2,1)S(1)}, bf16[1,384,1536]{2,1,0:T(8,128)(2,1)}, u32[]{:S(2)}) copy-start(bf16[1,384,1536]{2,1,0:T(8,128)(2,1)} %fusion.75) | copy-start | bytes 3538948
  348.2 14.0 %collective-permute-start = (bf16[128,384]{1,0:T(8,128)(2,1)S(1)}, bf16[128,384]{1,0:T(8,128)(2,1)S(1)}, u32[]{:S(2)}, u32[]{:S(2)}) collective-permute-start(bf16[128,384]{1,0:T(8,128)(2,1)S(1)} %get-tuple-element.18), channel_id=1, source_target_pairs={{0,0},{1,8},{2,16},{3,24},{4,32},{5,40},{6,48},{7,56},{8,64},{9,72... | collective-permute-start | bytes 294920 | tf_op jit(solution)/shard_map/ppermute | solution.py:135
  351.7 13.1 %collective-permute-start.1 = (bf16[128,384]{1,0:T(8,128)(2,1)S(1)}, bf16[128,384]{1,0:T(8,128)(2,1)S(1)}, u32[]{:S(2)}, u32[]{:S(2)}) collective-permute-start(bf16[128,384]{1,0:T(8,128)(2,1)S(1)} %get-tuple-element.19), channel_id=1, source_target_pairs={{0,64},{1,72},{2,80},{3,88},{4,96},{5,104},{6,112},{7,120},{8,0},{... | collective-permute-start | bytes 294920 | tf_op jit(solution)/shard_map/ppermute | solution.py:135
  (7 other events, 21.2 us)
Sparse Core Ops, SparseCore 0:
  10.3 59.0 all-gather.3
  71.8 26.0 reduce-scatter.1
  178.2 60.9 all-gather.7
  240.8 43.5 all-gather.5

commit v9 on v7

--- a/solution.py
+++ b/solution.py
@@ -100,12 +100,10 @@
     gate_terms = []
     up_terms = []
     for which in range(expert_count):
-        down_terms.append(contract_rows(hid_g * masks[which], dy_cols))
         gate_masked = gate_g * masks[which]
         up_masked = up_g * masks[which]
         gate_terms.append(contract_rows(x_cols, gate_masked))
         up_terms.append(contract_rows(x_cols, up_masked))
-    down_total = jnp.stack(down_terms, 0)
     gate_total = jnp.stack(gate_terms, 0)
     up_total = jnp.stack(up_terms, 0)
 
@@ -128,6 +126,10 @@
         )
         summed.append(jnp.sum(pieces, axis=0))
     summed = jnp.stack(summed, 0)
+    hid_g, summed = lax.optimization_barrier((hid_g, summed))
+    for which in range(expert_count):
+        down_terms.append(contract_rows(hid_g * masks[which], dy_cols))
+    down_total = jnp.stack(down_terms, 0)
     core = lax.axis_index("core")
     low = lax.axis_index("x") < 2
     got = []

time: 360 us -> 377 us (1.047)
  waiting for transfers between devices: 147 us -> 163 us
    all_to_all x1, waiting for transfers between devices: 18.7 us -> 31.9 us  [shards(): lax.all_to_all(rows_in, DP, split_axis=1, concat_axis=0, tiled=True)]
  transfers between devices with their start and end apart: 9 -> 9, of which waited for: 9 -> 8; matrix products, arithmetic and copies ran while one was open for 19% -> 14% of each run, Pallas kernels for 0% -> 0%
where the time goes in v9:
time: 377 us; the launch traced here: 376 us
  waiting for transfers between devices  163 us (43%)
  blocking collectives  75.3 us (20%)
  matrix products  64.2 us (17%)
  starting transfers between devices  32 us (8%)
  other arithmetic  14.9 us (4%)
  between operations  14.9 us (4%)
  local copies, waits for them, and re-layouts  11.6 us (3%)
    all_to_all x1, blocking collectives, shards(): lax.all_to_all(result, CHIPS, split_axis=0, concat_axis=0, tiled=True)  75.3 us
    all_gather x1, waiting for transfers between devices, shards(): packed = lax.all_gather(packed, DP, axis=0, tiled=True)  47 us
    dot_general x10, matrix products, contract_cols(): lax.dot_general(left_op, right_op, (((1,), (1,)), ((), ())), preferred_el...  34 us
    all_to_all x1, waiting for transfers between devices, shards(): lax.all_to_all(rows_in, DP, split_axis=1, concat_axis=0, tiled=True)  31.9 us
    all_to_all x1, waiting for transfers between devices, shards(): lax.all_to_all(out_grad, DP, split_axis=1, concat_axis=0, tiled=True)  30.3 us
    dot_general x6, matrix products, contract_rows(): lax.dot_general(left_op, right_op, (((0,), (0,)), ((), ())), preferred_el...  30.2 us
    reduce_scatter x1, waiting for transfers between devices, shards(): lax.psum_scatter(result.reshape(2, row_count // 2, ff), 'core', scatter_d...  28.4 us
    all_to_all x2, starting transfers between devices, shards(): lax.all_to_all(partial_rows.reshape(N_TP, rows_dev, width), TP, split_axi...  13.4 us
  transfers between devices with their start and end apart: 9, of which 8 were waited for; matrix products, arithmetic and copies ran while one was open for 14% of the time, Pallas kernels for 0%

profile of v9, /device:TPU:3, one launch (start us, length us, event | category | flops | bytes accessed | tf_op | source)
XLA Modules:
  0.0 376.3 jit_solution(1995785973323523957)
XLA Ops:
  11.7 6.3 %all-to-all-start = ((bf16[128,16,384]{0,2,1:T(8,128)(2,1)}), bf16[128,16,384]{0,2,1:T(8,128)(2,1)S(1)}, u32[]{:S(2)}, u32[]{:S(2)}) async-start(bf16[128,16,384]{0,2,1:T(8,128)(2,1)} %bitcast.1), calls=%async_computation | async-start | bytes 3145728 | tf_op jit(solution)/shard_map/all_to_all | solution.py:63
  19.2 30.3 %all-to-all-done = bf16[128,16,384]{0,2,1:T(8,128)(2,1)S(1)} async-done(((bf16[128,16,384]{0,2,1:T(8,128)(2,1)}), bf16[128,16,384]{0,2,1:T(8,128)(2,1)S(1)}, u32[]{:S(2)}, u32[]{:S(2)}) %all-to-all-start) | async-done | bytes 1572896 | tf_op jit(solution)/shard_map/all_to_all | solution.py:63
  53.5 3.5 fusion.115
  56.9 6.7 %convolution_add_fusion = f32[2048,1536]{1,0:T(8,128)} fusion(f32[2048,1536]{1,0:T(8,128)S(1)} %fusion.115, bf16[2048,384]{1,0:T(8,128)(2,1)S(1)} %bitcast.142, bf16[2,1536,384]{2,1,0:T(8,128)(2,1)S(1)} %copy-done.3), kind=kOutput, calls=%fused_computation.1 | convolution fusion | flops 2419064832 | bytes 27918336 | tf_op jit(solution)/shard_map/dot_general | solution.py:42
  63.6 5.8 %all-gather.3.cloned.1.call-done = bf16[2048,1536]{1,0:T(8,128)(2,1)} async-done(((bf16[128,1536]{1,0:T(8,128)(2,1)}), bf16[2048,1536]{1,0:T(8,128)(2,1)}) %all-gather.3.cloned.1.call-update) | async-done | bytes 6291472 | tf_op jit(solution)/shard_map/all_gather | solution.py:76
  69.5 28.4 %reduce-scatter.2.cloned.1.call-done = f32[1,1024,1536]{2,1,0:T(8,128)} async-done(((f32[2,1024,1536]{2,1,0:T(8,128)}), f32[1,1024,1536]{2,1,0:T(8,128)}) %reduce-scatter.2.cloned.1.call-update) | async-done | bytes 6291472 | tf_op jit(solution)/shard_map/reduce_scatter | solution.py:83
  98.0 75.3 %all_to_all.53 = f32[8,128,1536]{2,1,0:T(8,128)} all-to-all(f32[8,128,1536]{2,1,0:T(8,128)} %bitcast.144), channel_id=1, replica_groups=mesh['x'=4,'ylo'=2,'core'=2,'z'=4,'yhi'=2] {'x','ylo'}, dimensions={0} | all-to-all | bytes 12582912 | tf_op jit(solution)/shard_map/all_to_all | solution.py:86
  179.8 6.1 %all-to-all-start.4 = ((bf16[128,16,384]{0,2,1:T(8,128)(2,1)}), bf16[128,16,384]{0,2,1:T(8,128)(2,1)S(1)}, u32[]{:S(2)}, u32[]{:S(2)}) async-start(bf16[128,16,384]{0,2,1:T(8,128)(2,1)} %bitcast.36), calls=%async_computation.5 | async-start | bytes 3145728 | tf_op jit(solution)/shard_map/all_to_all | solution.py:89
  186.4 31.9 %all-to-all-done.4 = bf16[128,16,384]{0,2,1:T(8,128)(2,1)S(1)} async-done(((bf16[128,16,384]{0,2,1:T(8,128)(2,1)}), bf16[128,16,384]{0,2,1:T(8,128)(2,1)S(1)}, u32[]{:S(2)}, u32[]{:S(2)}) %all-to-all-start.4) | async-done | bytes 1572896 | tf_op jit(solution)/shard_map/all_to_all | solution.py:89
  219.2 47.0 %all-gather.5.cloned.1.call-done = bf16[2048,2,1536]{2,0,1:T(8,128)(2,1)} async-done(((bf16[128,2,1536]{2,0,1:T(8,128)(2,1)}), bf16[2048,2,1536]{2,0,1:T(8,128)(2,1)}) %all-gather.5.cloned.1.call-update) | async-done | bytes 12582928 | tf_op jit(solution)/shard_map/all_gather | solution.py:96
  266.2 4.2 %fusion.28 = f32[1024,384]{1,0:T(8,128)S(1)} fusion(bf16[2048,2,1536]{2,0,1:T(8,128)(2,1)} %all-gather.5.cloned.1.call-done, bf16[1024]{0:T(1024)(128)(2,1)S(1)} %broadcast_bitcast_fusion.4, bf16[2,384,1536]{2,1,0:T(8,128)(2,1)} %param.15), kind=kOutput, calls=%fused_computation.30 | convolution fusion | flops 1209532416 | bytes 5900288 | tf_op jit(solution)/shard_map/dot_general | solution.py:42
  279.4 6.7 %all-to-all-start.2 = ((f32[8,128,384]{2,1,0:T(8,128)}), f32[8,128,384]{2,1,0:T(8,128)S(1)}, u32[]{:S(2)}, u32[]{:S(2)}) async-start(f32[8,128,384]{2,1,0:T(8,128)} %bitcast.155), calls=%async_computation.3 | async-start | bytes 3145728 | tf_op jit(solution)/shard_map/all_to_all | solution.py:124
  286.1 4.2 %fusion.24 = f32[1024,384]{1,0:T(8,128)S(1)} fusion(bf16[2048,2,1536]{2,0,1:T(8,128)(2,1)} %all-gather.5.cloned.1.call-done, bf16[1024]{0:T(1024)(128)(2,1)S(1)} %broadcast_bitcast_fusion.3, bf16[2,384,1536]{2,1,0:T(8,128)(2,1)} %param.15), kind=kOutput, calls=%fused_computation.26 | convolution fusion | flops 1209532416 | bytes 5900288 | tf_op jit(solution)/shard_map/dot_general | solution.py:42
  290.4 3.9 %fusion.26 = f32[1024,384]{1,0:T(8,128)S(1)} fusion(bf16[2048,2,1536]{2,0,1:T(8,128)(2,1)} %all-gather.5.cloned.1.call-done, bf16[1024]{0:T(1024)(128)(2,1)S(1)} %broadcast_bitcast_fusion.3, bf16[2,384,1536]{2,1,0:T(8,128)(2,1)S(1)} %copy-done.16), kind=kOutput, calls=%fused_computation.28 | convolution fusion | flops 1209532416 | bytes 5900288 | tf_op jit(solution)/shard_map/dot_general | solution.py:42
  294.3 3.8 %fusion.79 = bf16[1,384,1536]{2,1,0:T(8,128)(2,1)} fusion(bf16[2048,384]{1,0:T(8,128)(2,1)S(1)} %bitcast.150, bf16[2048,2,1536]{2,0,1:T(8,128)(2,1)S(1)} %bitcast.159, bf16[2048]{0:T(1024)(128)(2,1)S(1)} %broadcast_bitcast_fusion.1), kind=kOutput, calls=%fused_computation.67 | convolution fusion | flops 2419654656 | bytes 9048064 | tf_op jit(solution)/shard_map/dot_general | solution.py:36
  298.1 3.8 %fusion.85 = bf16[1,384,1536]{2,1,0:T(8,128)(2,1)} fusion(bf16[2048,384]{1,0:T(8,128)(2,1)S(1)} %bitcast.151, bf16[2048,2,1536]{2,0,1:T(8,128)(2,1)S(1)} %bitcast.159, bf16[2048]{0:T(1024)(128)(2,1)S(1)} %broadcast_bitcast_fusion.1), kind=kOutput, calls=%fused_computation.69 | convolution fusion | flops 2419654656 | bytes 9048064 | tf_op jit(solution)/shard_map/dot_general | solution.py:36
  306.8 3.8 %fusion.76 = bf16[1,384,1536]{2,1,0:T(8,128)(2,1)} fusion(bf16[2048,384]{1,0:T(8,128)(2,1)S(1)} %bitcast.152, bf16[2048,2,1536]{2,0,1:T(8,128)(2,1)S(1)} %bitcast.159, bf16[2048]{0:T(1024)(128)(2,1)S(1)} %broadcast_bitcast_fusion), kind=kOutput, calls=%fused_computation.66 | convolution fusion | flops 2419654656 | bytes 9048064 | tf_op jit(solution)/shard_map/dot_general | solution.py:36
  310.6 6.7 %all-to-all-start.3 = ((f32[8,128,384]{2,1,0:T(8,128)}), f32[8,128,384]{2,1,0:T(8,128)S(1)}, u32[]{:S(2)}, u32[]{:S(2)}) async-start(f32[8,128,384]{2,1,0:T(8,128)} %bitcast.154), calls=%async_computation.4 | async-start | bytes 3145728 | tf_op jit(solution)/shard_map/all_to_all | solution.py:124
  320.6 5.6 %fusion.82 = bf16[1,384,1536]{2,1,0:T(8,128)(2,1)S(1)} fusion(bf16[2048,384]{1,0:T(8,128)(2,1)S(1)} %bitcast.153, bf16[2048,2,1536]{2,0,1:T(8,128)(2,1)} %all-gather.5.cloned.1.call-done, bf16[2048]{0:T(1024)(128)(2,1)S(1)} %broadcast_bitcast_fusion), kind=kOutput, calls=%fused_computation.68 | convolution fusion | flops 2419654656 | bytes 9048064 | tf_op jit(solution)/shard_map/dot_general | solution.py:36
  327.9 11.1 %all-to-all-done.3 = f32[8,128,384]{2,1,0:T(8,128)S(1)} async-done(((f32[8,128,384]{2,1,0:T(8,128)}), f32[8,128,384]{2,1,0:T(8,128)S(1)}, u32[]{:S(2)}, u32[]{:S(2)}) %all-to-all-start.3) | async-done | bytes 1572896 | tf_op jit(solution)/shard_map/all_to_all | solution.py:124
  339.1 6.9 %fusion.88 = bf16[1,1536,384]{2,1,0:T(8,128)(2,1)S(1)} fusion(bf16[2048,384]{1,0:T(8,128)(2,1)} %bitcast.148, bf16[2048,1536]{1,0:T(8,128)(2,1)} %all-gather.3.cloned.1.call-done, bf16[2048]{0:T(1024)(128)(2,1)S(1)} %broadcast_bitcast_fusion), kind=kOutput, calls=%fused_computation.70 | convolution fusion | flops 2419654656 | bytes 9048064 | tf_op jit(solution)/shard_map/dot_general | solution.py:36
  346.0 6.4 %fusion.91 = bf16[1,1536,384]{2,1,0:T(8,128)(2,1)S(1)} fusion(bf16[2048,384]{1,0:T(8,128)(2,1)S(1)} %bitcast.149, bf16[2048,1536]{1,0:T(8,128)(2,1)} %all-gather.3.cloned.1.call-done, bf16[2048]{0:T(1024)(128)(2,1)S(1)} %broadcast_bitcast_fusion.1), kind=kOutput, calls=%fused_computation.71 | convolution fusion | flops 2419654656 | bytes 9048064 | tf_op jit(solution)/shard_map/dot_general | solution.py:36
  352.4 3.6 collective-permute-start
  360.3 5.8 %collective-permute-done = bf16[128,384]{1,0:T(8,128)(2,1)S(1)} collective-permute-done((bf16[128,384]{1,0:T(8,128)(2,1)S(1)}, bf16[128,384]{1,0:T(8,128)(2,1)S(1)}, u32[]{:S(2)}, u32[]{:S(2)}) %collective-permute-start) | collective-permute-done | bytes 98336 | tf_op jit(solution)/shard_map/ppermute | solution.py:138
  (91 shorter events, 43.8 us)
Async XLA Ops:
  7.2 62.3 %all-gather.3.cloned.1.call-start = ((), (), s32[]{:S(2)}) async-start(), calls=%async_computation.6 | async-start | bytes 6684672 | tf_op jit(solution)/shard_map/all_gather | solution.py:76
  11.7 6.4 %copy-start.11 = (s32[16]{0:T(128)S(1)}, s32[16]{0:T(128)}, u32[]{:S(2)}) copy-start(s32[16]{0:T(128)} %constant.55) | copy-start | bytes 196
  11.7 6.4 %copy-start = (s32[16]{0:T(128)S(1)}, s32[16]{0:T(128)}, u32[]{:S(2)}) copy-start(s32[16]{0:T(128)} %param.18) | copy-start | bytes 196
  11.7 37.8 %all-to-all-start = ((bf16[128,16,384]{0,2,1:T(8,128)(2,1)}), bf16[128,16,384]{0,2,1:T(8,128)(2,1)S(1)}, u32[]{:S(2)}, u32[]{:S(2)}) async-start(bf16[128,16,384]{0,2,1:T(8,128)(2,1)} %bitcast.1), calls=%async_computation | async-start | bytes 3145728 | tf_op jit(solution)/shard_map/all_to_all | solution.py:63
  18.0 79.9 %reduce-scatter.2.cloned.1.call-start = ((), (), s32[]{:S(2)}) async-start(), calls=%async_computation.7 | async-start | bytes 18874368 | tf_op jit(solution)/shard_map/reduce_scatter | solution.py:83
  69.5 196.7 %all-gather.5.cloned.1.call-start = ((), (), s32[]{:S(2)}) async-start(), calls=%async_computation.8 | async-start | bytes 13369344 | tf_op jit(solution)/shard_map/all_gather | solution.py:96
  173.2 3.4 copy-start.8
  173.2 3.4 copy-start.9
  179.8 38.5 %all-to-all-start.4 = ((bf16[128,16,384]{0,2,1:T(8,128)(2,1)}), bf16[128,16,384]{0,2,1:T(8,128)(2,1)S(1)}, u32[]{:S(2)}, u32[]{:S(2)}) async-start(bf16[128,16,384]{0,2,1:T(8,128)(2,1)} %bitcast.36), calls=%async_computation.5 | async-start | bytes 3145728 | tf_op jit(solution)/shard_map/all_to_all | solution.py:89
  219.2 87.6 %copy-start.6 = (bf16[16,128,384]{2,1,0:T(8,128)(2,1)}, bf16[16,128,384]{2,1,0:T(8,128)(2,1)S(1)}, u32[]{:S(2)}) copy-start(bf16[16,128,384]{2,1,0:T(8,128)(2,1)S(1)} %copy.23) | copy-start | bytes 4718596
  266.1 5.9 %copy-start.12 = (bf16[2048,2,1536]{2,0,1:T(8,128)(2,1)S(1)}, bf16[2048,2,1536]{2,0,1:T(8,128)(2,1)}, u32[]{:S(2)}) copy-start(bf16[2048,2,1536]{2,0,1:T(8,128)(2,1)} %all-gather.5.cloned.1.call-done) | copy-start | bytes 37748740
  266.2 6.5 %copy-start.13 = (bf16[2,384,1536]{2,1,0:T(8,128)(2,1)S(1)}, bf16[2,384,1536]{2,1,0:T(8,128)(2,1)}, u32[]{:S(2)}) copy-start(bf16[2,384,1536]{2,1,0:T(8,128)(2,1)} %param.15) | copy-start | bytes 7077892
  279.4 31.2 %all-to-all-start.2 = ((f32[8,128,384]{2,1,0:T(8,128)}), f32[8,128,384]{2,1,0:T(8,128)S(1)}, u32[]{:S(2)}, u32[]{:S(2)}) async-start(f32[8,128,384]{2,1,0:T(8,128)} %bitcast.155), calls=%async_computation.3 | async-start | bytes 3145728 | tf_op jit(solution)/shard_map/all_to_all | solution.py:124
  286.1 4.2 %copy-start.16 = (bf16[2,384,1536]{2,1,0:T(8,128)(2,1)S(1)}, bf16[2,384,1536]{2,1,0:T(8,128)(2,1)}, u32[]{:S(2)}) copy-start(bf16[2,384,1536]{2,1,0:T(8,128)(2,1)} %param.14) | copy-start | bytes 7077892
  286.1 8.1 %slice-start = ((s8[12582912]{0:T(1024)(128)(4,1)}), s8[4194304]{0:T(1024)(128)(4,1)S(1)}, s32[]{:S(2)}) async-start(s8[12582912]{0:T(1024)(128)(4,1)} %bitcast.158), calls=%async_computation.9 | async-start | bytes 8388608
  286.1 8.1 %slice-start.1 = ((s8[12582912]{0:T(1024)(128)(4,1)}), s8[4194304]{0:T(1024)(128)(4,1)S(1)}, s32[]{:S(2)}) async-start(s8[12582912]{0:T(1024)(128)(4,1)} %bitcast.158), calls=%async_computation.10 | async-start | bytes 8388608
  290.4 3.9 %slice-start.2 = ((s8[12582912]{0:T(1024)(128)(4,1)}), s8[4194304]{0:T(1024)(128)(4,1)S(1)}, s32[]{:S(2)}) async-start(s8[12582912]{0:T(1024)(128)(4,1)} %bitcast.158), calls=%async_computation.11 | async-start | bytes 8388608
  298.1 3.8 %copy-start.14 = (bf16[2,384,1536]{2,1,0:T(8,128)(2,1)S(1)}, bf16[2,384,1536]{2,1,0:T(8,128)(2,1)}, u32[]{:S(2)}) copy-start(bf16[2,384,1536]{2,1,0:T(8,128)(2,1)} %param.15) | copy-start | bytes 7077892
  310.6 28.4 %all-to-all-start.3 = ((f32[8,128,384]{2,1,0:T(8,128)}), f32[8,128,384]{2,1,0:T(8,128)S(1)}, u32[]{:S(2)}, u32[]{:S(2)}) async-start(f32[8,128,384]{2,1,0:T(8,128)} %bitcast.154), calls=%async_computation.4 | async-start | bytes 3145728 | tf_op jit(solution)/shard_map/all_to_all | solution.py:124
  317.2 3.4 copy-start.7
  320.6 5.6 %copy-start.10 = (bf16[1,384,1536]{2,1,0:T(8,128)(2,1)S(1)}, bf16[1,384,1536]{2,1,0:T(8,128)(2,1)}, u32[]{:S(2)}) copy-start(bf16[1,384,1536]{2,1,0:T(8,128)(2,1)} %fusion.85) | copy-start | bytes 3538948
  339.1 6.9 %copy-start.2 = (bf16[16,128,384]{2,1,0:T(8,128)(2,1)S(1)}, bf16[16,128,384]{2,1,0:T(8,128)(2,1)}, u32[]{:S(2)}) copy-start(bf16[16,128,384]{2,1,0:T(8,128)(2,1)} %copy-done.1) | copy-start | bytes 4718596
  352.4 13.7 %collective-permute-start = (bf16[128,384]{1,0:T(8,128)(2,1)S(1)}, bf16[128,384]{1,0:T(8,128)(2,1)S(1)}, u32[]{:S(2)}, u32[]{:S(2)}) collective-permute-start(bf16[128,384]{1,0:T(8,128)(2,1)S(1)} %get-tuple-element.22), channel_id=1, source_target_pairs={{0,0},{1,8},{2,16},{3,24},{4,32},{5,40},{6,48},{7,56},{8,64},{9,72... | collective-permute-start | bytes 294920 | tf_op jit(solution)/shard_map/ppermute | solution.py:138
  356.0 13.0 %collective-permute-start.1 = (bf16[128,384]{1,0:T(8,128)(2,1)S(1)}, bf16[128,384]{1,0:T(8,128)(2,1)S(1)}, u32[]{:S(2)}, u32[]{:S(2)}) collective-permute-start(bf16[128,384]{1,0:T(8,128)(2,1)S(1)} %get-tuple-element.23), channel_id=1, source_target_pairs={{0,64},{1,72},{2,80},{3,88},{4,96},{5,104},{6,112},{7,120},{8,0},{... | collective-permute-start | bytes 294920 | tf_op jit(solution)/shard_map/ppermute | solution.py:138
  (5 other events, 9.2 us)
Sparse Core Ops, SparseCore 0:
  10.3 59.0 all-gather.2
  71.8 26.0 reduce-scatter.1
  178.3 87.8 all-gather.4

commit v10 on v7

--- a/solution.py
+++ b/solution.py
@@ -23,12 +23,11 @@
 POS_RANK = np.array([rank_of_pos(p) for p in range(N_DP)], np.int32)
 
 
-def deliver_perm(k):
+def deliver_perm(half, parity):
     pairs = []
-    for i in range(N_DP):
+    for i in range(parity, N_DP, 2):
         for t in range(N_TP):
-            dest = 8 * ((i % 2) ^ k) + t
-            pairs.append((i * N_TP + t, dest * N_TP + i // 2))
+            pairs.append((i * N_TP + t, (8 * half + t) * N_TP + i // 2))
     return pairs
 
 
@@ -127,16 +126,11 @@
             partial_rows.reshape(N_TP, rows_dev, width), TP, split_axis=0, concat_axis=0, tiled=True
         )
         summed.append(jnp.sum(pieces, axis=0))
-    summed = jnp.stack(summed, 0)
-    core = lax.axis_index("core")
-    low = lax.axis_index("x") < 2
-    got = []
-    for k in range(2):
-        piece = lax.dynamic_index_in_dim(summed, core ^ k, 0, keepdims=False)
-        got.append(lax.ppermute(piece, AXES, deliver_perm(k)))
-    first = jnp.where(low, got[0], got[1])
-    second = jnp.where(low, got[1], got[0])
-    input_grad = jnp.concatenate([first, second], axis=1).astype(jnp.bfloat16)
+    cols = []
+    for parity in range(2):
+        got = [lax.ppermute(summed[half], AXES, deliver_perm(half, parity)) for half in range(2)]
+        cols.append(got[0] + got[1])
+    input_grad = jnp.concatenate(cols, axis=1).astype(jnp.bfloat16)
     return (
         input_grad,
         gate_total.astype(jnp.bfloat16),

time: 360 us -> 371 us (1.031)
  starting transfers between devices: 30.8 us -> 35.1 us
  waiting for transfers between devices: 147 us -> 151 us
    ppermute x2 -> x4, waiting for transfers between devices: 7.56 us -> 17.7 us  [shards(): lax.ppermute(summed[half], AXES, deliver_perm(half, parity))]
    all_to_all x2, waiting for transfers between devices: 9.27 us -> 3.77 us  [shards(): lax.all_to_all(partial_rows.reshape(N_TP, rows_dev, width), TP, split_axi...]
    ppermute x2 -> x4, starting transfers between devices: 6.14 us -> 10.4 us  [shards(): lax.ppermute(summed[half], AXES, deliver_perm(half, parity))]
  transfers between devices with their start and end apart: 9 -> 11, of which waited for: 9 -> 9; matrix products, arithmetic and copies ran while one was open for 19% -> 19% of each run, Pallas kernels for 0% -> 0%
where the time goes in v10:
time: 371 us; the launch traced here: 369 us
  waiting for transfers between devices  151 us (41%)
  blocking collectives  75.3 us (20%)
  matrix products  65.8 us (18%)
  starting transfers between devices  35.1 us (9%)
  between operations  14.9 us (4%)
  other arithmetic  14.5 us (4%)
  local copies, waits for them, and re-layouts  11.9 us (3%)
    all_to_all x1, blocking collectives, shards(): lax.all_to_all(result, CHIPS, split_axis=0, concat_axis=0, tiled=True)  75.3 us
    all_gather x1, waiting for transfers between devices, shards(): packed = lax.all_gather(packed, DP, axis=0, tiled=True)  45.7 us
    dot_general x10, matrix products, contract_cols(): lax.dot_general(left_op, right_op, (((1,), (1,)), ((), ())), preferred_el...  34 us
    dot_general x6, matrix products, contract_rows(): lax.dot_general(left_op, right_op, (((0,), (0,)), ((), ())), preferred_el...  31.7 us
    all_to_all x1, waiting for transfers between devices, shards(): lax.all_to_all(out_grad, DP, split_axis=1, concat_axis=0, tiled=True)  30.3 us
    reduce_scatter x1, waiting for transfers between devices, shards(): lax.psum_scatter(result.reshape(2, row_count // 2, ff), 'core', scatter_d...  28.4 us
    all_to_all x1, waiting for transfers between devices, shards(): lax.all_to_all(rows_in, DP, split_axis=1, concat_axis=0, tiled=True)  18.7 us
    ppermute x4, waiting for transfers between devices, shards(): lax.ppermute(summed[half], AXES, deliver_perm(half, parity))  17.7 us
  transfers between devices with their start and end apart: 11, of which 9 were waited for; matrix products, arithmetic and copies ran while one was open for 19% of the time, Pallas kernels for 0%

profile of v10, /device:TPU:3, one launch (start us, length us, event | category | flops | bytes accessed | tf_op | source)
XLA Modules:
  0.0 368.7 jit_solution(5427078745420473154)
XLA Ops:
  11.7 6.3 %all-to-all-start = ((bf16[128,16,384]{0,2,1:T(8,128)(2,1)}), bf16[128,16,384]{0,2,1:T(8,128)(2,1)S(1)}, u32[]{:S(2)}, u32[]{:S(2)}) async-start(bf16[128,16,384]{0,2,1:T(8,128)(2,1)} %bitcast.1), calls=%async_computation | async-start | bytes 3145728 | tf_op jit(solution)/shard_map/all_to_all | solution.py:62
  19.2 30.3 %all-to-all-done = bf16[128,16,384]{0,2,1:T(8,128)(2,1)S(1)} async-done(((bf16[128,16,384]{0,2,1:T(8,128)(2,1)}), bf16[128,16,384]{0,2,1:T(8,128)(2,1)S(1)}, u32[]{:S(2)}, u32[]{:S(2)}) %all-to-all-start) | async-done | bytes 1572896 | tf_op jit(solution)/shard_map/all_to_all | solution.py:62
  52.7 3.5 fusion.115
  56.1 6.6 %convolution_add_fusion = f32[2048,1536]{1,0:T(8,128)} fusion(f32[2048,1536]{1,0:T(8,128)S(1)} %fusion.115, bf16[2048,384]{1,0:T(8,128)(2,1)S(1)} %bitcast.136, bf16[2,1536,384]{2,1,0:T(8,128)(2,1)S(1)} %copy-done.1), kind=kOutput, calls=%fused_computation.1 | convolution fusion | flops 2419064832 | bytes 27918336 | tf_op jit(solution)/shard_map/dot_general | solution.py:41
  62.8 6.6 %all-gather.3.cloned.1.call-done = bf16[2048,1536]{1,0:T(8,128)(2,1)} async-done(((bf16[128,1536]{1,0:T(8,128)(2,1)}), bf16[2048,1536]{1,0:T(8,128)(2,1)}) %all-gather.3.cloned.1.call-update) | async-done | bytes 6291472 | tf_op jit(solution)/shard_map/all_gather | solution.py:75
  69.5 28.4 %reduce-scatter.2.cloned.1.call-done = f32[1,1024,1536]{2,1,0:T(8,128)} async-done(((f32[2,1024,1536]{2,1,0:T(8,128)}), f32[1,1024,1536]{2,1,0:T(8,128)}) %reduce-scatter.2.cloned.1.call-update) | async-done | bytes 6291472 | tf_op jit(solution)/shard_map/reduce_scatter | solution.py:82
  97.9 75.3 %all_to_all.53 = f32[8,128,1536]{2,1,0:T(8,128)} all-to-all(f32[8,128,1536]{2,1,0:T(8,128)} %bitcast.138), channel_id=1, replica_groups=mesh['x'=4,'ylo'=2,'core'=2,'z'=4,'yhi'=2] {'x','ylo'}, dimensions={0} | all-to-all | bytes 12582912 | tf_op jit(solution)/shard_map/all_to_all | solution.py:85
  173.3 3.5 reduce_sum.27
  180.5 6.0 %all-to-all-start.4 = ((bf16[128,16,384]{0,2,1:T(8,128)(2,1)}), bf16[128,16,384]{0,2,1:T(8,128)(2,1)S(1)}, u32[]{:S(2)}, u32[]{:S(2)}) async-start(bf16[128,16,384]{0,2,1:T(8,128)(2,1)} %bitcast.32), calls=%async_computation.5 | async-start | bytes 3145728 | tf_op jit(solution)/shard_map/all_to_all | solution.py:88
  186.5 6.4 %fusion.88 = bf16[1,1536,384]{2,1,0:T(8,128)(2,1)S(1)} fusion(bf16[2048,384]{1,0:T(8,128)(2,1)S(1)} %bitcast.142, bf16[2048,1536]{1,0:T(8,128)(2,1)} %all-gather.3.cloned.1.call-done, bf16[2048]{0:T(1024)(128)(2,1)S(1)} %get-tuple-element.24), kind=kOutput, calls=%fused_computation.70 | convolution fusion | flops 2419654656 | bytes 9048064 | tf_op jit(solution)/shard_map/dot_general | solution.py:35
  192.9 6.3 %fusion.91 = bf16[1,1536,384]{2,1,0:T(8,128)(2,1)S(1)} fusion(bf16[2048,384]{1,0:T(8,128)(2,1)S(1)} %bitcast.143, bf16[2048,1536]{1,0:T(8,128)(2,1)} %all-gather.3.cloned.1.call-done, bf16[2048]{0:T(1024)(128)(2,1)S(1)} %get-tuple-element.25), kind=kOutput, calls=%fused_computation.71 | convolution fusion | flops 2419654656 | bytes 9048064 | tf_op jit(solution)/shard_map/dot_general | solution.py:35
  200.9 18.7 %all-to-all-done.4 = bf16[128,16,384]{0,2,1:T(8,128)(2,1)S(1)} async-done(((bf16[128,16,384]{0,2,1:T(8,128)(2,1)}), bf16[128,16,384]{0,2,1:T(8,128)(2,1)S(1)}, u32[]{:S(2)}, u32[]{:S(2)}) %all-to-all-start.4) | async-done | bytes 1572896 | tf_op jit(solution)/shard_map/all_to_all | solution.py:88
  221.1 45.7 %all-gather.5.cloned.1.call-done = bf16[2048,2,1536]{2,0,1:T(8,128)(2,1)} async-done(((bf16[128,2,1536]{2,0,1:T(8,128)(2,1)}), bf16[2048,2,1536]{2,0,1:T(8,128)(2,1)}) %all-gather.5.cloned.1.call-update) | async-done | bytes 12582928 | tf_op jit(solution)/shard_map/all_gather | solution.py:95
  266.8 4.2 %fusion.20 = f32[1024,384]{1,0:T(8,128)S(1)} fusion(bf16[2048,2,1536]{2,0,1:T(8,128)(2,1)} %all-gather.5.cloned.1.call-done, bf16[1024]{0:T(1024)(128)(2,1)S(1)} %broadcast_bitcast_fusion.2, bf16[2,384,1536]{2,1,0:T(8,128)(2,1)} %param.15), kind=kOutput, calls=%fused_computation.22 | convolution fusion | flops 1209532416 | bytes 5900288 | tf_op jit(solution)/shard_map/dot_general | solution.py:41
  279.4 6.8 %all-to-all-start.3 = ((f32[8,128,384]{2,1,0:T(8,128)}), f32[8,128,384]{2,1,0:T(8,128)S(1)}, u32[]{:S(2)}, u32[]{:S(2)}) async-start(f32[8,128,384]{2,1,0:T(8,128)} %bitcast.31), calls=%async_computation.4 | async-start | bytes 3145728 | tf_op jit(solution)/shard_map/all_to_all | solution.py:125
  286.2 4.2 %fusion.32 = f32[1024,384]{1,0:T(8,128)S(1)} fusion(bf16[2048,2,1536]{2,0,1:T(8,128)(2,1)} %all-gather.5.cloned.1.call-done, bf16[1024]{0:T(1024)(128)(2,1)S(1)} %broadcast_bitcast_fusion.5, bf16[2,384,1536]{2,1,0:T(8,128)(2,1)} %param.15), kind=kOutput, calls=%fused_computation.34 | convolution fusion | flops 1209532416 | bytes 5900288 | tf_op jit(solution)/shard_map/dot_general | solution.py:41
  290.4 3.9 %fusion.34 = f32[1024,384]{1,0:T(8,128)S(1)} fusion(bf16[2048,2,1536]{2,0,1:T(8,128)(2,1)} %all-gather.5.cloned.1.call-done, bf16[1024]{0:T(1024)(128)(2,1)S(1)} %broadcast_bitcast_fusion.5, bf16[2,384,1536]{2,1,0:T(8,128)(2,1)S(1)} %copy-done.14), kind=kOutput, calls=%fused_computation.36 | convolution fusion | flops 1209532416 | bytes 5900288 | tf_op jit(solution)/shard_map/dot_general | solution.py:41
  304.2 3.1 add_add_fusion.1
  308.5 5.4 %all-to-all-start.2 = ((f32[8,128,384]{2,1,0:T(8,128)}), f32[8,128,384]{2,1,0:T(8,128)S(1)}, u32[]{:S(2)}, u32[]{:S(2)}) async-start(f32[8,128,384]{2,1,0:T(8,128)} %bitcast.148), calls=%async_computation.3 | async-start | bytes 3145728 | tf_op jit(solution)/shard_map/all_to_all | solution.py:125
  313.9 7.1 %fusion.76 = bf16[1,384,1536]{2,1,0:T(8,128)(2,1)} fusion(bf16[2048,384]{1,0:T(8,128)(2,1)} %bitcast.144, bf16[2048,2,1536]{2,0,1:T(8,128)(2,1)} %all-gather.5.cloned.1.call-done, bf16[2048]{0:T(1024)(128)(2,1)S(1)} %get-tuple-element.24), kind=kOutput, calls=%fused_computation.66 | convolution fusion | flops 2419654656 | bytes 9048064 | tf_op jit(solution)/shard_map/dot_general | solution.py:35
  321.0 6.5 %fusion.79 = bf16[1,384,1536]{2,1,0:T(8,128)(2,1)} fusion(bf16[2048,384]{1,0:T(8,128)(2,1)S(1)} %bitcast.147, bf16[2048,2,1536]{2,0,1:T(8,128)(2,1)} %all-gather.5.cloned.1.call-done, bf16[2048]{0:T(1024)(128)(2,1)S(1)} %get-tuple-element.25), kind=kOutput, calls=%fused_computation.67 | convolution fusion | flops 2419654656 | bytes 9048064 | tf_op jit(solution)/shard_map/dot_general | solution.py:35
  327.7 5.5 %collective-permute-start.3 = (f32[128,384]{1,0:T(8,128)S(1)}, f32[128,384]{1,0:T(8,128)S(1)}, u32[]{:S(2)}, u32[]{:S(2)}) collective-permute-start(f32[128,384]{1,0:T(8,128)S(1)} %reduce_sum.29), channel_id=1, source_target_pairs={{8,64},{9,72},{10,80},{11,88},{12,96},{13,104},{14,112},{15,120},{... | collective-permute-start | bytes 589832 | tf_op jit(solution)/shard_map/ppermute | solution.py:131
  343.7 9.2 %collective-permute-done.2 = f32[128,384]{1,0:T(8,128)S(1)} collective-permute-done((f32[128,384]{1,0:T(8,128)S(1)}, f32[128,384]{1,0:T(8,128)S(1)}, u32[]{:S(2)}, u32[]{:S(2)}) %collective-permute-start.2) | collective-permute-done | bytes 196640 | tf_op jit(solution)/shard_map/ppermute | solution.py:131
  352.9 8.5 %collective-permute-done = f32[128,384]{1,0:T(8,128)S(1)} collective-permute-done((f32[128,384]{1,0:T(8,128)S(1)}, f32[128,384]{1,0:T(8,128)S(1)}, u32[]{:S(2)}, u32[]{:S(2)}) %collective-permute-start) | collective-permute-done | bytes 196640 | tf_op jit(solution)/shard_map/ppermute | solution.py:131
  (89 shorter events, 45.7 us)
Async XLA Ops:
  7.2 62.3 %all-gather.3.cloned.1.call-start = ((), (), s32[]{:S(2)}) async-start(), calls=%async_computation.6 | async-start | bytes 6684672 | tf_op jit(solution)/shard_map/all_gather | solution.py:75
  11.7 6.4 %copy-start.9 = (s32[16]{0:T(128)S(1)}, s32[16]{0:T(128)}, u32[]{:S(2)}) copy-start(s32[16]{0:T(128)} %constant.35) | copy-start | bytes 196
  11.7 6.4 %copy-start = (s32[16]{0:T(128)S(1)}, s32[16]{0:T(128)}, u32[]{:S(2)}) copy-start(s32[16]{0:T(128)} %param.18) | copy-start | bytes 196
  11.7 37.8 %all-to-all-start = ((bf16[128,16,384]{0,2,1:T(8,128)(2,1)}), bf16[128,16,384]{0,2,1:T(8,128)(2,1)S(1)}, u32[]{:S(2)}, u32[]{:S(2)}) async-start(bf16[128,16,384]{0,2,1:T(8,128)(2,1)} %bitcast.1), calls=%async_computation | async-start | bytes 3145728 | tf_op jit(solution)/shard_map/all_to_all | solution.py:62
  18.0 79.9 %reduce-scatter.2.cloned.1.call-start = ((), (), s32[]{:S(2)}) async-start(), calls=%async_computation.7 | async-start | bytes 18874368 | tf_op jit(solution)/shard_map/reduce_scatter | solution.py:82
  69.5 197.4 %all-gather.5.cloned.1.call-start = ((), (), s32[]{:S(2)}) async-start(), calls=%async_computation.8 | async-start | bytes 13369344 | tf_op jit(solution)/shard_map/all_gather | solution.py:95
  173.3 3.5 copy-start.6
  173.3 3.5 copy-start.7
  180.5 39.1 %all-to-all-start.4 = ((bf16[128,16,384]{0,2,1:T(8,128)(2,1)}), bf16[128,16,384]{0,2,1:T(8,128)(2,1)S(1)}, u32[]{:S(2)}, u32[]{:S(2)}) async-start(bf16[128,16,384]{0,2,1:T(8,128)(2,1)} %bitcast.32), calls=%async_computation.5 | async-start | bytes 3145728 | tf_op jit(solution)/shard_map/all_to_all | solution.py:88
  221.1 49.9 %copy-start.11 = (bf16[2,384,1536]{2,1,0:T(8,128)(2,1)S(1)}, bf16[2,384,1536]{2,1,0:T(8,128)(2,1)}, u32[]{:S(2)}) copy-start(bf16[2,384,1536]{2,1,0:T(8,128)(2,1)} %param.15) | copy-start | bytes 7077892
  266.8 5.9 %copy-start.10 = (bf16[2048,2,1536]{2,0,1:T(8,128)(2,1)S(1)}, bf16[2048,2,1536]{2,0,1:T(8,128)(2,1)}, u32[]{:S(2)}) copy-start(bf16[2048,2,1536]{2,0,1:T(8,128)(2,1)} %all-gather.5.cloned.1.call-done) | copy-start | bytes 37748740
  279.4 29.1 %all-to-all-start.3 = ((f32[8,128,384]{2,1,0:T(8,128)}), f32[8,128,384]{2,1,0:T(8,128)S(1)}, u32[]{:S(2)}, u32[]{:S(2)}) async-start(f32[8,128,384]{2,1,0:T(8,128)} %bitcast.31), calls=%async_computation.4 | async-start | bytes 3145728 | tf_op jit(solution)/shard_map/all_to_all | solution.py:125
  286.1 4.2 %copy-start.14 = (bf16[2,384,1536]{2,1,0:T(8,128)(2,1)S(1)}, bf16[2,384,1536]{2,1,0:T(8,128)(2,1)}, u32[]{:S(2)}) copy-start(bf16[2,384,1536]{2,1,0:T(8,128)(2,1)} %param.14) | copy-start | bytes 7077892
  286.1 8.2 %slice-start = ((s8[12582912]{0:T(1024)(128)(4,1)}), s8[4194304]{0:T(1024)(128)(4,1)S(1)}, s32[]{:S(2)}) async-start(s8[12582912]{0:T(1024)(128)(4,1)} %bitcast.149), calls=%async_computation.9 | async-start | bytes 8388608
  286.2 8.2 %slice-start.1 = ((s8[12582912]{0:T(1024)(128)(4,1)}), s8[4194304]{0:T(1024)(128)(4,1)S(1)}, s32[]{:S(2)}) async-start(s8[12582912]{0:T(1024)(128)(4,1)} %bitcast.149), calls=%async_computation.10 | async-start | bytes 8388608
  290.4 3.9 %copy-start.4 = (bf16[16,128,384]{2,1,0:T(8,128)(2,1)S(1)}, bf16[16,128,384]{2,1,0:T(8,128)(2,1)}, u32[]{:S(2)}) copy-start(bf16[16,128,384]{2,1,0:T(8,128)(2,1)} %copy.23) | copy-start | bytes 4718596
  290.4 4.0 %slice-start.2 = ((s8[12582912]{0:T(1024)(128)(4,1)}), s8[4194304]{0:T(1024)(128)(4,1)S(1)}, s32[]{:S(2)}) async-start(s8[12582912]{0:T(1024)(128)(4,1)} %bitcast.149), calls=%async_computation.11 | async-start | bytes 8388608
  308.5 27.2 %all-to-all-start.2 = ((f32[8,128,384]{2,1,0:T(8,128)}), f32[8,128,384]{2,1,0:T(8,128)S(1)}, u32[]{:S(2)}, u32[]{:S(2)}) async-start(f32[8,128,384]{2,1,0:T(8,128)} %bitcast.148), calls=%async_computation.3 | async-start | bytes 3145728 | tf_op jit(solution)/shard_map/all_to_all | solution.py:125
  313.9 7.1 %copy-start.5 = (bf16[16,128,384]{2,1,0:T(8,128)(2,1)S(1)}, bf16[16,128,384]{2,1,0:T(8,128)(2,1)}, u32[]{:S(2)}) copy-start(bf16[16,128,384]{2,1,0:T(8,128)(2,1)} %copy.23) | copy-start | bytes 4718596
  327.7 11.1 %copy-start.8 = (bf16[1,384,1536]{2,1,0:T(8,128)(2,1)S(1)}, bf16[1,384,1536]{2,1,0:T(8,128)(2,1)}, u32[]{:S(2)}) copy-start(bf16[1,384,1536]{2,1,0:T(8,128)(2,1)} %fusion.76) | copy-start | bytes 3538948
  327.7 16.0 %collective-permute-start.3 = (f32[128,384]{1,0:T(8,128)S(1)}, f32[128,384]{1,0:T(8,128)S(1)}, u32[]{:S(2)}, u32[]{:S(2)}) collective-permute-start(f32[128,384]{1,0:T(8,128)S(1)} %reduce_sum.29), channel_id=1, source_target_pairs={{8,64},{9,72},{10,80},{11,88},{12,96},{13,104},{14,112},{15,120},{... | collective-permute-start | bytes 589832 | tf_op jit(solution)/shard_map/ppermute | solution.py:131
  335.8 17.1 %collective-permute-start.2 = (f32[128,384]{1,0:T(8,128)S(1)}, f32[128,384]{1,0:T(8,128)S(1)}, u32[]{:S(2)}, u32[]{:S(2)}) collective-permute-start(f32[128,384]{1,0:T(8,128)S(1)} %reduce_sum.28), channel_id=1, source_target_pairs={{8,0},{9,8},{10,16},{11,24},{12,32},{13,40},{14,48},{15,56},{24,1}... | collective-permute-start | bytes 589832 | tf_op jit(solution)/shard_map/ppermute | solution.py:131
  341.7 11.2 %collective-permute-start.1 = (f32[128,384]{1,0:T(8,128)S(1)}, f32[128,384]{1,0:T(8,128)S(1)}, u32[]{:S(2)}, u32[]{:S(2)}) collective-permute-start(f32[128,384]{1,0:T(8,128)S(1)} %reduce_sum.29), channel_id=1, source_target_pairs={{0,64},{1,72},{2,80},{3,88},{4,96},{5,104},{6,112},{7,120},{16,65}... | collective-permute-start | bytes 589832 | tf_op jit(solution)/shard_map/ppermute | solution.py:131
  342.3 19.1 %collective-permute-start = (f32[128,384]{1,0:T(8,128)S(1)}, f32[128,384]{1,0:T(8,128)S(1)}, u32[]{:S(2)}, u32[]{:S(2)}) collective-permute-start(f32[128,384]{1,0:T(8,128)S(1)} %reduce_sum.28), channel_id=1, source_target_pairs={{0,0},{1,8},{2,16},{3,24},{4,32},{5,40},{6,48},{7,56},{16,1},{17,9... | collective-permute-start | bytes 589832 | tf_op jit(solution)/shard_map/ppermute | solution.py:131
  (5 other events, 10.8 us)
Sparse Core Ops, SparseCore 0:
  10.3 59.0 all-gather.2
  71.8 26.0 reduce-scatter.1
  178.3 88.4 all-gather.4

commit v11 on v7

--- a/solution.py
+++ b/solution.py
@@ -94,34 +94,30 @@
     ).astype(jnp.bfloat16)
     packed = jnp.stack([gate_grad, up_grad], axis=1)
     packed = lax.all_gather(packed, DP, axis=0, tiled=True)
-    gate_g, up_g = packed[:, 0], packed[:, 1]
+    both = packed.reshape(row_count, 2 * ff)
 
     down_terms = []
     gate_terms = []
     up_terms = []
     for which in range(expert_count):
         down_terms.append(contract_rows(hid_g * masks[which], dy_cols))
-        gate_masked = gate_g * masks[which]
-        up_masked = up_g * masks[which]
-        gate_terms.append(contract_rows(x_cols, gate_masked))
-        up_terms.append(contract_rows(x_cols, up_masked))
+        weight_grads = contract_rows(x_cols, both * masks[which])
+        gate_terms.append(weight_grads[:, :ff])
+        up_terms.append(weight_grads[:, ff:])
     down_total = jnp.stack(down_terms, 0)
     gate_total = jnp.stack(gate_terms, 0)
     up_total = jnp.stack(up_terms, 0)
 
     width = w_gate.shape[1]
     half_rows = row_count // 2
+    w_both = [jnp.concatenate([w_gate[which], w_up[which]], axis=1) for which in range(expert_count)]
     summed = []
     for half in range(2):
         rows = slice(half * half_rows, (half + 1) * half_rows)
         partial_rows = jnp.zeros((half_rows, width), jnp.float32)
         for which in range(expert_count):
-            gate_masked = gate_g[rows] * masks[which][rows]
-            up_masked = up_g[rows] * masks[which][rows]
-            partial_rows = (
-                partial_rows
-                + contract_cols(gate_masked, w_gate[which])
-                + contract_cols(up_masked, w_up[which])
+            partial_rows = partial_rows + contract_cols(
+                both[rows] * masks[which][rows], w_both[which]
             )
         pieces = lax.all_to_all(
             partial_rows.reshape(N_TP, rows_dev, width), TP, split_axis=0, concat_axis=0, tiled=True

time: 360 us -> 468 us (1.30); the launches traced: 360 us -> 459 us
  local copies, waits for them, and re-layouts: 11.9 us -> 78.8 us
  other arithmetic: 14.5 us -> 43 us
    mul x0 -> x6, local copies, waits for them, and re-layouts: none -> 34 us  [the longest x2 33.7 us: shards(): weight_grads = contract_rows(x_cols, both * masks[which])]
    slice x6 -> x5, local copies, waits for them, and re-layouts: 0.44 us -> 27.9 us  [the longest x3 27.7 us: shards(): both[rows] * masks[which][rows]]
    mul x0 -> x3, other arithmetic: none -> 27.1 us  [the longest x1 14.6 us: shards(): weight_grads = contract_rows(x_cols, both * masks[which])]
    all_to_all x2, waiting for transfers between devices: 9.27 us -> 15.1 us  [shards(): lax.all_to_all(partial_rows.reshape(N_TP, rows_dev, width), TP, split_axi...]
    all_gather x1, waiting for transfers between devices: 45.7 us -> 39.9 us  [shards(): packed = lax.all_gather(packed, DP, axis=0, tiled=True)]
    squeeze x0 -> x1, local copies, waits for them, and re-layouts: none -> 4.75 us  [shards(): w_up[which]]
    dot_general x10 -> x6, matrix products: 34 us -> 32.2 us  [contract_cols(): lax.dot_general(left_op, right_op, (((1,), (1,)), ((), ())), preferred_el...]
    dot_general x6 -> x4, matrix products: 31.7 us -> 32.7 us  [contract_rows(): lax.dot_general(left_op, right_op, (((0,), (0,)), ((), ())), preferred_el...]
  transfers between devices with their start and end apart: 9 -> 9, of which waited for: 9 -> 8; matrix products, arithmetic and copies ran while one was open for 19% -> 31% of each run, Pallas kernels for 0% -> 0%
where the time goes in v11:
time: 468 us; the launch traced here: 459 us
  waiting for transfers between devices  150 us (32%)
  local copies, waits for them, and re-layouts  78.8 us (17%)
  blocking collectives  75.3 us (16%)
  matrix products  65 us (14%)
  other arithmetic  43 us (9%)
  starting transfers between devices  32.1 us (7%)
  between operations  15.2 us (3%)
    all_to_all x1, blocking collectives, shards(): lax.all_to_all(result, CHIPS, split_axis=0, concat_axis=0, tiled=True)  75.3 us
    all_gather x1, waiting for transfers between devices, shards(): packed = lax.all_gather(packed, DP, axis=0, tiled=True)  39.9 us
    mul x2, local copies, waits for them, and re-layouts, shards(): weight_grads = contract_rows(x_cols, both * masks[which])  33.7 us
    dot_general x4, matrix products, contract_rows(): lax.dot_general(left_op, right_op, (((0,), (0,)), ((), ())), preferred_el...  32.7 us
    dot_general x6, matrix products, contract_cols(): lax.dot_general(left_op, right_op, (((1,), (1,)), ((), ())), preferred_el...  32.2 us
    all_to_all x1, waiting for transfers between devices, shards(): lax.all_to_all(out_grad, DP, split_axis=1, concat_axis=0, tiled=True)  30.3 us
    reduce_scatter x1, waiting for transfers between devices, shards(): lax.psum_scatter(result.reshape(2, row_count // 2, ff), 'core', scatter_d...  28.4 us
    slice x3, local copies, waits for them, and re-layouts, shards(): both[rows] * masks[which][rows]  27.7 us
  transfers between devices with their start and end apart: 9, of which 8 were waited for; matrix products, arithmetic and copies ran while one was open for 31% of the time, Pallas kernels for 0%

profile of v11, /device:TPU:3, one launch (start us, length us, event | category | flops | bytes accessed | tf_op | source)
XLA Modules:
  0.0 459.1 jit_solution(13706847392246411170)
XLA Ops:
  11.7 6.3 %all-to-all-start = ((bf16[128,16,384]{0,2,1:T(8,128)(2,1)}), bf16[128,16,384]{0,2,1:T(8,128)(2,1)S(1)}, u32[]{:S(2)}, u32[]{:S(2)}) async-start(bf16[128,16,384]{0,2,1:T(8,128)(2,1)} %bitcast.1), calls=%async_computation | async-start | bytes 3145728 | tf_op jit(solution)/shard_map/all_to_all | solution.py:63
  19.2 30.3 %all-to-all-done = bf16[128,16,384]{0,2,1:T(8,128)(2,1)S(1)} async-done(((bf16[128,16,384]{0,2,1:T(8,128)(2,1)}), bf16[128,16,384]{0,2,1:T(8,128)(2,1)S(1)}, u32[]{:S(2)}, u32[]{:S(2)}) %all-to-all-start) | async-done | bytes 1572896 | tf_op jit(solution)/shard_map/all_to_all | solution.py:63
  56.1 6.6 %convolution_add_fusion = f32[2048,1536]{1,0:T(8,128)} fusion(f32[2048,1536]{1,0:T(8,128)S(1)} %fusion.25, bf16[2048,384]{1,0:T(8,128)(2,1)S(1)} %bitcast.88, bf16[2,1536,384]{2,1,0:T(8,128)(2,1)S(1)} %copy-done.1), kind=kOutput, calls=%fused_computation.1 | convolution fusion | flops 2419064832 | bytes 27918336 | tf_op jit(solution)/shard_map/dot_general | solution.py:42
  62.8 6.6 %all-gather.3.cloned.1.call-done = bf16[2048,1536]{1,0:T(8,128)(2,1)} async-done(((bf16[128,1536]{1,0:T(8,128)(2,1)}), bf16[2048,1536]{1,0:T(8,128)(2,1)}) %all-gather.3.cloned.1.call-update) | async-done | bytes 6291472 | tf_op jit(solution)/shard_map/all_gather | solution.py:76
  69.5 28.4 %reduce-scatter.2.cloned.1.call-done = f32[1,1024,1536]{2,1,0:T(8,128)} async-done(((f32[2,1024,1536]{2,1,0:T(8,128)}), f32[1,1024,1536]{2,1,0:T(8,128)}) %reduce-scatter.2.cloned.1.call-update) | async-done | bytes 6291472 | tf_op jit(solution)/shard_map/reduce_scatter | solution.py:83
  98.0 75.3 %all_to_all.53 = f32[8,128,1536]{2,1,0:T(8,128)} all-to-all(f32[8,128,1536]{2,1,0:T(8,128)} %bitcast.92), channel_id=1, replica_groups=mesh['x'=4,'ylo'=2,'core'=2,'z'=4,'yhi'=2] {'x','ylo'}, dimensions={0} | all-to-all | bytes 12582912 | tf_op jit(solution)/shard_map/all_to_all | solution.py:86
  185.1 6.3 %all-to-all-start.4 = ((bf16[128,16,384]{0,2,1:T(8,128)(2,1)}), bf16[128,16,384]{0,2,1:T(8,128)(2,1)S(1)}, u32[]{:S(2)}, u32[]{:S(2)}) async-start(bf16[128,16,384]{0,2,1:T(8,128)(2,1)} %bitcast.30), calls=%async_computation.5 | async-start | bytes 3145728 | tf_op jit(solution)/shard_map/all_to_all | solution.py:89
  191.4 6.4 %fusion.12 = bf16[1,1536,384]{2,1,0:T(8,128)(2,1)S(1)} fusion(bf16[2048,384]{1,0:T(8,128)(2,1)S(1)} %bitcast.96, bf16[2048,1536]{1,0:T(8,128)(2,1)} %all-gather.3.cloned.1.call-done, bf16[2048]{0:T(1024)(128)(2,1)S(1)} %broadcast_bitcast_fusion), kind=kOutput, calls=%fused_computation.18 | convolution fusion | flops 2419654656 | bytes 9048064 | tf_op jit(solution)/shard_map/dot_general | solution.py:36
  197.9 6.5 %fusion.15 = bf16[1,1536,384]{2,1,0:T(8,128)(2,1)S(1)} fusion(bf16[2048,384]{1,0:T(8,128)(2,1)S(1)} %bitcast.97, bf16[2048,1536]{1,0:T(8,128)(2,1)} %all-gather.3.cloned.1.call-done, bf16[2048]{0:T(1024)(128)(2,1)S(1)} %broadcast_bitcast_fusion.1), kind=kOutput, calls=%fused_computation.19 | convolution fusion | flops 2419654656 | bytes 9048064 | tf_op jit(solution)/shard_map/dot_general | solution.py:36
  206.0 21.4 %all-to-all-done.4 = bf16[128,16,384]{0,2,1:T(8,128)(2,1)S(1)} async-done(((bf16[128,16,384]{0,2,1:T(8,128)(2,1)}), bf16[128,16,384]{0,2,1:T(8,128)(2,1)S(1)}, u32[]{:S(2)}, u32[]{:S(2)}) %all-to-all-start.4) | async-done | bytes 1572896 | tf_op jit(solution)/shard_map/all_to_all | solution.py:89
  229.0 39.9 %all-gather.5.cloned.1.call-done = bf16[2048,2,1536]{2,0,1:T(8,128)(2,1)} async-done(((bf16[128,2,1536]{2,0,1:T(8,128)(2,1)}), bf16[2048,2,1536]{2,0,1:T(8,128)(2,1)}) %all-gather.5.cloned.1.call-update) | async-done | bytes 12582928 | tf_op jit(solution)/shard_map/all_gather | solution.py:96
  268.9 10.3 %fusion.49 = (bf16[1024,2,1536]{2,0,1:T(8,128)(2,1)}, bf16[1024,2,1536]{2,0,1:T(8,128)(2,1)}) fusion(bf16[2048,2,1536]{2,0,1:T(8,128)(2,1)} %all-gather.5.cloned.1.call-done), kind=kLoop, calls=%fused_computation.92 | loop fusion | bytes 25165824 | tf_op jit(solution)/shard_map/slice | solution.py:120
  279.2 8.7 %copy.36 = bf16[1024,2,1536]{0,2,1:T(8,128)(2,1)} copy(bf16[1024,2,1536]{2,0,1:T(8,128)(2,1)} %get-tuple-element.14) | data formatting | bytes 12582912 | tf_op jit(solution)/shard_map/slice | solution.py:120
  287.9 6.3 %bitcast_multiply_fusion.1 = (bf16[1024,3072]{0,1:T(8,128)(2,1)S(1)}, bf16[1024,3072]{0,1:T(8,128)(2,1)}) fusion(bf16[1024,2,1536]{0,2,1:T(8,128)(2,1)} %copy.36, bf16[1024]{0:T(1024)(128)(2,1)S(1)} %broadcast_bitcast_fusion.3, bf16[1024]{0:T(1024)(128)(2,1)S(1)} %broadcast_bitcast_fusion.2), kind=kLoop, calls=%fused_computation.3 | loop fusion | flops 6291456 | bytes 18878464 | tf_op jit(solution)/shard_map/mul | solution.py:120
  294.2 6.4 %fusion.18 = f32[1024,384]{1,0:T(8,128)S(1)} fusion(bf16[1024,3072]{0,1:T(8,128)(2,1)} %get-tuple-element.17, bf16[384,1536]{1,0:T(8,128)(2,1)} %get-tuple-element.27, bf16[384,1536]{1,0:T(8,128)(2,1)} %get-tuple-element.46), kind=kOutput, calls=%fused_computation.25 | convolution fusion | flops 2420637696 | bytes 10223616 | tf_op jit(solution)/shard_map/dot_general | solution.py:42
  305.4 6.9 %all-to-all-start.3 = ((f32[8,128,384]{2,1,0:T(8,128)}), f32[8,128,384]{2,1,0:T(8,128)}, u32[]{:S(2)}, u32[]{:S(2)}) async-start(f32[8,128,384]{2,1,0:T(8,128)} %bitcast.100), calls=%async_computation.4 | async-start | bytes 3145728 | tf_op jit(solution)/shard_map/all_to_all | solution.py:122
  312.2 8.7 %copy.35 = bf16[1024,2,1536]{0,2,1:T(8,128)(2,1)} copy(bf16[1024,2,1536]{2,0,1:T(8,128)(2,1)} %get-tuple-element.15) | data formatting | bytes 12582912 | tf_op jit(solution)/shard_map/slice | solution.py:120
  333.4 14.6 %broadcast_multiply_fusion.1 = (bf16[2048,2,1536]{2,0,1:T(8,128)(2,1)}, bf16[2048,2,1536]{2,0,1:T(8,128)(2,1)}) fusion(bf16[2048,2,1536]{2,0,1:T(8,128)(2,1)} %all-gather.5.cloned.1.call-done, bf16[2048]{0:T(1024)(128)(2,1)S(1)} %broadcast_bitcast_fusion.1, bf16[2048]{0:T(1024)(128)(2,1)S(1)} %broadcast_bitcast_fusion), kind=kLoop, calls=%fused_computation.11 | loop fusion | flops 12582912 | bytes 37756928 | tf_op jit(solution)/shard_map/mul | solution.py:104
  348.0 16.9 %copy.39 = bf16[2048,2,1536]{0,2,1:T(8,128)(2,1)} copy(bf16[2048,2,1536]{2,0,1:T(8,128)(2,1)} %get-tuple-element.12) | data formatting | bytes 25165824 | tf_op jit(solution)/shard_map/mul | solution.py:104
  364.9 9.7 %convolution_convert_fusion.1 = bf16[384,3072]{1,0:T(8,128)(2,1)} fusion(bf16[2048,384]{1,0:T(8,128)(2,1)} %bitcast.98, bf16[2048,3072]{0,1:T(8,128)(2,1)} %bitcast.87), kind=kOutput, calls=%fused_computation.13 | convolution fusion | flops 4833017856 | bytes 16515072 | tf_op jit(solution)/shard_map/dot_general | solution.py:36
  379.3 16.8 %copy.40 = bf16[2048,2,1536]{0,2,1:T(8,128)(2,1)} copy(bf16[2048,2,1536]{2,0,1:T(8,128)(2,1)} %get-tuple-element.13) | data formatting | bytes 25165824 | tf_op jit(solution)/shard_map/mul | solution.py:104
  396.2 10.1 %convolution_convert_fusion = bf16[384,3072]{1,0:T(8,128)(2,1)} fusion(bf16[2048,384]{1,0:T(8,128)(2,1)S(1)} %bitcast.99, bf16[2048,3072]{0,1:T(8,128)(2,1)} %bitcast.86), kind=kOutput, calls=%fused_computation.12 | convolution fusion | flops 4833017856 | bytes 16515072 | tf_op jit(solution)/shard_map/dot_general | solution.py:36
  406.2 6.6 %all-to-all-start.2 = ((f32[8,128,384]{2,1,0:T(8,128)}), f32[8,128,384]{2,1,0:T(8,128)S(1)}, u32[]{:S(2)}, u32[]{:S(2)}) async-start(f32[8,128,384]{2,1,0:T(8,128)} %bitcast.21), calls=%async_computation.3 | async-start | bytes 3145728 | tf_op jit(solution)/shard_map/all_to_all | solution.py:122
  419.6 15.1 %all-to-all-done.2 = f32[8,128,384]{2,1,0:T(8,128)S(1)} async-done(((f32[8,128,384]{2,1,0:T(8,128)}), f32[8,128,384]{2,1,0:T(8,128)S(1)}, u32[]{:S(2)}, u32[]{:S(2)}) %all-to-all-start.2) | async-done | bytes 1572896 | tf_op jit(solution)/shard_map/all_to_all | solution.py:122
  (87 shorter events, 72.6 us)
Async XLA Ops:
  7.2 3.0 copy-start.3
  7.2 62.3 %all-gather.3.cloned.1.call-start = ((), (), s32[]{:S(2)}) async-start(), calls=%async_computation.6 | async-start | bytes 6684672 | tf_op jit(solution)/shard_map/all_gather | solution.py:76
  11.7 6.4 %copy-start.12 = (s32[16]{0:T(128)S(1)}, s32[16]{0:T(128)}, u32[]{:S(2)}) copy-start(s32[16]{0:T(128)} %constant.55) | copy-start | bytes 196
  11.7 6.4 %copy-start = (s32[16]{0:T(128)S(1)}, s32[16]{0:T(128)}, u32[]{:S(2)}) copy-start(s32[16]{0:T(128)} %param.18) | copy-start | bytes 196
  11.7 37.8 %all-to-all-start = ((bf16[128,16,384]{0,2,1:T(8,128)(2,1)}), bf16[128,16,384]{0,2,1:T(8,128)(2,1)S(1)}, u32[]{:S(2)}, u32[]{:S(2)}) async-start(bf16[128,16,384]{0,2,1:T(8,128)(2,1)} %bitcast.1), calls=%async_computation | async-start | bytes 3145728 | tf_op jit(solution)/shard_map/all_to_all | solution.py:63
  18.0 79.9 %reduce-scatter.2.cloned.1.call-start = ((), (), s32[]{:S(2)}) async-start(), calls=%async_computation.7 | async-start | bytes 18874368 | tf_op jit(solution)/shard_map/reduce_scatter | solution.py:83
  69.5 199.5 %all-gather.5.cloned.1.call-start = ((), (), s32[]{:S(2)}) async-start(), calls=%async_computation.8 | async-start | bytes 13369344 | tf_op jit(solution)/shard_map/all_gather | solution.py:96
  173.3 3.4 copy-start.6
  173.3 3.4 copy-start.7
  178.8 4.8 %copy-start.4 = (bf16[128,6144]{1,0:T(8,128)(2,1)S(1)}, bf16[128,6144]{1,0:T(8,128)(2,1)}, u32[]{:S(2)}) copy-start(bf16[128,6144]{1,0:T(8,128)(2,1)} %param.10) | copy-start | bytes 4718596
  185.1 42.4 %all-to-all-start.4 = ((bf16[128,16,384]{0,2,1:T(8,128)(2,1)}), bf16[128,16,384]{0,2,1:T(8,128)(2,1)S(1)}, u32[]{:S(2)}, u32[]{:S(2)}) async-start(bf16[128,16,384]{0,2,1:T(8,128)(2,1)} %bitcast.30), calls=%async_computation.5 | async-start | bytes 3145728 | tf_op jit(solution)/shard_map/all_to_all | solution.py:89
  294.1 6.4 %copy-start.8 = (bf16[384,1536]{1,0:T(8,128)(2,1)S(1)}, bf16[384,1536]{1,0:T(8,128)(2,1)}, u32[]{:S(2)}) copy-start(bf16[384,1536]{1,0:T(8,128)(2,1)} %get-tuple-element.26) | copy-start | bytes 3538948
  294.2 6.4 %copy-start.10 = (bf16[384,1536]{1,0:T(8,128)(2,1)S(1)}, bf16[384,1536]{1,0:T(8,128)(2,1)}, u32[]{:S(2)}) copy-start(bf16[384,1536]{1,0:T(8,128)(2,1)} %get-tuple-element.47) | copy-start | bytes 3538948
  305.4 100.9 %all-to-all-start.3 = ((f32[8,128,384]{2,1,0:T(8,128)}), f32[8,128,384]{2,1,0:T(8,128)}, u32[]{:S(2)}, u32[]{:S(2)}) async-start(f32[8,128,384]{2,1,0:T(8,128)} %bitcast.100), calls=%async_computation.4 | async-start | bytes 3145728 | tf_op jit(solution)/shard_map/all_to_all | solution.py:122
  348.0 26.6 %slice-start = ((s8[6291456]{0:T(1024)(128)(4,1)}), s8[2097152]{0:T(1024)(128)(4,1)S(1)}, s32[]{:S(2)}) async-start(s8[6291456]{0:T(1024)(128)(4,1)} %bitcast.90), calls=%async_computation.9 | async-start | bytes 4194304
  364.8 9.7 %slice-start.1 = ((s8[6291456]{0:T(1024)(128)(4,1)}), s8[4194304]{0:T(1024)(128)(4,1)S(1)}, s32[]{:S(2)}) async-start(s8[6291456]{0:T(1024)(128)(4,1)} %bitcast.90), calls=%async_computation.10 | async-start | bytes 8388608
  364.8 9.7 %copy-start.9 = (bf16[384,1536]{1,0:T(8,128)(2,1)S(1)}, bf16[384,1536]{1,0:T(8,128)(2,1)}, u32[]{:S(2)}) copy-start(bf16[384,1536]{1,0:T(8,128)(2,1)} %get-tuple-element.26) | copy-start | bytes 3538948
  364.9 9.8 %copy-start.11 = (bf16[384,1536]{1,0:T(8,128)(2,1)S(1)}, bf16[384,1536]{1,0:T(8,128)(2,1)}, u32[]{:S(2)}) copy-start(bf16[384,1536]{1,0:T(8,128)(2,1)} %get-tuple-element.47) | copy-start | bytes 3538948
  364.9 9.8 %copy-start.13 = (f32[1024,384]{1,0:T(8,128)S(1)}, f32[1024,384]{1,0:T(8,128)}, u32[]{:S(2)}) copy-start(f32[1024,384]{1,0:T(8,128)} %fusion.19) | copy-start | bytes 4718596
  379.3 16.8 %copy-start.5 = (bf16[16,128,384]{2,1,0:T(8,128)(2,1)S(1)}, bf16[16,128,384]{2,1,0:T(8,128)(2,1)}, u32[]{:S(2)}) copy-start(bf16[16,128,384]{2,1,0:T(8,128)(2,1)} %copy.38) | copy-start | bytes 4718596
  406.2 28.4 %all-to-all-start.2 = ((f32[8,128,384]{2,1,0:T(8,128)}), f32[8,128,384]{2,1,0:T(8,128)S(1)}, u32[]{:S(2)}, u32[]{:S(2)}) async-start(f32[8,128,384]{2,1,0:T(8,128)} %bitcast.21), calls=%async_computation.3 | async-start | bytes 3145728 | tf_op jit(solution)/shard_map/all_to_all | solution.py:122
  412.9 2.4 copy-start.2
  434.8 14.0 %collective-permute-start = (bf16[128,384]{1,0:T(8,128)(2,1)S(1)}, bf16[128,384]{1,0:T(8,128)(2,1)S(1)}, u32[]{:S(2)}, u32[]{:S(2)}) collective-permute-start(bf16[128,384]{1,0:T(8,128)(2,1)S(1)} %get-tuple-element.34), channel_id=1, source_target_pairs={{0,0},{1,8},{2,16},{3,24},{4,32},{5,40},{6,48},{7,56},{8,64},{9,72... | collective-permute-start | bytes 294920 | tf_op jit(solution)/shard_map/ppermute | solution.py:132
  438.3 13.1 %collective-permute-start.1 = (bf16[128,384]{1,0:T(8,128)(2,1)S(1)}, bf16[128,384]{1,0:T(8,128)(2,1)S(1)}, u32[]{:S(2)}, u32[]{:S(2)}) collective-permute-start(bf16[128,384]{1,0:T(8,128)(2,1)S(1)} %get-tuple-element.35), channel_id=1, source_target_pairs={{0,64},{1,72},{2,80},{3,88},{4,96},{5,104},{6,112},{7,120},{8,0},{... | collective-permute-start | bytes 294920 | tf_op jit(solution)/shard_map/ppermute | solution.py:132
  (1 other events, 1.7 us)
Sparse Core Ops, SparseCore 0:
  10.3 59.0 all-gather.2
  71.8 26.0 reduce-scatter.1
  178.3 90.5 all-gather.4

commit v12 on v7

--- a/solution.py
+++ b/solution.py
@@ -100,11 +100,10 @@
     gate_terms = []
     up_terms = []
     for which in range(expert_count):
-        down_terms.append(contract_rows(hid_g * masks[which], dy_cols))
-        gate_masked = gate_g * masks[which]
-        up_masked = up_g * masks[which]
-        gate_terms.append(contract_rows(x_cols, gate_masked))
-        up_terms.append(contract_rows(x_cols, up_masked))
+        down_terms.append(contract_rows(hid_g, dy_cols * masks[which]))
+        x_masked = x_cols * masks[which]
+        gate_terms.append(contract_rows(x_masked, gate_g))
+        up_terms.append(contract_rows(x_masked, up_g))
     down_total = jnp.stack(down_terms, 0)
     gate_total = jnp.stack(gate_terms, 0)
     up_total = jnp.stack(up_terms, 0)

time: 360 us -> 362 us (level)
  waiting for transfers between devices: 147 us -> 142 us
    all_gather x1, waiting for transfers between devices: 45.7 us -> 38.8 us  [shards(): packed = lax.all_gather(packed, DP, axis=0, tiled=True)]
    mul x0 -> x2, local copies, waits for them, and re-layouts: none -> 4.17 us  [shards(): x_masked = x_cols * masks[which]]
  transfers between devices with their start and end apart: 9 -> 9, of which waited for: 9 -> 9; matrix products, arithmetic and copies ran while one was open for 19% -> 21% of each run, Pallas kernels for 0% -> 0%
where the time goes in v12:
time: 362 us; the launch traced here: 361 us
  waiting for transfers between devices  142 us (39%)
  blocking collectives  75.3 us (21%)
  matrix products  67.8 us (19%)
  starting transfers between devices  29.7 us (8%)
  other arithmetic  17.5 us (5%)
  between operations  14.8 us (4%)
  local copies, waits for them, and re-layouts  13.3 us (4%)
    all_to_all x1, blocking collectives, shards(): lax.all_to_all(result, CHIPS, split_axis=0, concat_axis=0, tiled=True)  75.3 us
    all_gather x1, waiting for transfers between devices, shards(): packed = lax.all_gather(packed, DP, axis=0, tiled=True)  38.8 us
    dot_general x6, matrix products, contract_rows(): lax.dot_general(left_op, right_op, (((0,), (0,)), ((), ())), preferred_el...  34 us
    dot_general x10, matrix products, contract_cols(): lax.dot_general(left_op, right_op, (((1,), (1,)), ((), ())), preferred_el...  33.9 us
    all_to_all x1, waiting for transfers between devices, shards(): lax.all_to_all(out_grad, DP, split_axis=1, concat_axis=0, tiled=True)  30.3 us
    reduce_scatter x1, waiting for transfers between devices, shards(): lax.psum_scatter(result.reshape(2, row_count // 2, ff), 'core', scatter_d...  28.4 us
    all_to_all x1, waiting for transfers between devices, shards(): lax.all_to_all(rows_in, DP, split_axis=1, concat_axis=0, tiled=True)  21.1 us
    all_to_all x2, starting transfers between devices, shards(): lax.all_to_all(partial_rows.reshape(N_TP, rows_dev, width), TP, split_axi...  11.3 us
  transfers between devices with their start and end apart: 9, of which 9 were waited for; matrix products, arithmetic and copies ran while one was open for 21% of the time, Pallas kernels for 0%

profile of v12, /device:TPU:3, one launch (start us, length us, event | category | flops | bytes accessed | tf_op | source)
XLA Modules:
  0.0 361.0 jit_solution(1451505704242105002)
XLA Ops:
  11.7 6.3 %all-to-all-start = ((bf16[128,16,384]{0,2,1:T(8,128)(2,1)}), bf16[128,16,384]{0,2,1:T(8,128)(2,1)S(1)}, u32[]{:S(2)}, u32[]{:S(2)}) async-start(bf16[128,16,384]{0,2,1:T(8,128)(2,1)} %bitcast.1), calls=%async_computation | async-start | bytes 3145728 | tf_op jit(solution)/shard_map/all_to_all | solution.py:63
  19.2 30.3 %all-to-all-done = bf16[128,16,384]{0,2,1:T(8,128)(2,1)S(1)} async-done(((bf16[128,16,384]{0,2,1:T(8,128)(2,1)}), bf16[128,16,384]{0,2,1:T(8,128)(2,1)S(1)}, u32[]{:S(2)}, u32[]{:S(2)}) %all-to-all-start) | async-done | bytes 1572896 | tf_op jit(solution)/shard_map/all_to_all | solution.py:63
  56.1 6.7 %convolution_add_fusion = f32[2048,1536]{1,0:T(8,128)} fusion(f32[2048,1536]{1,0:T(8,128)S(1)} %fusion.67, bf16[2048,384]{1,0:T(8,128)(2,1)S(1)} %bitcast.147, bf16[2,1536,384]{2,1,0:T(8,128)(2,1)S(1)} %copy-done.1), kind=kOutput, calls=%fused_computation.1 | convolution fusion | flops 2419064832 | bytes 27918336 | tf_op jit(solution)/shard_map/dot_general | solution.py:42
  62.8 6.6 %all-gather.3.cloned.1.call-done = bf16[2048,1536]{1,0:T(8,128)(2,1)} async-done(((bf16[128,1536]{1,0:T(8,128)(2,1)}), bf16[2048,1536]{1,0:T(8,128)(2,1)}) %all-gather.3.cloned.1.call-update) | async-done | bytes 6291472 | tf_op jit(solution)/shard_map/all_gather | solution.py:76
  69.5 28.4 %reduce-scatter.2.cloned.1.call-done = f32[1,1024,1536]{2,1,0:T(8,128)} async-done(((f32[2,1024,1536]{2,1,0:T(8,128)}), f32[1,1024,1536]{2,1,0:T(8,128)}) %reduce-scatter.2.cloned.1.call-update) | async-done | bytes 6291472 | tf_op jit(solution)/shard_map/reduce_scatter | solution.py:83
  97.9 75.3 %all_to_all.47 = f32[8,128,1536]{2,1,0:T(8,128)} all-to-all(f32[8,128,1536]{2,1,0:T(8,128)} %bitcast.149), channel_id=1, replica_groups=mesh['x'=4,'ylo'=2,'core'=2,'z'=4,'yhi'=2] {'x','ylo'}, dimensions={0} | all-to-all | bytes 12582912 | tf_op jit(solution)/shard_map/all_to_all | solution.py:86
  182.4 6.2 %all-to-all-start.4 = ((bf16[128,16,384]{0,2,1:T(8,128)(2,1)}), bf16[128,16,384]{0,2,1:T(8,128)(2,1)S(1)}, u32[]{:S(2)}, u32[]{:S(2)}) async-start(bf16[128,16,384]{0,2,1:T(8,128)(2,1)} %bitcast.36), calls=%async_computation.5 | async-start | bytes 3145728 | tf_op jit(solution)/shard_map/all_to_all | solution.py:89
  188.6 6.9 %fusion.41 = bf16[1,1536,384]{2,1,0:T(8,128)(2,1)S(1)} fusion(bf16[2048,1536]{1,0:T(8,128)(2,1)} %all-gather.3.cloned.1.call-done, bf16[2048,384]{1,0:T(8,128)(2,1)S(1)} %copy-done.9), kind=kOutput, calls=%fused_computation.47 | convolution fusion | flops 2416508928 | bytes 9043968 | tf_op jit(solution)/shard_map/dot_general | solution.py:36
  195.5 6.3 %fusion.40 = bf16[1,1536,384]{2,1,0:T(8,128)(2,1)S(1)} fusion(bf16[2048,1536]{1,0:T(8,128)(2,1)} %all-gather.3.cloned.1.call-done, bf16[2048,384]{1,0:T(8,128)(2,1)S(1)} %copy-done.8), kind=kOutput, calls=%fused_computation.46 | convolution fusion | flops 2416508928 | bytes 9043968 | tf_op jit(solution)/shard_map/dot_general | solution.py:36
  203.5 21.1 %all-to-all-done.4 = bf16[128,16,384]{0,2,1:T(8,128)(2,1)S(1)} async-done(((bf16[128,16,384]{0,2,1:T(8,128)(2,1)}), bf16[128,16,384]{0,2,1:T(8,128)(2,1)S(1)}, u32[]{:S(2)}, u32[]{:S(2)}) %all-to-all-start.4) | async-done | bytes 1572896 | tf_op jit(solution)/shard_map/all_to_all | solution.py:89
  230.2 38.8 %all-gather.5.cloned.1.call-done = bf16[2048,2,1536]{2,0,1:T(8,128)(2,1)} async-done(((bf16[128,2,1536]{2,0,1:T(8,128)(2,1)}), bf16[2048,2,1536]{2,0,1:T(8,128)(2,1)}) %all-gather.5.cloned.1.call-update) | async-done | bytes 12582928 | tf_op jit(solution)/shard_map/all_gather | solution.py:96
  268.9 4.2 %fusion.4 = f32[1024,384]{1,0:T(8,128)S(1)} fusion(bf16[2048,2,1536]{2,0,1:T(8,128)(2,1)} %all-gather.5.cloned.1.call-done, bf16[1024]{0:T(1024)(128)(2,1)S(1)} %broadcast_bitcast_fusion.2, bf16[2,384,1536]{2,1,0:T(8,128)(2,1)} %param.15), kind=kOutput, calls=%fused_computation.8 | convolution fusion | flops 1209532416 | bytes 5900288 | tf_op jit(solution)/shard_map/dot_general | solution.py:42
  281.5 6.6 %all-to-all-start.3 = ((f32[8,128,384]{2,1,0:T(8,128)}), f32[8,128,384]{2,1,0:T(8,128)S(1)}, u32[]{:S(2)}, u32[]{:S(2)}) async-start(f32[8,128,384]{2,1,0:T(8,128)} %bitcast.32), calls=%async_computation.4 | async-start | bytes 3145728 | tf_op jit(solution)/shard_map/all_to_all | solution.py:125
  288.1 4.2 %fusion.16 = f32[1024,384]{1,0:T(8,128)S(1)} fusion(bf16[2048,2,1536]{2,0,1:T(8,128)(2,1)} %all-gather.5.cloned.1.call-done, bf16[1024]{0:T(1024)(128)(2,1)S(1)} %broadcast_bitcast_fusion.5, bf16[2,384,1536]{2,1,0:T(8,128)(2,1)} %param.15), kind=kOutput, calls=%fused_computation.20 | convolution fusion | flops 1209532416 | bytes 5900288 | tf_op jit(solution)/shard_map/dot_general | solution.py:42
  292.3 3.9 %fusion.18 = f32[1024,384]{1,0:T(8,128)S(1)} fusion(bf16[2048,2,1536]{2,0,1:T(8,128)(2,1)} %all-gather.5.cloned.1.call-done, bf16[1024]{0:T(1024)(128)(2,1)S(1)} %broadcast_bitcast_fusion.5, bf16[2,384,1536]{2,1,0:T(8,128)(2,1)S(1)} %copy-done.16), kind=kOutput, calls=%fused_computation.22 | convolution fusion | flops 1209532416 | bytes 5900288 | tf_op jit(solution)/shard_map/dot_general | solution.py:42
  296.3 3.7 %fusion.45 = bf16[1,384,1536]{2,1,0:T(8,128)(2,1)} fusion(bf16[2048,384]{1,0:T(8,128)(2,1)S(1)} %bitcast.153, bf16[2048,2,1536]{2,0,1:T(8,128)(2,1)S(1)} %bitcast.159), kind=kOutput, calls=%fused_computation.51 | convolution fusion | flops 2416508928 | bytes 9043968 | tf_op jit(solution)/shard_map/dot_general | solution.py:36
  304.8 3.7 %fusion.43 = bf16[1,384,1536]{2,1,0:T(8,128)(2,1)} fusion(bf16[2048,384]{1,0:T(8,128)(2,1)S(1)} %bitcast.154, bf16[2048,2,1536]{2,0,1:T(8,128)(2,1)S(1)} %bitcast.159), kind=kOutput, calls=%fused_computation.49 | convolution fusion | flops 2416508928 | bytes 9043968 | tf_op jit(solution)/shard_map/dot_general | solution.py:36
  310.4 4.7 %all-to-all-start.2 = ((f32[8,128,384]{2,1,0:T(8,128)}), f32[8,128,384]{2,1,0:T(8,128)S(1)}, u32[]{:S(2)}, u32[]{:S(2)}) async-start(f32[8,128,384]{2,1,0:T(8,128)} %bitcast.155), calls=%async_computation.3 | async-start | bytes 3145728 | tf_op jit(solution)/shard_map/all_to_all | solution.py:125
  315.2 7.0 %fusion.44 = bf16[1,384,1536]{2,1,0:T(8,128)(2,1)} fusion(bf16[2048,384]{1,0:T(8,128)(2,1)} %bitcast.151, bf16[2048,2,1536]{2,0,1:T(8,128)(2,1)} %all-gather.5.cloned.1.call-done), kind=kOutput, calls=%fused_computation.50 | convolution fusion | flops 2416508928 | bytes 9043968 | tf_op jit(solution)/shard_map/dot_general | solution.py:36
  322.2 6.4 %fusion.42 = bf16[1,384,1536]{2,1,0:T(8,128)(2,1)} fusion(bf16[2048,384]{1,0:T(8,128)(2,1)S(1)} %bitcast.152, bf16[2048,2,1536]{2,0,1:T(8,128)(2,1)} %all-gather.5.cloned.1.call-done), kind=kOutput, calls=%fused_computation.48 | convolution fusion | flops 2416508928 | bytes 9043968 | tf_op jit(solution)/shard_map/dot_general | solution.py:36
  328.7 8.2 %all-to-all-done.2 = f32[8,128,384]{2,1,0:T(8,128)S(1)} async-done(((f32[8,128,384]{2,1,0:T(8,128)}), f32[8,128,384]{2,1,0:T(8,128)S(1)}, u32[]{:S(2)}, u32[]{:S(2)}) %all-to-all-start.2) | async-done | bytes 1572896 | tf_op jit(solution)/shard_map/all_to_all | solution.py:125
  337.1 3.5 collective-permute-start
  342.9 3.8 %pad_maximum_fusion = (bf16[2,384,1536]{2,1,0:T(8,128)(2,1)}, bf16[2,384,1536]{2,1,0:T(8,128)(2,1)}) fusion(bf16[1,384,1536]{2,1,0:T(8,128)(2,1)} %fusion.42, bf16[1,384,1536]{2,1,0:T(8,128)(2,1)} %fusion.43, bf16[1,384,1536]{2,1,0:T(8,128)(2,1)} %fusion.44, bf16[1,384,1536]{2,1,0:T(8,128)(2,1)S(1)} %copy-done.10), kind=kLoop, calls=%fused_computation.52 | loop fusion | flops 2359296 | bytes 9437184 | tf_op jit(solution)/shard_map/stack | solution.py:108
  346.8 4.3 %collective-permute-done = bf16[128,384]{1,0:T(8,128)(2,1)S(1)} collective-permute-done((bf16[128,384]{1,0:T(8,128)(2,1)S(1)}, bf16[128,384]{1,0:T(8,128)(2,1)S(1)}, u32[]{:S(2)}, u32[]{:S(2)}) %collective-permute-start) | collective-permute-done | bytes 98336 | tf_op jit(solution)/shard_map/ppermute | solution.py:135
  (91 shorter events, 49.0 us)
Async XLA Ops:
  7.2 62.3 %all-gather.3.cloned.1.call-start = ((), (), s32[]{:S(2)}) async-start(), calls=%async_computation.6 | async-start | bytes 6684672 | tf_op jit(solution)/shard_map/all_gather | solution.py:76
  11.7 6.4 %copy-start.11 = (s32[16]{0:T(128)S(1)}, s32[16]{0:T(128)}, u32[]{:S(2)}) copy-start(s32[16]{0:T(128)} %constant.55) | copy-start | bytes 196
  11.7 6.4 %copy-start = (s32[16]{0:T(128)S(1)}, s32[16]{0:T(128)}, u32[]{:S(2)}) copy-start(s32[16]{0:T(128)} %param.18) | copy-start | bytes 196
  11.7 37.8 %all-to-all-start = ((bf16[128,16,384]{0,2,1:T(8,128)(2,1)}), bf16[128,16,384]{0,2,1:T(8,128)(2,1)S(1)}, u32[]{:S(2)}, u32[]{:S(2)}) async-start(bf16[128,16,384]{0,2,1:T(8,128)(2,1)} %bitcast.1), calls=%async_computation | async-start | bytes 3145728 | tf_op jit(solution)/shard_map/all_to_all | solution.py:63
  18.0 79.9 %reduce-scatter.2.cloned.1.call-start = ((), (), s32[]{:S(2)}) async-start(), calls=%async_computation.7 | async-start | bytes 18874368 | tf_op jit(solution)/shard_map/reduce_scatter | solution.py:83
  69.5 199.5 %all-gather.5.cloned.1.call-start = ((), (), s32[]{:S(2)}) async-start(), calls=%async_computation.8 | async-start | bytes 13369344 | tf_op jit(solution)/shard_map/all_gather | solution.py:96
  173.3 3.5 copy-start.7
  182.4 6.2 %copy-start.9 = (bf16[2048,384]{1,0:T(8,128)(2,1)S(1)}, bf16[2048,384]{1,0:T(8,128)(2,1)}, u32[]{:S(2)}) copy-start(bf16[2048,384]{1,0:T(8,128)(2,1)} %get-tuple-element.13) | copy-start | bytes 4718596
  182.4 42.1 %all-to-all-start.4 = ((bf16[128,16,384]{0,2,1:T(8,128)(2,1)}), bf16[128,16,384]{0,2,1:T(8,128)(2,1)S(1)}, u32[]{:S(2)}, u32[]{:S(2)}) async-start(bf16[128,16,384]{0,2,1:T(8,128)(2,1)} %bitcast.36), calls=%async_computation.5 | async-start | bytes 3145728 | tf_op jit(solution)/shard_map/all_to_all | solution.py:89
  188.6 6.9 %copy-start.8 = (bf16[2048,384]{1,0:T(8,128)(2,1)S(1)}, bf16[2048,384]{1,0:T(8,128)(2,1)}, u32[]{:S(2)}) copy-start(bf16[2048,384]{1,0:T(8,128)(2,1)} %get-tuple-element.12) | copy-start | bytes 4718596
  230.2 43.0 %copy-start.13 = (bf16[2,384,1536]{2,1,0:T(8,128)(2,1)S(1)}, bf16[2,384,1536]{2,1,0:T(8,128)(2,1)}, u32[]{:S(2)}) copy-start(bf16[2,384,1536]{2,1,0:T(8,128)(2,1)} %param.15) | copy-start | bytes 7077892
  268.9 5.9 %copy-start.12 = (bf16[2048,2,1536]{2,0,1:T(8,128)(2,1)S(1)}, bf16[2048,2,1536]{2,0,1:T(8,128)(2,1)}, u32[]{:S(2)}) copy-start(bf16[2048,2,1536]{2,0,1:T(8,128)(2,1)} %all-gather.5.cloned.1.call-done) | copy-start | bytes 37748740
  281.5 29.0 %all-to-all-start.3 = ((f32[8,128,384]{2,1,0:T(8,128)}), f32[8,128,384]{2,1,0:T(8,128)S(1)}, u32[]{:S(2)}, u32[]{:S(2)}) async-start(f32[8,128,384]{2,1,0:T(8,128)} %bitcast.32), calls=%async_computation.4 | async-start | bytes 3145728 | tf_op jit(solution)/shard_map/all_to_all | solution.py:125
  288.1 4.2 %copy-start.16 = (bf16[2,384,1536]{2,1,0:T(8,128)(2,1)S(1)}, bf16[2,384,1536]{2,1,0:T(8,128)(2,1)}, u32[]{:S(2)}) copy-start(bf16[2,384,1536]{2,1,0:T(8,128)(2,1)} %param.14) | copy-start | bytes 7077892
  288.1 8.1 %slice-start = ((s8[12582912]{0:T(1024)(128)(4,1)}), s8[4194304]{0:T(1024)(128)(4,1)S(1)}, s32[]{:S(2)}) async-start(s8[12582912]{0:T(1024)(128)(4,1)} %bitcast.158), calls=%async_computation.9 | async-start | bytes 8388608
  288.1 8.1 %slice-start.1 = ((s8[12582912]{0:T(1024)(128)(4,1)}), s8[4194304]{0:T(1024)(128)(4,1)S(1)}, s32[]{:S(2)}) async-start(s8[12582912]{0:T(1024)(128)(4,1)} %bitcast.158), calls=%async_computation.10 | async-start | bytes 8388608
  292.3 3.9 %copy-start.5 = (bf16[16,128,384]{2,1,0:T(8,128)(2,1)S(1)}, bf16[16,128,384]{2,1,0:T(8,128)(2,1)}, u32[]{:S(2)}) copy-start(bf16[16,128,384]{2,1,0:T(8,128)(2,1)} %copy.23) | copy-start | bytes 4718596
  292.3 4.0 %slice-start.2 = ((s8[12582912]{0:T(1024)(128)(4,1)}), s8[4194304]{0:T(1024)(128)(4,1)S(1)}, s32[]{:S(2)}) async-start(s8[12582912]{0:T(1024)(128)(4,1)} %bitcast.158), calls=%async_computation.11 | async-start | bytes 8388608
  296.3 3.7 %copy-start.14 = (bf16[2,384,1536]{2,1,0:T(8,128)(2,1)S(1)}, bf16[2,384,1536]{2,1,0:T(8,128)(2,1)}, u32[]{:S(2)}) copy-start(bf16[2,384,1536]{2,1,0:T(8,128)(2,1)} %param.15) | copy-start | bytes 7077892
  310.4 26.5 %all-to-all-start.2 = ((f32[8,128,384]{2,1,0:T(8,128)}), f32[8,128,384]{2,1,0:T(8,128)S(1)}, u32[]{:S(2)}, u32[]{:S(2)}) async-start(f32[8,128,384]{2,1,0:T(8,128)} %bitcast.155), calls=%async_computation.3 | async-start | bytes 3145728 | tf_op jit(solution)/shard_map/all_to_all | solution.py:125
  315.2 7.0 %copy-start.4 = (bf16[16,128,384]{2,1,0:T(8,128)(2,1)S(1)}, bf16[16,128,384]{2,1,0:T(8,128)(2,1)}, u32[]{:S(2)}) copy-start(bf16[16,128,384]{2,1,0:T(8,128)(2,1)} %copy.24) | copy-start | bytes 4718596
  328.7 14.2 %copy-start.10 = (bf16[1,384,1536]{2,1,0:T(8,128)(2,1)S(1)}, bf16[1,384,1536]{2,1,0:T(8,128)(2,1)}, u32[]{:S(2)}) copy-start(bf16[1,384,1536]{2,1,0:T(8,128)(2,1)} %fusion.45) | copy-start | bytes 3538948
  337.1 14.0 %collective-permute-start = (bf16[128,384]{1,0:T(8,128)(2,1)S(1)}, bf16[128,384]{1,0:T(8,128)(2,1)S(1)}, u32[]{:S(2)}, u32[]{:S(2)}) collective-permute-start(bf16[128,384]{1,0:T(8,128)(2,1)S(1)} %get-tuple-element.22), channel_id=1, source_target_pairs={{0,0},{1,8},{2,16},{3,24},{4,32},{5,40},{6,48},{7,56},{8,64},{9,72... | collective-permute-start | bytes 294920 | tf_op jit(solution)/shard_map/ppermute | solution.py:135
  340.6 13.1 %collective-permute-start.1 = (bf16[128,384]{1,0:T(8,128)(2,1)S(1)}, bf16[128,384]{1,0:T(8,128)(2,1)S(1)}, u32[]{:S(2)}, u32[]{:S(2)}) collective-permute-start(bf16[128,384]{1,0:T(8,128)(2,1)S(1)} %get-tuple-element.23), channel_id=1, source_target_pairs={{0,64},{1,72},{2,80},{3,88},{4,96},{5,104},{6,112},{7,120},{8,0},{... | collective-permute-start | bytes 294920 | tf_op jit(solution)/shard_map/ppermute | solution.py:135
  (5 other events, 12.2 us)
Sparse Core Ops, SparseCore 0:
  10.3 59.0 all-gather.2
  71.8 26.0 reduce-scatter.1
  178.3 90.5 all-gather.4

commit v13 on v12

--- a/solution.py
+++ b/solution.py
@@ -115,12 +115,8 @@
         rows = slice(half * half_rows, (half + 1) * half_rows)
         partial_rows = jnp.zeros((half_rows, width), jnp.float32)
         for which in range(expert_count):
-            gate_masked = gate_g[rows] * masks[which][rows]
-            up_masked = up_g[rows] * masks[which][rows]
-            partial_rows = (
-                partial_rows
-                + contract_cols(gate_masked, w_gate[which])
-                + contract_cols(up_masked, w_up[which])
+            partial_rows = partial_rows + masks[which][rows].astype(jnp.float32) * (
+                contract_cols(gate_g[rows], w_gate[which]) + contract_cols(up_g[rows], w_up[which])
             )
         pieces = lax.all_to_all(
             partial_rows.reshape(N_TP, rows_dev, width), TP, split_axis=0, concat_axis=0, tiled=True

time: 362 us -> 363 us (level)
  no operation moved by 1% of the time
where the time goes in v13:
time: 363 us; the launch traced here: 362 us
  waiting for transfers between devices  142 us (39%)
  blocking collectives  75.3 us (21%)
  matrix products  69.2 us (19%)
  starting transfers between devices  29.8 us (8%)
  other arithmetic  17.6 us (5%)
  between operations  14.8 us (4%)
  local copies, waits for them, and re-layouts  13.3 us (4%)
    all_to_all x1, blocking collectives, shards(): lax.all_to_all(result, CHIPS, split_axis=0, concat_axis=0, tiled=True)  75.3 us
    all_gather x1, waiting for transfers between devices, shards(): packed = lax.all_gather(packed, DP, axis=0, tiled=True)  38.8 us
    dot_general x10, matrix products, contract_cols(): lax.dot_general(left_op, right_op, (((1,), (1,)), ((), ())), preferred_el...  35.3 us
    dot_general x6, matrix products, contract_rows(): lax.dot_general(left_op, right_op, (((0,), (0,)), ((), ())), preferred_el...  33.9 us
    all_to_all x1, waiting for transfers between devices, shards(): lax.all_to_all(out_grad, DP, split_axis=1, concat_axis=0, tiled=True)  30.3 us
    reduce_scatter x1, waiting for transfers between devices, shards(): lax.psum_scatter(result.reshape(2, row_count // 2, ff), 'core', scatter_d...  28.4 us
    all_to_all x1, waiting for transfers between devices, shards(): lax.all_to_all(rows_in, DP, split_axis=1, concat_axis=0, tiled=True)  21.1 us
    all_to_all x2, starting transfers between devices, shards(): lax.all_to_all(partial_rows.reshape(N_TP, rows_dev, width), TP, split_axi...  11.3 us
  transfers between devices with their start and end apart: 9, of which 9 were waited for; matrix products, arithmetic and copies ran while one was open for 21% of the time, Pallas kernels for 0%

profile of v13, /device:TPU:3, one launch (start us, length us, event | category | flops | bytes accessed | tf_op | source)
XLA Modules:
  0.0 362.4 jit_solution(7207597975494367538)
XLA Ops:
  11.7 6.3 %all-to-all-start = ((bf16[128,16,384]{0,2,1:T(8,128)(2,1)}), bf16[128,16,384]{0,2,1:T(8,128)(2,1)S(1)}, u32[]{:S(2)}, u32[]{:S(2)}) async-start(bf16[128,16,384]{0,2,1:T(8,128)(2,1)} %bitcast.2), calls=%async_computation | async-start | bytes 3145728 | tf_op jit(solution)/shard_map/all_to_all | solution.py:63
  19.2 30.3 %all-to-all-done = bf16[128,16,384]{0,2,1:T(8,128)(2,1)S(1)} async-done(((bf16[128,16,384]{0,2,1:T(8,128)(2,1)}), bf16[128,16,384]{0,2,1:T(8,128)(2,1)S(1)}, u32[]{:S(2)}, u32[]{:S(2)}) %all-to-all-start) | async-done | bytes 1572896 | tf_op jit(solution)/shard_map/all_to_all | solution.py:63
  56.1 6.7 %convolution_add_fusion = f32[2048,1536]{1,0:T(8,128)} fusion(f32[2048,1536]{1,0:T(8,128)S(1)} %fusion.31, bf16[2048,384]{1,0:T(8,128)(2,1)S(1)} %bitcast.139, bf16[2,1536,384]{2,1,0:T(8,128)(2,1)S(1)} %copy-done.1), kind=kOutput, calls=%fused_computation.1 | convolution fusion | flops 2419064832 | bytes 27918336 | tf_op jit(solution)/shard_map/dot_general | solution.py:42
  62.8 6.6 %all-gather.3.cloned.1.call-done = bf16[2048,1536]{1,0:T(8,128)(2,1)} async-done(((bf16[128,1536]{1,0:T(8,128)(2,1)}), bf16[2048,1536]{1,0:T(8,128)(2,1)}) %all-gather.3.cloned.1.call-update) | async-done | bytes 6291472 | tf_op jit(solution)/shard_map/all_gather | solution.py:76
  69.5 28.4 %reduce-scatter.2.cloned.1.call-done = f32[1,1024,1536]{2,1,0:T(8,128)} async-done(((f32[2,1024,1536]{2,1,0:T(8,128)}), f32[1,1024,1536]{2,1,0:T(8,128)}) %reduce-scatter.2.cloned.1.call-update) | async-done | bytes 6291472 | tf_op jit(solution)/shard_map/reduce_scatter | solution.py:83
  97.9 75.3 %all_to_all.47 = f32[8,128,1536]{2,1,0:T(8,128)} all-to-all(f32[8,128,1536]{2,1,0:T(8,128)} %bitcast.141), channel_id=1, replica_groups=mesh['x'=4,'ylo'=2,'core'=2,'z'=4,'yhi'=2] {'x','ylo'}, dimensions={0} | all-to-all | bytes 12582912 | tf_op jit(solution)/shard_map/all_to_all | solution.py:86
  182.4 6.2 %all-to-all-start.4 = ((bf16[128,16,384]{0,2,1:T(8,128)(2,1)}), bf16[128,16,384]{0,2,1:T(8,128)(2,1)S(1)}, u32[]{:S(2)}, u32[]{:S(2)}) async-start(bf16[128,16,384]{0,2,1:T(8,128)(2,1)} %bitcast.32), calls=%async_computation.5 | async-start | bytes 3145728 | tf_op jit(solution)/shard_map/all_to_all | solution.py:89
  188.6 6.9 %fusion.17 = bf16[1,1536,384]{2,1,0:T(8,128)(2,1)S(1)} fusion(bf16[2048,1536]{1,0:T(8,128)(2,1)} %all-gather.3.cloned.1.call-done, bf16[2048,384]{1,0:T(8,128)(2,1)S(1)} %copy-done.9), kind=kOutput, calls=%fused_computation.27 | convolution fusion | flops 2416508928 | bytes 9043968 | tf_op jit(solution)/shard_map/dot_general | solution.py:36
  195.5 6.3 %fusion.16 = bf16[1,1536,384]{2,1,0:T(8,128)(2,1)S(1)} fusion(bf16[2048,1536]{1,0:T(8,128)(2,1)} %all-gather.3.cloned.1.call-done, bf16[2048,384]{1,0:T(8,128)(2,1)S(1)} %copy-done.8), kind=kOutput, calls=%fused_computation.26 | convolution fusion | flops 2416508928 | bytes 9043968 | tf_op jit(solution)/shard_map/dot_general | solution.py:36
  203.4 21.1 %all-to-all-done.4 = bf16[128,16,384]{0,2,1:T(8,128)(2,1)S(1)} async-done(((bf16[128,16,384]{0,2,1:T(8,128)(2,1)}), bf16[128,16,384]{0,2,1:T(8,128)(2,1)S(1)}, u32[]{:S(2)}, u32[]{:S(2)}) %all-to-all-start.4) | async-done | bytes 1572896 | tf_op jit(solution)/shard_map/all_to_all | solution.py:89
  230.1 38.8 %all-gather.5.cloned.1.call-done = bf16[2048,2,1536]{2,0,1:T(8,128)(2,1)} async-done(((bf16[128,2,1536]{2,0,1:T(8,128)(2,1)}), bf16[2048,2,1536]{2,0,1:T(8,128)(2,1)}) %all-gather.5.cloned.1.call-update) | async-done | bytes 12582928 | tf_op jit(solution)/shard_map/all_gather | solution.py:96
  268.9 4.2 %fusion.12 = f32[1024,384]{1,0:T(8,128)S(1)} fusion(bf16[2048,2,1536]{2,0,1:T(8,128)(2,1)} %all-gather.5.cloned.1.call-done, bf16[2,384,1536]{2,1,0:T(8,128)(2,1)} %param.14), kind=kOutput, calls=%fused_computation.22 | convolution fusion | flops 1207959552 | bytes 5898240 | tf_op jit(solution)/shard_map/dot_general | solution.py:42
  282.8 6.7 %all-to-all-start.3 = ((f32[8,128,384]{2,1,0:T(8,128)}), f32[8,128,384]{2,1,0:T(8,128)S(1)}, u32[]{:S(2)}, u32[]{:S(2)}) async-start(f32[8,128,384]{2,1,0:T(8,128)} %bitcast.28), calls=%async_computation.4 | async-start | bytes 3145728 | tf_op jit(solution)/shard_map/all_to_all | solution.py:121
  289.5 4.2 %fusion.10 = f32[1024,384]{1,0:T(8,128)S(1)} fusion(bf16[2048,2,1536]{2,0,1:T(8,128)(2,1)} %all-gather.5.cloned.1.call-done, bf16[2,384,1536]{2,1,0:T(8,128)(2,1)} %param.15), kind=kOutput, calls=%fused_computation.20 | convolution fusion | flops 1207959552 | bytes 5898240 | tf_op jit(solution)/shard_map/dot_general | solution.py:42
  293.7 3.9 %fusion.8 = f32[1024,384]{1,0:T(8,128)S(1)} fusion(bf16[2048,2,1536]{2,0,1:T(8,128)(2,1)} %all-gather.5.cloned.1.call-done, bf16[2,384,1536]{2,1,0:T(8,128)(2,1)S(1)} %copy-done.13), kind=kOutput, calls=%fused_computation.18 | convolution fusion | flops 1207959552 | bytes 5898240 | tf_op jit(solution)/shard_map/dot_general | solution.py:42
  297.7 3.7 %fusion.21 = bf16[1,384,1536]{2,1,0:T(8,128)(2,1)} fusion(bf16[2048,384]{1,0:T(8,128)(2,1)S(1)} %bitcast.145, bf16[2048,2,1536]{2,0,1:T(8,128)(2,1)S(1)} %bitcast.151), kind=kOutput, calls=%fused_computation.31 | convolution fusion | flops 2416508928 | bytes 9043968 | tf_op jit(solution)/shard_map/dot_general | solution.py:36
  306.2 3.7 %fusion.19 = bf16[1,384,1536]{2,1,0:T(8,128)(2,1)} fusion(bf16[2048,384]{1,0:T(8,128)(2,1)S(1)} %bitcast.146, bf16[2048,2,1536]{2,0,1:T(8,128)(2,1)S(1)} %bitcast.151), kind=kOutput, calls=%fused_computation.29 | convolution fusion | flops 2416508928 | bytes 9043968 | tf_op jit(solution)/shard_map/dot_general | solution.py:36
  311.9 4.7 %all-to-all-start.2 = ((f32[8,128,384]{2,1,0:T(8,128)}), f32[8,128,384]{2,1,0:T(8,128)S(1)}, u32[]{:S(2)}, u32[]{:S(2)}) async-start(f32[8,128,384]{2,1,0:T(8,128)} %bitcast.147), calls=%async_computation.3 | async-start | bytes 3145728 | tf_op jit(solution)/shard_map/all_to_all | solution.py:121
  316.5 7.0 %fusion.20 = bf16[1,384,1536]{2,1,0:T(8,128)(2,1)} fusion(bf16[2048,384]{1,0:T(8,128)(2,1)} %bitcast.143, bf16[2048,2,1536]{2,0,1:T(8,128)(2,1)} %all-gather.5.cloned.1.call-done), kind=kOutput, calls=%fused_computation.30 | convolution fusion | flops 2416508928 | bytes 9043968 | tf_op jit(solution)/shard_map/dot_general | solution.py:36
  323.6 6.4 %fusion.18 = bf16[1,384,1536]{2,1,0:T(8,128)(2,1)} fusion(bf16[2048,384]{1,0:T(8,128)(2,1)S(1)} %bitcast.144, bf16[2048,2,1536]{2,0,1:T(8,128)(2,1)} %all-gather.5.cloned.1.call-done), kind=kOutput, calls=%fused_computation.28 | convolution fusion | flops 2416508928 | bytes 9043968 | tf_op jit(solution)/shard_map/dot_general | solution.py:36
  330.1 8.2 %all-to-all-done.2 = f32[8,128,384]{2,1,0:T(8,128)S(1)} async-done(((f32[8,128,384]{2,1,0:T(8,128)}), f32[8,128,384]{2,1,0:T(8,128)S(1)}, u32[]{:S(2)}, u32[]{:S(2)}) %all-to-all-start.2) | async-done | bytes 1572896 | tf_op jit(solution)/shard_map/all_to_all | solution.py:121
  338.5 3.5 collective-permute-start
  344.3 3.8 %pad_maximum_fusion = (bf16[2,384,1536]{2,1,0:T(8,128)(2,1)}, bf16[2,384,1536]{2,1,0:T(8,128)(2,1)}) fusion(bf16[1,384,1536]{2,1,0:T(8,128)(2,1)} %fusion.18, bf16[1,384,1536]{2,1,0:T(8,128)(2,1)} %fusion.19, bf16[1,384,1536]{2,1,0:T(8,128)(2,1)} %fusion.20, bf16[1,384,1536]{2,1,0:T(8,128)(2,1)S(1)} %copy-done.10), kind=kLoop, calls=%fused_computation.32 | loop fusion | flops 2359296 | bytes 9437184 | tf_op jit(solution)/shard_map/stack | solution.py:108
  348.1 4.3 %collective-permute-done = bf16[128,384]{1,0:T(8,128)(2,1)S(1)} collective-permute-done((bf16[128,384]{1,0:T(8,128)(2,1)S(1)}, bf16[128,384]{1,0:T(8,128)(2,1)S(1)}, u32[]{:S(2)}, u32[]{:S(2)}) %collective-permute-start) | collective-permute-done | bytes 98336 | tf_op jit(solution)/shard_map/ppermute | solution.py:131
  (89 shorter events, 50.5 us)
Async XLA Ops:
  7.2 62.3 %all-gather.3.cloned.1.call-start = ((), (), s32[]{:S(2)}) async-start(), calls=%async_computation.6 | async-start | bytes 6684672 | tf_op jit(solution)/shard_map/all_gather | solution.py:76
  11.7 6.4 %copy-start.11 = (s32[16]{0:T(128)S(1)}, s32[16]{0:T(128)}, u32[]{:S(2)}) copy-start(s32[16]{0:T(128)} %constant.55) | copy-start | bytes 196
  11.7 6.4 %copy-start = (s32[16]{0:T(128)S(1)}, s32[16]{0:T(128)}, u32[]{:S(2)}) copy-start(s32[16]{0:T(128)} %param.18) | copy-start | bytes 196
  11.7 37.8 %all-to-all-start = ((bf16[128,16,384]{0,2,1:T(8,128)(2,1)}), bf16[128,16,384]{0,2,1:T(8,128)(2,1)S(1)}, u32[]{:S(2)}, u32[]{:S(2)}) async-start(bf16[128,16,384]{0,2,1:T(8,128)(2,1)} %bitcast.2), calls=%async_computation | async-start | bytes 3145728 | tf_op jit(solution)/shard_map/all_to_all | solution.py:63
  18.0 79.9 %reduce-scatter.2.cloned.1.call-start = ((), (), s32[]{:S(2)}) async-start(), calls=%async_computation.7 | async-start | bytes 18874368 | tf_op jit(solution)/shard_map/reduce_scatter | solution.py:83
  69.5 199.4 %all-gather.5.cloned.1.call-start = ((), (), s32[]{:S(2)}) async-start(), calls=%async_computation.8 | async-start | bytes 13369344 | tf_op jit(solution)/shard_map/all_gather | solution.py:96
  173.3 3.5 copy-start.6
  173.3 3.5 copy-start.7
  182.4 6.2 %copy-start.9 = (bf16[2048,384]{1,0:T(8,128)(2,1)S(1)}, bf16[2048,384]{1,0:T(8,128)(2,1)}, u32[]{:S(2)}) copy-start(bf16[2048,384]{1,0:T(8,128)(2,1)} %get-tuple-element.13) | copy-start | bytes 4718596
  182.4 42.1 %all-to-all-start.4 = ((bf16[128,16,384]{0,2,1:T(8,128)(2,1)}), bf16[128,16,384]{0,2,1:T(8,128)(2,1)S(1)}, u32[]{:S(2)}, u32[]{:S(2)}) async-start(bf16[128,16,384]{0,2,1:T(8,128)(2,1)} %bitcast.32), calls=%async_computation.5 | async-start | bytes 3145728 | tf_op jit(solution)/shard_map/all_to_all | solution.py:89
  188.6 6.9 %copy-start.8 = (bf16[2048,384]{1,0:T(8,128)(2,1)S(1)}, bf16[2048,384]{1,0:T(8,128)(2,1)}, u32[]{:S(2)}) copy-start(bf16[2048,384]{1,0:T(8,128)(2,1)} %get-tuple-element.12) | copy-start | bytes 4718596
  268.9 5.9 %copy-start.12 = (bf16[2048,2,1536]{2,0,1:T(8,128)(2,1)S(1)}, bf16[2048,2,1536]{2,0,1:T(8,128)(2,1)}, u32[]{:S(2)}) copy-start(bf16[2048,2,1536]{2,0,1:T(8,128)(2,1)} %all-gather.5.cloned.1.call-done) | copy-start | bytes 37748740
  274.8 3.2 copy-start.14
  282.8 29.0 %all-to-all-start.3 = ((f32[8,128,384]{2,1,0:T(8,128)}), f32[8,128,384]{2,1,0:T(8,128)S(1)}, u32[]{:S(2)}, u32[]{:S(2)}) async-start(f32[8,128,384]{2,1,0:T(8,128)} %bitcast.28), calls=%async_computation.4 | async-start | bytes 3145728 | tf_op jit(solution)/shard_map/all_to_all | solution.py:121
  289.5 4.2 %copy-start.13 = (bf16[2,384,1536]{2,1,0:T(8,128)(2,1)S(1)}, bf16[2,384,1536]{2,1,0:T(8,128)(2,1)}, u32[]{:S(2)}) copy-start(bf16[2,384,1536]{2,1,0:T(8,128)(2,1)} %param.14) | copy-start | bytes 7077892
  289.5 8.1 %slice-start = ((s8[12582912]{0:T(1024)(128)(4,1)}), s8[4194304]{0:T(1024)(128)(4,1)S(1)}, s32[]{:S(2)}) async-start(s8[12582912]{0:T(1024)(128)(4,1)} %bitcast.150), calls=%async_computation.9 | async-start | bytes 8388608
  289.5 8.1 %slice-start.1 = ((s8[12582912]{0:T(1024)(128)(4,1)}), s8[4194304]{0:T(1024)(128)(4,1)S(1)}, s32[]{:S(2)}) async-start(s8[12582912]{0:T(1024)(128)(4,1)} %bitcast.150), calls=%async_computation.10 | async-start | bytes 8388608
  293.7 3.9 %copy-start.5 = (bf16[16,128,384]{2,1,0:T(8,128)(2,1)S(1)}, bf16[16,128,384]{2,1,0:T(8,128)(2,1)}, u32[]{:S(2)}) copy-start(bf16[16,128,384]{2,1,0:T(8,128)(2,1)} %copy.23) | copy-start | bytes 4718596
  293.7 4.0 %slice-start.2 = ((s8[12582912]{0:T(1024)(128)(4,1)}), s8[4194304]{0:T(1024)(128)(4,1)S(1)}, s32[]{:S(2)}) async-start(s8[12582912]{0:T(1024)(128)(4,1)} %bitcast.150), calls=%async_computation.11 | async-start | bytes 8388608
  311.9 26.4 %all-to-all-start.2 = ((f32[8,128,384]{2,1,0:T(8,128)}), f32[8,128,384]{2,1,0:T(8,128)S(1)}, u32[]{:S(2)}, u32[]{:S(2)}) async-start(f32[8,128,384]{2,1,0:T(8,128)} %bitcast.147), calls=%async_computation.3 | async-start | bytes 3145728 | tf_op jit(solution)/shard_map/all_to_all | solution.py:121
  316.5 7.0 %copy-start.4 = (bf16[16,128,384]{2,1,0:T(8,128)(2,1)S(1)}, bf16[16,128,384]{2,1,0:T(8,128)(2,1)}, u32[]{:S(2)}) copy-start(bf16[16,128,384]{2,1,0:T(8,128)(2,1)} %copy.24) | copy-start | bytes 4718596
  330.1 14.2 %copy-start.10 = (bf16[1,384,1536]{2,1,0:T(8,128)(2,1)S(1)}, bf16[1,384,1536]{2,1,0:T(8,128)(2,1)}, u32[]{:S(2)}) copy-start(bf16[1,384,1536]{2,1,0:T(8,128)(2,1)} %fusion.21) | copy-start | bytes 3538948
  338.5 14.0 %collective-permute-start = (bf16[128,384]{1,0:T(8,128)(2,1)S(1)}, bf16[128,384]{1,0:T(8,128)(2,1)S(1)}, u32[]{:S(2)}, u32[]{:S(2)}) collective-permute-start(bf16[128,384]{1,0:T(8,128)(2,1)S(1)} %get-tuple-element.22), channel_id=1, source_target_pairs={{0,0},{1,8},{2,16},{3,24},{4,32},{5,40},{6,48},{7,56},{8,64},{9,72... | collective-permute-start | bytes 294920 | tf_op jit(solution)/shard_map/ppermute | solution.py:131
  342.0 13.1 %collective-permute-start.1 = (bf16[128,384]{1,0:T(8,128)(2,1)S(1)}, bf16[128,384]{1,0:T(8,128)(2,1)S(1)}, u32[]{:S(2)}, u32[]{:S(2)}) collective-permute-start(bf16[128,384]{1,0:T(8,128)(2,1)S(1)} %get-tuple-element.23), channel_id=1, source_target_pairs={{0,64},{1,72},{2,80},{3,88},{4,96},{5,104},{6,112},{7,120},{8,0},{... | collective-permute-start | bytes 294920 | tf_op jit(solution)/shard_map/ppermute | solution.py:131
  (4 other events, 8.7 us)
Sparse Core Ops, SparseCore 0:
  10.3 59.0 all-gather.2
  71.8 26.0 reduce-scatter.1
  178.3 90.5 all-gather.4
